TPU v7x, 256 devices: a whole 4x4x8 slice. The times are simulated.
256 devices in a mesh: slab: 4 (over x), dev: 64 (over y, z, core).
Axes of the slice: x: 4, y: 4, z: 8, core: 2. Of those that a mesh axis runs over, the one named last changes fastest.
Arguments:
- pixels: bfloat16 [12288, 384], P(('slab', 'dev')), may hold values from -14 to 14
- tile_clip: int32 [12288], P(('slab', 'dev')), may hold values from 0 to 511, never falling along the last dimension, each value on 1 to 72 neighbouring positions
- tile_encoder: int32 [12288, 1], P(('slab', 'dev')), may hold values from 0 to 63; in each aligned block of 48 rows (0 to 47, 48 to 95, ...) at most 2 rows name the same one
- slot_owner: int32 [32768, 1], P(('slab', 'dev')), may hold values from 0 to 63; in each aligned block of 128 rows (0 to 127, 128 to 255, ...) at most 2 rows name the same one
- conv_first: bfloat16 [3, 3, 3, 3, 128], replicated, may hold values from -0.625 to 0.625
- gain_first: float32 [128], replicated, may hold values from 0.25 to 1.75
- bias_first: float32 [128], replicated, may hold values from -2.5 to 2.5
- conv_down: bfloat16 [3, 3, 3, 128, 256], replicated, may hold values from -0.109375 to 0.109375
- gain_second: float32 [256], replicated, may hold values from 0.25 to 1.75
- bias_second: float32 [256], replicated, may hold values from -2.5 to 2.5
- project: bfloat16 [256, 128], replicated, may hold values from -0.375 to 0.375
- project_bias: float32 [128], replicated, may hold values from -2.5 to 2.5
Outputs:
- packed: bfloat16 [1048576, 128], P(('slab', 'dev'))
Inputs may be any that keep to these rules, and one draw needn't show every extreme that they name: `tile_encoder`: no loader sends more than 2 of its tiles to one encoder. `slot_owner`: the 128 slots of each encoder name every owner exactly 2 times. `tile_clip`: every clip has at least one tile.
All inputs are finite; a program needn't handle non-finite values.
Results may differ from a plain program's by a relative error of at most 0.0061.
Values may be sent and summed in bfloat16 or wider, within the bound.
No kernel may reach another device: no remote copies, remote signals or barrier semaphores. Data moves between devices by JAX's collectives and lax.ppermute only.
A program may use at most 64 MiB of HBM per device.

v0:
```python
import math

import jax
import jax.numpy as jnp
from jax import lax
from jax.sharding import PartitionSpec as P

C1 = 128
C2 = 256
LAT = 128
GROUPS = 32
FR = 2
HT = 8
WT = 8
CLIP_DEV = 2
LROWS = 32


epsilon = 1e-05
layout = ("NDHWC", "DHWIO", "NDHWC")


def conv_local(inputs, kernel, stride):
    return lax.conv_general_dilated(
        inputs,
        kernel,
        (1, stride, stride),
        ((2, 0), (1, 1), (1, 1)),
        dimension_numbers=layout,
        preferred_element_type=jnp.float32,
    )


def group_sums(values):
    tiles = values.shape[0]
    width = values.shape[-1]
    grouped = values.reshape(tiles, -1, GROUPS, width // GROUPS)
    return (jnp.sum(grouped, axis=(1, 3)), jnp.sum(grouped * grouped, axis=(1, 3)))


def finish_stats(totals, totals_sq, tile_count, per_tile):
    voxels = tile_count * per_tile
    means = totals / voxels[:, None]
    variance = totals_sq / voxels[:, None] - means * means
    return (means, lax.rsqrt(variance + epsilon))


def clip_params(sums, squares, member, per_tile):
    precise = lax.Precision.HIGHEST
    totals = jnp.dot(member.T, sums, precision=precise)
    totals_sq = jnp.dot(member.T, squares, precision=precise)
    tile_count = jnp.sum(member, axis=0)
    totals, totals_sq, tile_count = lax.psum((totals, totals_sq, tile_count), ("slab", "dev"))
    means, scales = finish_stats(totals, totals_sq, tile_count, per_tile)
    return (jnp.dot(member, means, precision=precise), jnp.dot(member, scales, precision=precise))


def normalize(values, means, scales, gain, offset):
    tiles = values.shape[0]
    width = values.shape[-1]
    grouped = values.astype(jnp.float32).reshape(tiles, -1, GROUPS, width // GROUPS)
    scaled = (grouped - means[:, None, :, None]) * scales[:, None, :, None]
    result = scaled.reshape(values.shape) * gain + offset
    return jax.nn.silu(result).astype(jnp.bfloat16)


def arrival_rank(targets):
    order = jnp.arange(targets.shape[0])
    earlier = (targets[None, :] == targets[:, None]) & (order[None, :] < order[:, None])
    return jnp.sum(earlier.astype(jnp.int32), axis=1)


def encode(tiles, clips, weights):
    (
        conv_first,
        gain_first,
        bias_first,
        conv_down,
        gain_second,
        bias_second,
        project,
        project_bias,
    ) = weights
    how_many = tiles.shape[0]
    block_size = math.gcd(32, how_many)
    blocks = how_many // block_size
    clip_total = CLIP_DEV * lax.axis_size("slab") * lax.axis_size("dev")
    member = (clips[:, None] == jnp.arange(clip_total, dtype=jnp.int32)[None, :]).astype(
        jnp.float32
    )

    def first_section(inputs):
        hidden = conv_local(inputs, conv_first, 1).astype(jnp.bfloat16)
        sums, squares = group_sums(hidden.astype(jnp.float32))
        return (hidden, sums, squares)

    first_out, sums_a, squares_a = lax.map(
        first_section, tiles.reshape(blocks, block_size, FR, HT, WT, 3)
    )
    means_a, scales_a = clip_params(
        sums_a.reshape(how_many, GROUPS),
        squares_a.reshape(how_many, GROUPS),
        member,
        FR * HT * WT * (C1 // GROUPS),
    )

    def second_section(packet):
        hidden, means, scales = packet
        active = normalize(hidden, means, scales, gain_first, bias_first)
        down = conv_local(active, conv_down, 2).astype(jnp.bfloat16)
        sums, squares = group_sums(down.astype(jnp.float32))
        return (down, sums, squares)

    second_out, sums_b, squares_b = lax.map(
        second_section,
        (
            first_out,
            means_a.reshape(blocks, block_size, GROUPS),
            scales_a.reshape(blocks, block_size, GROUPS),
        ),
    )
    means_b, scales_b = clip_params(
        sums_b.reshape(how_many, GROUPS),
        squares_b.reshape(how_many, GROUPS),
        member,
        LROWS * (C2 // GROUPS),
    )

    def third_section(packet):
        hidden, means, scales = packet
        active = normalize(hidden, means, scales, gain_second, bias_second)
        flat = active.reshape(-1, C2)
        latent = jnp.dot(flat, project, preferred_element_type=jnp.float32) + project_bias
        return latent.astype(jnp.bfloat16).reshape(block_size, LROWS, LAT)

    latents = lax.map(
        third_section,
        (
            second_out,
            means_b.reshape(blocks, block_size, GROUPS),
            scales_b.reshape(blocks, block_size, GROUPS),
        ),
    ).reshape(how_many, LROWS, LAT)
    live = clips >= 0
    return jnp.where(live[:, None, None], latents, jnp.zeros_like(latents))


def per_device(
    pixels,
    tile_clip,
    tile_encoder,
    slot_owner,
    conv_first,
    gain_first,
    bias_first,
    conv_down,
    gain_second,
    bias_second,
    project,
    project_bias,
):
    weights = (
        conv_first,
        gain_first,
        bias_first,
        conv_down,
        gain_second,
        bias_second,
        project,
        project_bias,
    )
    group_width = lax.axis_size("dev")
    slots = slot_owner.shape[0]
    capacity = slots // group_width
    encoder = tile_encoder[:, 0]
    owner = slot_owner[:, 0]
    owner_rank = arrival_rank(owner)
    place = encoder * capacity + arrival_rank(encoder)
    target = owner * capacity + owner_rank
    pixel_slots = jnp.zeros((slots, pixels.shape[1]), jnp.bfloat16).at[place].set(pixels)
    clip_slots = jnp.full((slots,), -1, jnp.int32).at[place].set(tile_clip)
    arrived, arrived_clip = (
        lax.all_to_all(
            pixel_slots.reshape(group_width, capacity, pixels.shape[1]),
            "dev",
            split_axis=0,
            concat_axis=0,
            tiled=True,
        ),
        lax.all_to_all(
            clip_slots.reshape(group_width, capacity),
            "dev",
            split_axis=0,
            concat_axis=0,
            tiled=True,
        ),
    )
    latents = encode(arrived.reshape(slots, FR, HT, WT, 3), arrived_clip.reshape(slots), weights)
    outgoing = jnp.zeros((slots, LROWS, LAT), jnp.bfloat16).at[target].set(latents)
    received = lax.all_to_all(
        outgoing.reshape(group_width, capacity, LROWS, LAT),
        "dev",
        split_axis=0,
        concat_axis=0,
        tiled=True,
    )
    return received.reshape(slots * LROWS, LAT)


def solution(mesh):
    in_specs = (
        P(("slab", "dev"), None),
        P(("slab", "dev")),
        P(("slab", "dev"), None),
        P(("slab", "dev"), None),
        P(),
        P(),
        P(),
        P(),
        P(),
        P(),
        P(),
        P(),
    )
    out_specs = P(("slab", "dev"), None)
    return jax.shard_map(
        per_device, mesh=mesh, in_specs=in_specs, out_specs=out_specs, check_vma=False
    )
```

profile of v0, /device:TPU:1, one launch (start us, length us, event | category | flops | bytes accessed | tf_op | source)
XLA Modules:
  0.0 736.7 jit_solution(13731434651015779585)
XLA Ops:
  6.5 0.9 convert_reduce_fusion.4
  7.4 0.7 fusion.61
  8.1 0.9 scatter_custom_fusion
  9.0 0.8 all_to_all.12
  9.7 13.1 %all-to-all-start = ((s32[64,1,2]{2,1,0:T(1,128)}), s32[64,1,2]{2,1,0:T(1,128)S(1)}, u32[]{:S(2)}, u32[]{:S(2)}) async-start(s32[64,1,2]{2,1,0:T(1,128)} %bitcast.27), calls=%async_computation | async-start | bytes 65536 | tf_op jit(solution)/shard_map/all_to_all | solution.py:190
  22.9 0.9 convert_reduce_fusion.3
  23.8 1.0 scatter_custom_fusion.1
  24.8 0.7 reshape.99
  25.5 6.6 all-to-all-done
  32.1 4.7 all-to-all-start.1
  36.9 0.7 fusion.60
  37.5 0.5 broadcast.78
  38.1 0.7 reduce.11
  39.0 77.7 %psum.39 = f32[512]{0:T(512)S(1)} all-reduce(f32[512]{0:T(512)S(1)} %convert_reduce_fusion.2), channel_id=1, replica_groups=mesh['slab'=4,'dev'=64] {'slab','dev'}, use_global_device_ids=true, to_apply=%region_12.13 | all-reduce | flops 512 | bytes 4096 | tf_op jit(solution)/shard_map/psum | solution.py:53
  116.7 9.8 %reshape_reshape.3 = bf16[4,32,2,8,8,3]{5,4,3,2,1,0:T(8,128)(2,1)} reshape(bf16[64,2,384]{2,1,0:T(2,128)(2,1)S(1)} %all-to-all-done.1) | data formatting | bytes 196608 | tf_op jit(solution)/shard_map/reshape;reshape | solution.py:98
  126.5 6.0 copy.71
  132.5 12.5 %while.38 = (s32[]{:T(128)}, bf16[4,32,2,8,8,128]{5,1,4,3,2,0:T(8,128)(2,1)}, f32[4,32,32]{1,0,2:T(4,128)S(1)}, f32[4,32,32]{1,0,2:T(4,128)S(1)}, bf16[4,32,2,8,...) while((s32[]{:T(128)}, ...), condition=%wide.region_9.10_spmd, body=%wide.region_4.9_spmd.sunk | while | flops 38303744 | bytes 3461229 | solution.py:97
  132.6 2.3 bitcast_dynamic-update-slice_fusion.4
  135.7 2.3 bitcast_dynamic-update-slice_fusion.4
  138.8 2.3 bitcast_dynamic-update-slice_fusion.4
  141.9 2.3 bitcast_dynamic-update-slice_fusion.4
  145.1 0.9 fusion.31
  146.1 0.9 fusion.33
  147.3 241.2 %all-reduce.7.cloned.1.call-done = (f32[512,32]{0,1:T(8,128)}, f32[512,32]{0,1:T(8,128)}) async-done(((f32[512,32]{0,1:T(8,128)}, f32[512,32]{0,1:T(8,128)}), (f32[512,32]{0,1:T(8,128)}, f32[512,32]{0,1:T(8,128)})) %all-reduce.7.cloned.1.call-update) | async-done | bytes 131088 | tf_op jit(solution)/shard_map/psum | solution.py:53
  388.5 1.2 fusion.32
  389.6 1.1 fusion.30
  391.1 20.0 %while.39 = (s32[]{:T(128)}, bf16[4,32,2,4,4,256]{5,1,4,3,2,0:T(8,128)(2,1)}, f32[4,32,32]{1,0,2:T(4,128)S(1)}, f32[4,32,32]{1,0,2:T(4,128)S(1)}, bf16[4,32,2,8,...) while((s32[]{:T(128)}, ...), condition=%wide.region_19.20_spmd, body=%wide.region_14.19_spmd.sunk | while | flops 767817728 | bytes 4835457 | solution.py:114
  391.3 4.2 bitcast_dynamic-update-slice_fusion.5
  396.4 4.2 bitcast_dynamic-update-slice_fusion.5
  401.4 4.1 bitcast_dynamic-update-slice_fusion.5
  406.4 4.1 bitcast_dynamic-update-slice_fusion.5
  411.2 0.9 fusion.27
  412.2 0.9 fusion.29
  413.2 242.8 %all-reduce.5.cloned.1.call-done = (f32[512,32]{0,1:T(8,128)}, f32[512,32]{0,1:T(8,128)}) async-done(((f32[512,32]{0,1:T(8,128)}, f32[512,32]{0,1:T(8,128)}), (f32[512,32]{0,1:T(8,128)}, f32[512,32]{0,1:T(8,128)})) %all-reduce.5.cloned.1.call-update) | async-done | bytes 131088 | tf_op jit(solution)/shard_map/psum | solution.py:53
  655.9 1.2 fusion.28
  657.1 1.1 fusion.26
  658.5 27.5 %while.40 = (s32[]{:T(128)}, bf16[4,32,32,128]{3,2,1,0:T(8,128)(2,1)}, bf16[4,32,2,4,4,256]{5,1,4,3,2,0:T(8,128)(2,1)}, f32[4,32,32]{1,0,2:T(4,128)S(1)}, f32[4,...) while((s32[]{:T(128)}, ...), condition=%wide.region_23.24_spmd, body=%wide.region_22.23_spmd.sunk | while | flops 69992448 | bytes 16346221 | solution.py:136
  658.8 0.4 mul.229
  659.8 1.2 dynamic-slice_convert_fusion.2
  661.0 0.7 copy.112
  661.6 1.4 reshape.151
  663.0 1.7 fusion.84
  664.7 0.7 constant_dynamic-update-slice_fusion.2
  666.7 1.2 dynamic-slice_convert_fusion.2
  667.8 0.7 copy.112
  668.5 1.4 reshape.151
  669.9 1.7 fusion.84
  671.6 0.7 constant_dynamic-update-slice_fusion.2
  673.2 0.4 sub.95
  673.6 1.2 dynamic-slice_convert_fusion.2
  674.7 0.7 copy.112
  675.4 1.4 reshape.151
  676.8 1.7 fusion.84
  678.5 0.7 constant_dynamic-update-slice_fusion.2
  680.1 0.4 sub.95
  680.4 1.2 dynamic-slice_convert_fusion.2
  681.6 0.7 copy.112
  682.3 1.4 reshape.151
  683.6 1.7 fusion.84
  685.3 0.7 constant_dynamic-update-slice_fusion.2
  686.1 1.4 bitcast_select_fusion
  687.6 4.5 scatter_fusion
  692.1 36.8 %all_to_all.19 = bf16[64,2,32,128]{3,2,1,0:T(8,128)(2,1)S(1)} all-to-all(bf16[64,2,32,128]{3,2,1,0:T(8,128)(2,1)S(1)} %bitcast.144), channel_id=1, replica_groups=mesh['slab'=4,'dev'=64] {'dev'}, dimensions={0} | all-to-all | bytes 2097152 | tf_op jit(solution)/shard_map/all_to_all | solution.py:200
  728.9 1.0 copy.160
  (150 shorter events, 11.7 us)
Async XLA Ops:
  9.7 22.4 %all-to-all-start = ((s32[64,1,2]{2,1,0:T(1,128)}), s32[64,1,2]{2,1,0:T(1,128)S(1)}, u32[]{:S(2)}, u32[]{:S(2)}) async-start(s32[64,1,2]{2,1,0:T(1,128)} %bitcast.27), calls=%async_computation | async-start | bytes 65536 | tf_op jit(solution)/shard_map/all_to_all | solution.py:190
  32.1 84.6 %all-to-all-start.1 = ((bf16[64,2,384]{2,1,0:T(2,128)(2,1)}), bf16[64,2,384]{2,1,0:T(2,128)(2,1)S(1)}, u32[]{:S(2)}, u32[]{:S(2)}) async-start(bf16[64,2,384]{2,1,0:T(2,128)(2,1)} %reshape.99), calls=%async_computation.1 | async-start | bytes 196608 | tf_op jit(solution)/shard_map/all_to_all | solution.py:183
  36.8 351.6 %all-reduce.7.cloned.1.call-start = ((), (), s32[]{:S(2)}) async-start(), calls=%async_computation.4 | async-start | bytes 262144 | tf_op jit(solution)/shard_map/psum | solution.py:53
  126.5 6.0 copy-start
  132.5 258.5 %copy-start.1 = (bf16[3,3,3,128,256]{4,3,2,1,0:T(8,128)(2,1)S(1)}, bf16[3,3,3,128,256]{4,3,2,1,0:T(8,128)(2,1)}, u32[]{:S(2)}) copy-start(bf16[3,3,3,128,256]{4,3,2,1,0:T(8,128)(2,1)} %param.25) | copy-start | bytes 5308420
  132.5 258.5 %copy-start.5 = (f32[128]{0:T(128)S(1)}, f32[128]{0:T(128)}, u32[]{:S(2)}) copy-start(f32[128]{0:T(128)} %param.23) | copy-start | bytes 1540
  132.5 258.5 %copy-start.6 = (f32[128]{0:T(128)S(1)}, f32[128]{0:T(128)}, u32[]{:S(2)}) copy-start(f32[128]{0:T(128)} %param.24) | copy-start | bytes 1540
  147.0 508.9 %all-reduce.5.cloned.1.call-start = ((), (), s32[]{:S(2)}) async-start(), calls=%async_computation.3 | async-start | bytes 262144 | tf_op jit(solution)/shard_map/psum | solution.py:53
  391.1 267.4 %copy-start.2 = (bf16[256,128]{1,0:T(8,128)(2,1)S(1)}, bf16[256,128]{1,0:T(8,128)(2,1)}, u32[]{:S(2)}) copy-start(bf16[256,128]{1,0:T(8,128)(2,1)} %param.28) | copy-start | bytes 196612
  391.1 267.4 %copy-start.3 = (f32[256]{0:T(256)S(1)}, f32[256]{0:T(256)}, u32[]{:S(2)}) copy-start(f32[256]{0:T(256)} %param.26) | copy-start | bytes 3076
  391.1 267.4 %copy-start.4 = (f32[256]{0:T(256)S(1)}, f32[256]{0:T(256)}, u32[]{:S(2)}) copy-start(f32[256]{0:T(256)} %param.27) | copy-start | bytes 3076
  391.1 267.4 %copy-start.7 = (f32[128]{0:T(128)S(1)}, f32[128]{0:T(128)}, u32[]{:S(2)}) copy-start(f32[128]{0:T(128)} %param.29) | copy-start | bytes 1540
Sparse Core Ops, SparseCore 0:
  147.2 241.2 all-reduce.6
  413.3 242.6 all-reduce.4
where the time goes:
time: 738 us; the launch traced here: 737 us
  waiting for transfers between devices  491 us (67%)
  blocking collectives  114 us (15%)
  local copies, waits for them, and re-layouts  45.8 us (6%)
  matrix products  40.6 us (6%)
  starting transfers between devices  18.1 us (2%)
  between operations  13.8 us (2%)
  other arithmetic  12.6 us (2%)
    psum x2, waiting for transfers between devices, clip_params(): lax.psum((totals, totals_sq, tile_count), ('slab', 'dev'))  484 us
    psum x1, blocking collectives, clip_params(): lax.psum((totals, totals_sq, tile_count), ('slab', 'dev'))  77.7 us
    all_to_all x1, blocking collectives, per_device(): lax.all_to_all(outgoing.reshape(group_width, capacity, LROWS, LAT), 'dev'...  36.8 us
    conv_general_dilated x8, matrix products, conv_local(): lax.conv_general_dilated(inputs, kernel, (1, stride, stride), ((2, 0), (1...  25.7 us
  transfers between devices with their start and end apart: 4, of which 3 were waited for; matrix products, arithmetic and copies ran while one was open for 1% of the time, Pallas kernels for 0%

commit v1 on v0

v1 whole, which is shorter than its diff:
```python
import jax
import jax.numpy as jnp
from jax import lax
from jax.sharding import PartitionSpec as P

C1 = 128
C2 = 256
LAT = 128
GROUPS = 32
FR = 2
HT = 8
WT = 8
LROWS = 32
AXES = ("slab", "dev")


epsilon = 1e-05
layout = ("NDHWC", "DHWIO", "NDHWC")
precise = lax.Precision.HIGHEST


def conv_local(inputs, kernel, stride):
    return lax.conv_general_dilated(
        inputs,
        kernel,
        (1, stride, stride),
        ((2, 0), (1, 1), (1, 1)),
        dimension_numbers=layout,
        preferred_element_type=jnp.float32,
    )


def group_sums(values):
    tiles = values.shape[0]
    width = values.shape[-1]
    grouped = values.reshape(tiles, -1, GROUPS, width // GROUPS)
    return (jnp.sum(grouped, axis=(1, 3)), jnp.sum(grouped * grouped, axis=(1, 3)))


def shifted(x, shift, n):
    if shift > 0:
        perm = [(i, i + shift) for i in range(n - shift)]
    else:
        perm = [(i, i + shift) for i in range(-shift, n)]
    return lax.ppermute(x, AXES, perm)


def clip_totals(clips, stats):
    n = lax.axis_size("slab") * lax.axis_size("dev")
    member = (clips[:, None] == clips[None, :]).astype(jnp.float32)
    own = jnp.dot(member, stats, precision=precise)
    clip_f = clips.astype(jnp.float32)
    to_right = jnp.concatenate([clip_f[-1:], own[-1]])[None, :]
    to_left = jnp.concatenate([clip_f[:1], own[0]])[None, :]
    received = jnp.concatenate(
        [
            shifted(to_right, 1, n),
            shifted(to_right, 2, n),
            shifted(to_left, -1, n),
            shifted(to_left, -2, n),
        ],
        axis=0,
    )
    match = (clip_f[:, None] == received[None, :, 0]).astype(jnp.float32)
    return own + jnp.dot(match, received[:, 1:], precision=precise)


def finish_stats(totals, per_tile):
    voxels = totals[:, -1:] * per_tile
    means = totals[:, :GROUPS] / voxels
    variance = totals[:, GROUPS : 2 * GROUPS] / voxels - means * means
    return (means, lax.rsqrt(variance + epsilon))


def normalize(values, means, scales, gain, offset):
    tiles = values.shape[0]
    width = values.shape[-1]
    grouped = values.astype(jnp.float32).reshape(tiles, -1, GROUPS, width // GROUPS)
    scaled = (grouped - means[:, None, :, None]) * scales[:, None, :, None]
    result = scaled.reshape(values.shape) * gain + offset
    return jax.nn.silu(result).astype(jnp.bfloat16)


def arrival_rank(targets):
    order = jnp.arange(targets.shape[0])
    earlier = (targets[None, :] == targets[:, None]) & (order[None, :] < order[:, None])
    return jnp.sum(earlier.astype(jnp.int32), axis=1)


def encode(tiles, clips, weights):
    (
        conv_first,
        gain_first,
        bias_first,
        conv_down,
        gain_second,
        bias_second,
        project,
        project_bias,
    ) = weights
    how_many = tiles.shape[0]
    ones = jnp.ones((how_many, 1), jnp.float32)

    hidden = conv_local(tiles, conv_first, 1).astype(jnp.bfloat16)
    sums, squares = group_sums(hidden.astype(jnp.float32))
    totals = clip_totals(clips, jnp.concatenate([sums, squares, ones], axis=1))
    means, scales = finish_stats(totals, FR * HT * WT * (C1 // GROUPS))
    active = normalize(hidden, means, scales, gain_first, bias_first)

    down = conv_local(active, conv_down, 2).astype(jnp.bfloat16)
    sums, squares = group_sums(down.astype(jnp.float32))
    totals = clip_totals(clips, jnp.concatenate([sums, squares, ones], axis=1))
    means, scales = finish_stats(totals, LROWS * (C2 // GROUPS))
    active = normalize(down, means, scales, gain_second, bias_second)

    flat = active.reshape(-1, C2)
    latent = jnp.dot(flat, project, preferred_element_type=jnp.float32) + project_bias
    return latent.astype(jnp.bfloat16).reshape(how_many, LROWS, LAT)


def per_device(
    pixels,
    tile_clip,
    tile_encoder,
    slot_owner,
    conv_first,
    gain_first,
    bias_first,
    conv_down,
    gain_second,
    bias_second,
    project,
    project_bias,
):
    weights = (
        conv_first,
        gain_first,
        bias_first,
        conv_down,
        gain_second,
        bias_second,
        project,
        project_bias,
    )
    group_width = lax.axis_size("dev")
    slots = slot_owner.shape[0]
    capacity = slots // group_width
    encoder = tile_encoder[:, 0]
    owner = slot_owner[:, 0]
    place = encoder * capacity + arrival_rank(encoder)
    target = owner * capacity + arrival_rank(owner)

    tiles = pixels.reshape(pixels.shape[0], FR, HT, WT, 3)
    latents = encode(tiles, tile_clip, weights)

    outgoing = jnp.zeros((slots, LROWS, LAT), jnp.bfloat16).at[place].set(latents)
    arrived = lax.all_to_all(
        outgoing.reshape(group_width, capacity, LROWS, LAT),
        "dev",
        split_axis=0,
        concat_axis=0,
        tiled=True,
    ).reshape(slots, LROWS, LAT)
    forward = jnp.zeros((slots, LROWS, LAT), jnp.bfloat16).at[target].set(arrived)
    received = lax.all_to_all(
        forward.reshape(group_width, capacity, LROWS, LAT),
        "dev",
        split_axis=0,
        concat_axis=0,
        tiled=True,
    )
    return received.reshape(slots * LROWS, LAT)


def solution(mesh):
    in_specs = (
        P(AXES, None),
        P(AXES),
        P(AXES, None),
        P(AXES, None),
        P(),
        P(),
        P(),
        P(),
        P(),
        P(),
        P(),
        P(),
    )
    out_specs = P(AXES, None)
    return jax.shard_map(
        per_device, mesh=mesh, in_specs=in_specs, out_specs=out_specs, check_vma=False
    )
```

time: 738 us -> 145 us (0.20)
  waiting for transfers between devices: 491 us -> 35.6 us
  blocking collectives: 114 us -> 34.5 us
  matrix products: 40.6 us -> 9.12 us
  local copies, waits for them, and re-layouts: 45.8 us -> 22.2 us
  starting transfers between devices: 18.1 us -> 38.2 us
  between operations: 13.8 us -> 0.48 us
  other arithmetic: 12.6 us -> 3.94 us
    psum x2 -> x0, waiting for transfers between devices: 484 us -> none  [clip_params(): lax.psum((totals, totals_sq, tile_count), ('slab', 'dev'))]
    psum x1 -> x0, blocking collectives: 77.7 us -> none  [clip_params(): lax.psum((totals, totals_sq, tile_count), ('slab', 'dev'))]
    ppermute x0 -> x8, starting transfers between devices: none -> 24.1 us  [shifted(): return lax.ppermute(x, AXES, perm)]
    all_to_all x2 -> x1, waiting for transfers between devices: 6.6 us -> 28.3 us  [per_device(): lax.all_to_all(outgoing.reshape(group_width, capacity, LROWS, LAT), 'dev'...]
    conv_general_dilated x8 -> x2, matrix products: 25.7 us -> 7.72 us  [conv_local(): lax.conv_general_dilated(inputs, kernel, (1, stride, stride), ((2, 0), (1...]
    dot_general x12 -> x5, matrix products: 15 us -> 1.4 us  [the longest x2 0.61 us: clip_totals(): return own + jnp.dot(match, received[:, 1:], precision=precise)]
    scatter x3 -> x2, local copies, waits for them, and re-layouts: 6.35 us -> 15.2 us  [the longest x1 9.72 us: per_device(): jnp.zeros((slots, LROWS, LAT), jnp.bfloat16).at[target].set(arrived)]
    while x5 -> x0, local copies, waits for them, and re-layouts: 8.7 us -> none  [the longest x1 6 us: encode(): lax.map(first_section, tiles.reshape(blocks, block_size, FR, HT, WT, 3))]
  transfers between devices with their start and end apart: 4 -> 9, of which waited for: 3 -> 5; matrix products, arithmetic and copies ran while one was open for 1% -> 1% of each run, Pallas kernels for 0% -> 0%
where the time goes in v1:
time: 145 us; the launch traced here: 144 us
  starting transfers between devices  38.2 us (26%)
  waiting for transfers between devices  35.6 us (25%)
  blocking collectives  34.5 us (24%)
  local copies, waits for them, and re-layouts  22.2 us (15%)
  matrix products  9.12 us (6%)
  other arithmetic  3.94 us (3%)
    all_to_all x1, blocking collectives, per_device(): lax.all_to_all(forward.reshape(group_width, capacity, LROWS, LAT), 'dev',...  34.5 us
    all_to_all x1, waiting for transfers between devices, per_device(): lax.all_to_all(outgoing.reshape(group_width, capacity, LROWS, LAT), 'dev'...  28.3 us
    ppermute x8, starting transfers between devices, shifted(): return lax.ppermute(x, AXES, perm)  24.1 us
    all_to_all x1, starting transfers between devices, per_device(): lax.all_to_all(outgoing.reshape(group_width, capacity, LROWS, LAT), 'dev'...  14.1 us
    scatter x1, local copies, waits for them, and re-layouts, per_device(): jnp.zeros((slots, LROWS, LAT), jnp.bfloat16).at[target].set(arrived)  9.72 us
    conv_general_dilated x2, matrix products, conv_local(): lax.conv_general_dilated(inputs, kernel, (1, stride, stride), ((2, 0), (1...  7.72 us
    ppermute x8, waiting for transfers between devices, shifted(): return lax.ppermute(x, AXES, perm)  7.3 us
    scatter x1, local copies, waits for them, and re-layouts, per_device(): jnp.zeros((slots, LROWS, LAT), jnp.bfloat16).at[place].set(latents)  5.5 us
  transfers between devices with their start and end apart: 9, of which 5 were waited for; matrix products, arithmetic and copies ran while one was open for 1% of the time, Pallas kernels for 0%

profile of v1, /device:TPU:1, one launch (start us, length us, event | category | flops | bytes accessed | tf_op | source)
XLA Modules:
  0.0 144.0 jit_solution(10381132903046124562)
XLA Ops:
  0.0 1.0 copy.52
  1.0 0.1 reshape.53
  1.1 0.0 copy-start.8
  1.1 0.0 copy-start.9
  1.1 0.0 copy-start.6
  1.1 0.0 copy-start.7
  1.1 3.3 %convert_reduce_fusion = (f32[48,128]{1,0:T(8,128)S(1)}, f32[48,128]{1,0:T(8,128)S(1)}, bf16[48,2,8,8,128]{4,0,3,2,1:T(8,128)(2,1)}) fusion(bf16[48,2,8,8,3]{0,4,3,2,1:T(4,128)(2,1)S(1)} %reshape.53, bf16[3,3,3,3,128]{4,3,2,1,0:T(4,128)(2,1)} %param.16), kind=kOutput, calls=%fused_computation.4 | convolution fusion | flops 57446400 | bytes 1679616 | tf_op jit(solution)/shard_map/conv_general_dilated | solution.py:23
  4.5 0.1 copy.53
  4.6 0.1 copy.54
  4.8 0.1 pad.21.clone
  4.9 0.2 fusion.27
  5.1 0.6 fusion.67
  5.7 0.7 maximum_bitcast_fusion
  6.4 4.9 %collective-permute-start = (f32[1,66]{1,0:T(1,128)S(1)}, f32[1,66]{1,0:T(1,128)S(1)}, u32[]{:S(2)}, u32[]{:S(2)}) collective-permute-start(f32[1,66]{1,0:T(1,128)S(1)} %maximum_bitcast_fusion), channel_id=1, source_target_pairs={{0,1},{1,2},{2,3},{3,4},{4,5},{5,6},{6,7},{7,8},{8,9},{9,10},{10,1... | collective-permute-start | bytes 800 | tf_op jit(solution)/shard_map/ppermute | solution.py:45
  11.3 3.5 %collective-permute-start.1 = (f32[1,66]{1,0:T(1,128)S(1)}, f32[1,66]{1,0:T(1,128)S(1)}, u32[]{:S(2)}, u32[]{:S(2)}) collective-permute-start(f32[1,66]{1,0:T(1,128)S(1)} %maximum_bitcast_fusion), channel_id=1, source_target_pairs={{0,2},{1,3},{2,4},{3,5},{4,6},{5,7},{6,8},{7,9},{8,10},{9,11},{10,... | collective-permute-start | bytes 800 | tf_op jit(solution)/shard_map/ppermute | solution.py:45
  14.9 0.7 maximum_bitcast_fusion.1
  15.6 1.9 %collective-permute-start.2 = (f32[1,66]{1,0:T(1,128)S(1)}, f32[1,66]{1,0:T(1,128)S(1)}, u32[]{:S(2)}, u32[]{:S(2)}) collective-permute-start(f32[1,66]{1,0:T(1,128)S(1)} %maximum_bitcast_fusion.1), channel_id=1, source_target_pairs={{1,0},{2,1},{3,2},{4,3},{5,4},{6,5},{7,6},{8,7},{9,8},{10,9},{11,1... | collective-permute-start | bytes 800 | tf_op jit(solution)/shard_map/ppermute | solution.py:45
  17.5 1.3 collective-permute-start.3
  18.8 0.2 convert_reduce_fusion.3
  19.0 0.1 copy.55
  19.1 1.4 collective-permute-done.2
  20.4 1.5 %collective-permute-done.3 = f32[1,66]{1,0:T(1,128)S(1)} collective-permute-done((f32[1,66]{1,0:T(1,128)S(1)}, f32[1,66]{1,0:T(1,128)S(1)}, u32[]{:S(2)}, u32[]{:S(2)}) %collective-permute-start.3) | collective-permute-done | bytes 296 | tf_op jit(solution)/shard_map/ppermute | solution.py:45
  22.0 0.1 slice_reduce_fusion.1
  22.1 0.3 convolution_add_fusion.2
  22.5 0.1 copy.57
  22.6 0.1 copy.58
  22.6 0.0 copy-done.6
  22.7 4.4 %convert_reduce_fusion.1 = (f32[48,256]{1,0:T(8,128)S(1)}, f32[48,256]{1,0:T(8,128)S(1)}, bf16[48,2,4,4,256]{4,0,3,2,1:T(8,128)(2,1)S(1)}) fusion(bf16[3,3,3,128,256]{4,3,2,1,0:T(8,128)(2,1)S(1)} %copy-done, bf16[48,2,8,8,128]{4,0,3,2,1:T(8,128)(2,1)} %get-tuple-element.19, f32[128]{0:T(128)S(1)} %copy-done.6, f32[128]{0:T(128)S(1)} %copy-done.7, ...), kind=kOutput, calls=%fused_computation.19 | convolution fusion | flops 1151705088 | bytes 4277248 | tf_op jit(solution)/shard_map/conv_general_dilated | solution.py:23
  27.1 0.0 copy-start.3
  27.1 0.0 copy-start.4
  27.1 0.1 copy.59
  27.2 0.1 copy.60
  27.3 0.1 bitcast_reduce_fusion
  27.4 0.2 fusion.32
  27.6 0.7 maximum_bitcast_fusion.2
  28.4 4.6 %collective-permute-start.4 = (f32[1,66]{1,0:T(1,128)S(1)}, f32[1,66]{1,0:T(1,128)S(1)}, u32[]{:S(2)}, u32[]{:S(2)}) collective-permute-start(f32[1,66]{1,0:T(1,128)S(1)} %maximum_bitcast_fusion.2), channel_id=1, source_target_pairs={{0,1},{1,2},{2,3},{3,4},{4,5},{5,6},{6,7},{7,8},{8,9},{9,10},{10,1... | collective-permute-start | bytes 800 | tf_op jit(solution)/shard_map/ppermute | solution.py:45
  33.0 4.7 %collective-permute-start.5 = (f32[1,66]{1,0:T(1,128)S(1)}, f32[1,66]{1,0:T(1,128)S(1)}, u32[]{:S(2)}, u32[]{:S(2)}) collective-permute-start(f32[1,66]{1,0:T(1,128)S(1)} %maximum_bitcast_fusion.2), channel_id=1, source_target_pairs={{0,2},{1,3},{2,4},{3,5},{4,6},{5,7},{6,8},{7,9},{8,10},{9,11},{10,... | collective-permute-start | bytes 800 | tf_op jit(solution)/shard_map/ppermute | solution.py:45
  37.6 0.7 maximum_bitcast_fusion.3
  38.3 1.9 %collective-permute-start.6 = (f32[1,66]{1,0:T(1,128)S(1)}, f32[1,66]{1,0:T(1,128)S(1)}, u32[]{:S(2)}, u32[]{:S(2)}) collective-permute-start(f32[1,66]{1,0:T(1,128)S(1)} %maximum_bitcast_fusion.3), channel_id=1, source_target_pairs={{1,0},{2,1},{3,2},{4,3},{5,4},{6,5},{7,6},{8,7},{9,8},{10,9},{11,1... | collective-permute-start | bytes 800 | tf_op jit(solution)/shard_map/ppermute | solution.py:45
  40.2 1.3 collective-permute-start.7
  41.5 0.1 copy.61
  41.6 1.5 %collective-permute-done.6 = f32[1,66]{1,0:T(1,128)S(1)} collective-permute-done((f32[1,66]{1,0:T(1,128)S(1)}, f32[1,66]{1,0:T(1,128)S(1)}, u32[]{:S(2)}, u32[]{:S(2)}) %collective-permute-start.6) | collective-permute-done | bytes 296 | tf_op jit(solution)/shard_map/ppermute | solution.py:45
  43.2 2.8 %collective-permute-done.7 = f32[1,66]{1,0:T(1,128)S(1)} collective-permute-done((f32[1,66]{1,0:T(1,128)S(1)}, f32[1,66]{1,0:T(1,128)S(1)}, u32[]{:S(2)}, u32[]{:S(2)}) %collective-permute-start.7) | collective-permute-done | bytes 296 | tf_op jit(solution)/shard_map/ppermute | solution.py:45
  46.0 0.1 slice_reduce_fusion
  46.2 0.3 convolution_add_fusion.1
  46.5 0.1 copy.63
  46.6 0.1 copy.64
  46.7 0.5 fusion.20
  47.3 0.0 copy-start.2
  47.3 0.0 copy-start.5
  47.3 0.4 copy.65
  47.7 0.2 reshape.54
  47.9 0.2 copy-done.2
  48.1 0.4 fusion.10
  48.5 1.1 broadcast.36.clone
  49.6 5.5 %scatter_fusion = bf16[128,32,128]{2,1,0:T(8,128)(2,1)} fusion(bf16[128,32,128]{2,1,0:T(8,128)(2,1)} %broadcast.36.clone, s32[48]{0:T(128)S(1)} %fusion.61, bf16[48,32,128]{2,1,0:T(8,128)(2,1)S(1)} %bitcast.62), kind=kCustom, calls=%fused_computation | custom fusion | bytes 1179840 | tf_op jit(solution)/shard_map/scatter | solution.py:156
  55.1 14.1 %all-to-all-start = ((bf16[64,2,32,128]{3,2,1,0:T(8,128)(2,1)}), bf16[64,2,32,128]{3,2,1,0:T(8,128)(2,1)S(1)}, u32[]{:S(2)}, u32[]{:S(2)}) async-start(bf16[64,2,32,128]{3,2,1,0:T(8,128)(2,1)} %bitcast.25), calls=%async_computation | async-start | bytes 2097152 | tf_op jit(solution)/shard_map/all_to_all | solution.py:157
  69.2 0.2 convert_reduce_fusion.2
  69.4 28.3 %all-to-all-done = bf16[64,2,32,128]{3,2,1,0:T(8,128)(2,1)S(1)} async-done(((bf16[64,2,32,128]{3,2,1,0:T(8,128)(2,1)}), bf16[64,2,32,128]{3,2,1,0:T(8,128)(2,1)S(1)}, u32[]{:S(2)}, u32[]{:S(2)}) %all-to-all-start) | async-done | bytes 1048608 | tf_op jit(solution)/shard_map/all_to_all | solution.py:157
  97.7 1.0 copy-done.1
  98.7 0.1 broadcast.36
  98.8 9.7 %scatter_fusion.1 = bf16[128,32,128]{2,1,0:T(8,128)(2,1)S(1)} fusion(bf16[128,32,128]{2,1,0:T(8,128)(2,1)S(1)} %broadcast.36, s32[128]{0:T(128)S(1)} %fusion.60, bf16[128,32,128]{2,1,0:T(8,128)(2,1)} %bitcast.60), kind=kCustom, calls=%fused_computation.1 | custom fusion | bytes 3146240 | tf_op jit(solution)/shard_map/scatter | solution.py:164
  108.5 34.5 %all_to_all.10 = bf16[64,2,32,128]{3,2,1,0:T(8,128)(2,1)S(1)} all-to-all(bf16[64,2,32,128]{3,2,1,0:T(8,128)(2,1)S(1)} %bitcast.59), channel_id=1, replica_groups=mesh['slab'=4,'dev'=64] {'dev'}, dimensions={0} | all-to-all | bytes 2097152 | tf_op jit(solution)/shard_map/all_to_all | solution.py:165
  143.1 1.0 copy.71
  (32 shorter events, 0.3 us)
Async XLA Ops:
  0.0 22.6 %copy-start = (bf16[3,3,3,128,256]{4,3,2,1,0:T(8,128)(2,1)S(1)}, bf16[3,3,3,128,256]{4,3,2,1,0:T(8,128)(2,1)}, u32[]{:S(2)}) copy-start(bf16[3,3,3,128,256]{4,3,2,1,0:T(8,128)(2,1)} %param.19) | copy-start | bytes 5308420
  1.1 3.7 %copy-start.8 = (s32[48]{0:T(128)S(1)}, s32[48]{0:T(128)}, u32[]{:S(2)}) copy-start(s32[48]{0:T(128)} %param.13) | copy-start | bytes 580
  1.1 17.7 %copy-start.9 = (s32[48,1]{0,1:T(1,128)S(1)}, s32[48,1]{0,1:T(1,128)}, u32[]{:S(2)}) copy-start(s32[48,1]{0,1:T(1,128)} %param.14) | copy-start | bytes 580
  1.1 21.5 %copy-start.6 = (f32[128]{0:T(128)S(1)}, f32[128]{0:T(128)}, u32[]{:S(2)}) copy-start(f32[128]{0:T(128)} %param.18) | copy-start | bytes 1540
  1.1 21.5 %copy-start.7 = (f32[128]{0:T(128)S(1)}, f32[128]{0:T(128)}, u32[]{:S(2)}) copy-start(f32[128]{0:T(128)} %param.17) | copy-start | bytes 1540
  6.4 12.6 %collective-permute-start = (f32[1,66]{1,0:T(1,128)S(1)}, f32[1,66]{1,0:T(1,128)S(1)}, u32[]{:S(2)}, u32[]{:S(2)}) collective-permute-start(f32[1,66]{1,0:T(1,128)S(1)} %maximum_bitcast_fusion), channel_id=1, source_target_pairs={{0,1},{1,2},{2,3},{3,4},{4,5},{5,6},{6,7},{7,8},{8,9},{9,10},{10,1... | collective-permute-start | bytes 800 | tf_op jit(solution)/shard_map/ppermute | solution.py:45
  11.3 7.7 %collective-permute-start.1 = (f32[1,66]{1,0:T(1,128)S(1)}, f32[1,66]{1,0:T(1,128)S(1)}, u32[]{:S(2)}, u32[]{:S(2)}) collective-permute-start(f32[1,66]{1,0:T(1,128)S(1)} %maximum_bitcast_fusion), channel_id=1, source_target_pairs={{0,2},{1,3},{2,4},{3,5},{4,6},{5,7},{6,8},{7,9},{8,10},{9,11},{10,... | collective-permute-start | bytes 800 | tf_op jit(solution)/shard_map/ppermute | solution.py:45
  15.6 4.9 %collective-permute-start.2 = (f32[1,66]{1,0:T(1,128)S(1)}, f32[1,66]{1,0:T(1,128)S(1)}, u32[]{:S(2)}, u32[]{:S(2)}) collective-permute-start(f32[1,66]{1,0:T(1,128)S(1)} %maximum_bitcast_fusion.1), channel_id=1, source_target_pairs={{1,0},{2,1},{3,2},{4,3},{5,4},{6,5},{7,6},{8,7},{9,8},{10,9},{11,1... | collective-permute-start | bytes 800 | tf_op jit(solution)/shard_map/ppermute | solution.py:45
  17.5 4.5 %collective-permute-start.3 = (f32[1,66]{1,0:T(1,128)S(1)}, f32[1,66]{1,0:T(1,128)S(1)}, u32[]{:S(2)}, u32[]{:S(2)}) collective-permute-start(f32[1,66]{1,0:T(1,128)S(1)} %maximum_bitcast_fusion.1), channel_id=1, source_target_pairs={{2,0},{3,1},{4,2},{5,3},{6,4},{7,5},{8,6},{9,7},{10,8},{11,9},{12,... | collective-permute-start | bytes 800 | tf_op jit(solution)/shard_map/ppermute | solution.py:45
  27.1 19.6 %copy-start.3 = (f32[256]{0:T(256)S(1)}, f32[256]{0:T(256)}, u32[]{:S(2)}) copy-start(f32[256]{0:T(256)} %param.21) | copy-start | bytes 3076
  27.1 19.6 %copy-start.4 = (f32[256]{0:T(256)S(1)}, f32[256]{0:T(256)}, u32[]{:S(2)}) copy-start(f32[256]{0:T(256)} %param.20) | copy-start | bytes 3076
  28.4 13.3 %collective-permute-start.4 = (f32[1,66]{1,0:T(1,128)S(1)}, f32[1,66]{1,0:T(1,128)S(1)}, u32[]{:S(2)}, u32[]{:S(2)}) collective-permute-start(f32[1,66]{1,0:T(1,128)S(1)} %maximum_bitcast_fusion.2), channel_id=1, source_target_pairs={{0,1},{1,2},{2,3},{3,4},{4,5},{5,6},{6,7},{7,8},{8,9},{9,10},{10,1... | collective-permute-start | bytes 800 | tf_op jit(solution)/shard_map/ppermute | solution.py:45
  33.0 8.7 %collective-permute-start.5 = (f32[1,66]{1,0:T(1,128)S(1)}, f32[1,66]{1,0:T(1,128)S(1)}, u32[]{:S(2)}, u32[]{:S(2)}) collective-permute-start(f32[1,66]{1,0:T(1,128)S(1)} %maximum_bitcast_fusion.2), channel_id=1, source_target_pairs={{0,2},{1,3},{2,4},{3,5},{4,6},{5,7},{6,8},{7,9},{8,10},{9,11},{10,... | collective-permute-start | bytes 800 | tf_op jit(solution)/shard_map/ppermute | solution.py:45
  38.3 4.9 %collective-permute-start.6 = (f32[1,66]{1,0:T(1,128)S(1)}, f32[1,66]{1,0:T(1,128)S(1)}, u32[]{:S(2)}, u32[]{:S(2)}) collective-permute-start(f32[1,66]{1,0:T(1,128)S(1)} %maximum_bitcast_fusion.3), channel_id=1, source_target_pairs={{1,0},{2,1},{3,2},{4,3},{5,4},{6,5},{7,6},{8,7},{9,8},{10,9},{11,1... | collective-permute-start | bytes 800 | tf_op jit(solution)/shard_map/ppermute | solution.py:45
  40.2 5.8 %collective-permute-start.7 = (f32[1,66]{1,0:T(1,128)S(1)}, f32[1,66]{1,0:T(1,128)S(1)}, u32[]{:S(2)}, u32[]{:S(2)}) collective-permute-start(f32[1,66]{1,0:T(1,128)S(1)} %maximum_bitcast_fusion.3), channel_id=1, source_target_pairs={{2,0},{3,1},{4,2},{5,3},{6,4},{7,5},{8,6},{9,7},{10,8},{11,9},{12,... | collective-permute-start | bytes 800 | tf_op jit(solution)/shard_map/ppermute | solution.py:45
  47.3 0.8 copy-start.2
  47.3 0.8 copy-start.5
  49.6 19.6 %copy-start.10 = (s32[128,1]{0,1:T(1,128)S(1)}, s32[128,1]{0,1:T(1,128)}, u32[]{:S(2)}) copy-start(s32[128,1]{0,1:T(1,128)} %param.15) | copy-start | bytes 1540
  55.1 42.6 %all-to-all-start = ((bf16[64,2,32,128]{3,2,1,0:T(8,128)(2,1)}), bf16[64,2,32,128]{3,2,1,0:T(8,128)(2,1)S(1)}, u32[]{:S(2)}, u32[]{:S(2)}) async-start(bf16[64,2,32,128]{3,2,1,0:T(8,128)(2,1)} %bitcast.25), calls=%async_computation | async-start | bytes 2097152 | tf_op jit(solution)/shard_map/all_to_all | solution.py:157
  97.7 1.0 copy-start.1

commit v2 on v1

--- a/solution.py
+++ b/solution.py
@@ -87,35 +87,36 @@
     return jnp.sum(earlier.astype(jnp.int32), axis=1)
 
 
-def encode(tiles, clips, weights):
-    (
-        conv_first,
-        gain_first,
-        bias_first,
-        conv_down,
-        gain_second,
-        bias_second,
-        project,
-        project_bias,
-    ) = weights
-    how_many = tiles.shape[0]
-    ones = jnp.ones((how_many, 1), jnp.float32)
-
+def route(values, place, slots):
+    pick = (jnp.arange(slots, dtype=jnp.int32)[:, None] == place[None, :]).astype(values.dtype)
+    if values.dtype == jnp.float32:
+        moved = jnp.dot(pick, values, precision=precise)
+    else:
+        moved = jnp.dot(pick, values, preferred_element_type=jnp.float32)
+    return moved.astype(values.dtype)
+
+
+def to_encoders(values, group_width, capacity):
+    shape = values.shape
+    moved = lax.all_to_all(
+        values.reshape((group_width, capacity) + shape[1:]),
+        "dev",
+        split_axis=0,
+        concat_axis=0,
+        tiled=True,
+    )
+    return moved.reshape(shape)
+
+
+def first_conv(tiles, conv_first):
     hidden = conv_local(tiles, conv_first, 1).astype(jnp.bfloat16)
-    sums, squares = group_sums(hidden.astype(jnp.float32))
-    totals = clip_totals(clips, jnp.concatenate([sums, squares, ones], axis=1))
-    means, scales = finish_stats(totals, FR * HT * WT * (C1 // GROUPS))
+    return hidden, group_sums(hidden.astype(jnp.float32))
+
+
+def second_conv(hidden, means, scales, gain_first, bias_first, conv_down):
     active = normalize(hidden, means, scales, gain_first, bias_first)
-
     down = conv_local(active, conv_down, 2).astype(jnp.bfloat16)
-    sums, squares = group_sums(down.astype(jnp.float32))
-    totals = clip_totals(clips, jnp.concatenate([sums, squares, ones], axis=1))
-    means, scales = finish_stats(totals, LROWS * (C2 // GROUPS))
-    active = normalize(down, means, scales, gain_second, bias_second)
-
-    flat = active.reshape(-1, C2)
-    latent = jnp.dot(flat, project, preferred_element_type=jnp.float32) + project_bias
-    return latent.astype(jnp.bfloat16).reshape(how_many, LROWS, LAT)
+    return down, group_sums(down.astype(jnp.float32))
 
 
 def per_device(
@@ -132,43 +133,50 @@
     project,
     project_bias,
 ):
-    weights = (
-        conv_first,
-        gain_first,
-        bias_first,
-        conv_down,
-        gain_second,
-        bias_second,
-        project,
-        project_bias,
-    )
     group_width = lax.axis_size("dev")
     slots = slot_owner.shape[0]
     capacity = slots // group_width
+    how_many = pixels.shape[0]
     encoder = tile_encoder[:, 0]
     owner = slot_owner[:, 0]
     place = encoder * capacity + arrival_rank(encoder)
     target = owner * capacity + arrival_rank(owner)
-
-    tiles = pixels.reshape(pixels.shape[0], FR, HT, WT, 3)
-    latents = encode(tiles, tile_clip, weights)
-
-    outgoing = jnp.zeros((slots, LROWS, LAT), jnp.bfloat16).at[place].set(latents)
-    arrived = lax.all_to_all(
-        outgoing.reshape(group_width, capacity, LROWS, LAT),
-        "dev",
-        split_axis=0,
-        concat_axis=0,
-        tiled=True,
-    ).reshape(slots, LROWS, LAT)
-    forward = jnp.zeros((slots, LROWS, LAT), jnp.bfloat16).at[target].set(arrived)
-    received = lax.all_to_all(
-        forward.reshape(group_width, capacity, LROWS, LAT),
-        "dev",
-        split_axis=0,
-        concat_axis=0,
-        tiled=True,
-    )
+    ones = jnp.ones((how_many, 1), jnp.float32)
+
+    slot_pixels = to_encoders(route(pixels, place, slots), group_width, capacity)
+
+    tiles = pixels.reshape(how_many, FR, HT, WT, 3)
+    hidden, (sums, squares) = first_conv(tiles, conv_first)
+    totals = clip_totals(tile_clip, jnp.concatenate([sums, squares, ones], axis=1))
+    means_a, scales_a = finish_stats(totals, FR * HT * WT * (C1 // GROUPS))
+    slot_a = to_encoders(
+        route(jnp.concatenate([means_a, scales_a], axis=1), place, slots), group_width, capacity
+    )
+    down, (sums, squares) = second_conv(hidden, means_a, scales_a, gain_first, bias_first, conv_down)
+    totals = clip_totals(tile_clip, jnp.concatenate([sums, squares, ones], axis=1))
+    means_b, scales_b = finish_stats(totals, LROWS * (C2 // GROUPS))
+    slot_b = to_encoders(
+        route(jnp.concatenate([means_b, scales_b, ones], axis=1), place, slots),
+        group_width,
+        capacity,
+    )
+
+    slot_tiles = slot_pixels.reshape(slots, FR, HT, WT, 3)
+    slot_hidden, _ = first_conv(slot_tiles, conv_first)
+    slot_down, _ = second_conv(
+        slot_hidden, slot_a[:, :GROUPS], slot_a[:, GROUPS:], gain_first, bias_first, conv_down
+    )
+    active = normalize(
+        slot_down, slot_b[:, :GROUPS], slot_b[:, GROUPS : 2 * GROUPS], gain_second, bias_second
+    )
+    flat = active.reshape(-1, C2)
+    latent = jnp.dot(flat, project, preferred_element_type=jnp.float32) + project_bias
+    latent = latent.astype(jnp.bfloat16).reshape(slots, LROWS * LAT)
+    live = slot_b[:, 2 * GROUPS :] > 0.5
+    latent = jnp.where(live, latent, jnp.zeros_like(latent))
+
+    forward = route(latent, target, slots)
+    received = to_encoders(forward, group_width, capacity)
     return received.reshape(slots * LROWS, LAT)
 
 

time: 145 us -> 189 us (1.30)
  matrix products: 9.12 us -> 44.3 us
  starting transfers between devices: 38.2 us -> 51.5 us
  waiting for transfers between devices: 35.6 us -> 25.6 us
  local copies, waits for them, and re-layouts: 22.2 us -> 28 us
    conv_general_dilated x2 -> x4, matrix products: 7.72 us -> 37.1 us  [conv_local(): lax.conv_general_dilated(inputs, kernel, (1, stride, stride), ((2, 0), (1...]
    scatter x2 -> x0, local copies, waits for them, and re-layouts: 15.2 us -> none  [the longest x1 9.72 us: per_device(): jnp.zeros((slots, LROWS, LAT), jnp.bfloat16).at[target].set(arrived)]
    all_to_all x1 -> x3, starting transfers between devices: 14.1 us -> 27.5 us  [to_encoders(): lax.all_to_all(values.reshape((group_width, capacity) + shape[1:]), 'dev'...]
    another operation x2, local copies, waits for them, and re-layouts: 1.24 us -> 12.4 us  [the longest x1 9.76 us: per_device(): slot_tiles = slot_pixels.reshape(slots, FR, HT, WT, 3)]
    reshape x2 -> x5, local copies, waits for them, and re-layouts: 0.25 us -> 7.78 us  [the longest x1 4.01 us: per_device(): flat = active.reshape(-1, C2)]
    ppermute x8, waiting for transfers between devices: 7.3 us -> 0.02 us  [shifted(): return lax.ppermute(x, AXES, perm)]
    dot_general x1 -> x5, matrix products: 0.36 us -> 6.22 us  [the longest x2 2.87 us: route(): moved = jnp.dot(pick, values, preferred_element_type=jnp.float32)]
    all_to_all x1 -> x3, waiting for transfers between devices: 28.3 us -> 25.6 us  [to_encoders(): lax.all_to_all(values.reshape((group_width, capacity) + shape[1:]), 'dev'...]
  transfers between devices with their start and end apart: 9 -> 11, of which waited for: 5 -> 3; matrix products, arithmetic and copies ran while one was open for 1% -> 4% of each run, Pallas kernels for 0% -> 0%
where the time goes in v2:
time: 189 us; the launch traced here: 188 us
  starting transfers between devices  51.5 us (27%)
  matrix products  44.3 us (23%)
  blocking collectives  32.9 us (17%)
  local copies, waits for them, and re-layouts  28 us (15%)
  waiting for transfers between devices  25.6 us (14%)
  other arithmetic  5 us (3%)
    conv_general_dilated x4, matrix products, conv_local(): lax.conv_general_dilated(inputs, kernel, (1, stride, stride), ((2, 0), (1...  37.1 us
    all_to_all x1, blocking collectives, to_encoders(): lax.all_to_all(values.reshape((group_width, capacity) + shape[1:]), 'dev'...  32.9 us
    all_to_all x3, starting transfers between devices, to_encoders(): lax.all_to_all(values.reshape((group_width, capacity) + shape[1:]), 'dev'...  27.5 us
    all_to_all x3, waiting for transfers between devices, to_encoders(): lax.all_to_all(values.reshape((group_width, capacity) + shape[1:]), 'dev'...  25.6 us
    ppermute x8, starting transfers between devices, shifted(): return lax.ppermute(x, AXES, perm)  23.9 us
    another operation x1, local copies, waits for them, and re-layouts, per_device(): slot_tiles = slot_pixels.reshape(slots, FR, HT, WT, 3)  9.76 us
    reshape x1, local copies, waits for them, and re-layouts, per_device(): flat = active.reshape(-1, C2)  4.01 us
  transfers between devices with their start and end apart: 11, of which 3 were waited for; matrix products, arithmetic and copies ran while one was open for 4% of the time, Pallas kernels for 0%

profile of v2, /device:TPU:1, one launch (start us, length us, event | category | flops | bytes accessed | tf_op | source)
XLA Modules:
  0.0 187.8 jit_solution(15106913369505011329)
XLA Ops:
  0.1 0.8 convert_element_type.65
  0.8 0.6 fusion.83
  1.4 0.9 copy.99
  2.4 3.3 %convert_reduce_fusion = (f32[48,128]{1,0:T(8,128)S(1)}, f32[48,128]{1,0:T(8,128)S(1)}, bf16[48,2,8,8,128]{4,0,3,2,1:T(8,128)(2,1)}) fusion(bf16[48,2,8,8,3]{0,4,3,2,1:T(4,128)(2,1)S(1)} %reshape.79, bf16[3,3,3,3,128]{4,3,2,1,0:T(4,128)(2,1)} %param.16), kind=kOutput, calls=%fused_computation.6 | convolution fusion | flops 57446400 | bytes 1679616 | tf_op jit(solution)/shard_map/conv_general_dilated | solution.py:23
  5.7 0.1 copy.100
  5.8 0.1 copy.101
  6.1 0.2 fusion.27
  6.4 0.7 maximum_bitcast_fusion.1
  7.1 1.3 collective-permute-start.3
  8.4 5.1 %collective-permute-start.2 = (f32[1,66]{1,0:T(1,128)S(1)}, f32[1,66]{1,0:T(1,128)S(1)}, u32[]{:S(2)}, u32[]{:S(2)}) collective-permute-start(f32[1,66]{1,0:T(1,128)S(1)} %maximum_bitcast_fusion.1), channel_id=1, source_target_pairs={{1,0},{2,1},{3,2},{4,3},{5,4},{6,5},{7,6},{8,7},{9,8},{10,9},{11,1... | collective-permute-start | bytes 800 | tf_op jit(solution)/shard_map/ppermute | solution.py:45
  13.5 0.7 maximum_bitcast_fusion
  14.2 4.3 %collective-permute-start.1 = (f32[1,66]{1,0:T(1,128)S(1)}, f32[1,66]{1,0:T(1,128)S(1)}, u32[]{:S(2)}, u32[]{:S(2)}) collective-permute-start(f32[1,66]{1,0:T(1,128)S(1)} %maximum_bitcast_fusion), channel_id=1, source_target_pairs={{0,2},{1,3},{2,4},{3,5},{4,6},{5,7},{6,8},{7,9},{8,10},{9,11},{10,... | collective-permute-start | bytes 800 | tf_op jit(solution)/shard_map/ppermute | solution.py:45
  18.4 2.0 %collective-permute-start = (f32[1,66]{1,0:T(1,128)S(1)}, f32[1,66]{1,0:T(1,128)S(1)}, u32[]{:S(2)}, u32[]{:S(2)}) collective-permute-start(f32[1,66]{1,0:T(1,128)S(1)} %maximum_bitcast_fusion), channel_id=1, source_target_pairs={{0,1},{1,2},{2,3},{3,4},{4,5},{5,6},{6,7},{7,8},{8,9},{9,10},{10,1... | collective-permute-start | bytes 800 | tf_op jit(solution)/shard_map/ppermute | solution.py:45
  20.5 0.2 convert_reduce_fusion.2
  20.7 0.2 convert_reduce_fusion.3
  20.9 0.2 convolution_convert_fusion.2
  21.0 0.1 copy.102
  21.1 0.7 reshape.82
  21.8 0.1 slice_reduce_fusion.1
  22.0 0.3 convolution_add_fusion.2
  22.3 0.2 fusion.23
  22.7 4.4 %convert_reduce_fusion.1 = (f32[48,256]{1,0:T(8,128)S(1)}, f32[48,256]{1,0:T(8,128)S(1)}) fusion(bf16[3,3,3,128,256]{4,3,2,1,0:T(8,128)(2,1)S(1)} %copy-done, bf16[48,2,8,8,128]{4,0,3,2,1:T(8,128)(2,1)} %get-tuple-element.23, f32[128]{0:T(128)S(1)} %copy-done.10, f32[128]{0:T(128)S(1)} %copy-done.11, f32[48,128]{1,0:T(8,128)S(1)} %copy.105, ...), kind=kOutput, calls=%fused_computation.22 | convolution fusion | flops 1151705088 | bytes 3490816 | tf_op jit(solution)/shard_map/conv_general_dilated | solution.py:23
  27.1 0.1 copy.106
  27.2 0.1 copy.107
  27.3 0.1 bitcast_reduce_fusion
  27.4 0.2 fusion.32
  27.6 0.7 maximum_bitcast_fusion.3
  28.3 1.3 collective-permute-start.7
  29.6 2.3 %collective-permute-start.6 = (f32[1,66]{1,0:T(1,128)S(1)}, f32[1,66]{1,0:T(1,128)S(1)}, u32[]{:S(2)}, u32[]{:S(2)}) collective-permute-start(f32[1,66]{1,0:T(1,128)S(1)} %maximum_bitcast_fusion.3), channel_id=1, source_target_pairs={{1,0},{2,1},{3,2},{4,3},{5,4},{6,5},{7,6},{8,7},{9,8},{10,9},{11,1... | collective-permute-start | bytes 800 | tf_op jit(solution)/shard_map/ppermute | solution.py:45
  31.9 0.7 maximum_bitcast_fusion.2
  32.6 4.3 %collective-permute-start.5 = (f32[1,66]{1,0:T(1,128)S(1)}, f32[1,66]{1,0:T(1,128)S(1)}, u32[]{:S(2)}, u32[]{:S(2)}) collective-permute-start(f32[1,66]{1,0:T(1,128)S(1)} %maximum_bitcast_fusion.2), channel_id=1, source_target_pairs={{0,2},{1,3},{2,4},{3,5},{4,6},{5,7},{6,8},{7,9},{8,10},{9,11},{10,... | collective-permute-start | bytes 800 | tf_op jit(solution)/shard_map/ppermute | solution.py:45
  36.9 3.5 %collective-permute-start.4 = (f32[1,66]{1,0:T(1,128)S(1)}, f32[1,66]{1,0:T(1,128)S(1)}, u32[]{:S(2)}, u32[]{:S(2)}) collective-permute-start(f32[1,66]{1,0:T(1,128)S(1)} %maximum_bitcast_fusion.2), channel_id=1, source_target_pairs={{0,1},{1,2},{2,3},{3,4},{4,5},{5,6},{6,7},{7,8},{8,9},{9,10},{10,1... | collective-permute-start | bytes 800 | tf_op jit(solution)/shard_map/ppermute | solution.py:45
  40.3 0.1 copy.108
  40.4 0.7 reshape.92
  41.1 18.4 %all-to-all-start.2 = ((f32[64,1,128]{2,1,0:T(1,128)}), f32[64,1,128]{2,1,0:T(1,128)S(1)}, u32[]{:S(2)}, u32[]{:S(2)}) async-start(f32[64,1,128]{2,1,0:T(1,128)} %reshape.92), calls=%async_computation.2 | async-start | bytes 65536 | tf_op jit(solution)/shard_map/all_to_all | solution.py:101
  59.6 0.1 slice_reduce_fusion
  59.7 0.3 convolution_add_fusion.1
  60.0 0.9 fusion.24
  60.9 7.9 %all-to-all-done.2 = f32[64,1,128]{2,1,0:T(1,128)S(1)} async-done(((f32[64,1,128]{2,1,0:T(1,128)}), f32[64,1,128]{2,1,0:T(1,128)S(1)}, u32[]{:S(2)}, u32[]{:S(2)}) %all-to-all-start.2) | async-done | bytes 32800 | tf_op jit(solution)/shard_map/all_to_all | solution.py:101
  68.8 4.7 %all-to-all-start = ((f32[64,2,65]{2,1,0:T(2,128)}), f32[64,2,65]{2,1,0:T(2,128)S(1)}, u32[]{:S(2)}, u32[]{:S(2)}) async-start(f32[64,2,65]{2,1,0:T(2,128)} %bitcast.18), calls=%async_computation | async-start | bytes 131072 | tf_op jit(solution)/shard_map/all_to_all | solution.py:101
  73.5 0.5 broadcast.62
  74.1 0.7 reduce.14
  74.8 0.1 reshape.93
  74.9 0.1 fusion.81
  75.1 0.1 copy.116
  75.2 0.1 copy.114
  75.3 8.1 %all-to-all-done = f32[64,2,65]{2,1,0:T(2,128)S(1)} async-done(((f32[64,2,65]{2,1,0:T(2,128)}), f32[64,2,65]{2,1,0:T(2,128)S(1)}, u32[]{:S(2)}, u32[]{:S(2)}) %all-to-all-start) | async-done | bytes 33312 | tf_op jit(solution)/shard_map/all_to_all | solution.py:101
  83.4 4.5 %all-to-all-start.1 = ((bf16[64,2,384]{2,1,0:T(2,128)(2,1)}), bf16[64,2,384]{2,1,0:T(2,128)(2,1)S(1)}, u32[]{:S(2)}, u32[]{:S(2)}) async-start(bf16[64,2,384]{2,1,0:T(2,128)(2,1)} %reshape.82), calls=%async_computation.1 | async-start | bytes 196608 | tf_op jit(solution)/shard_map/all_to_all | solution.py:101
  87.9 0.1 fusion.82
  88.2 0.1 copy.120
  88.3 0.1 copy.118
  88.4 0.2 fusion.26
  88.5 9.6 %all-to-all-done.1 = bf16[64,2,384]{2,1,0:T(2,128)(2,1)S(1)} async-done(((bf16[64,2,384]{2,1,0:T(2,128)(2,1)}), bf16[64,2,384]{2,1,0:T(2,128)(2,1)S(1)}, u32[]{:S(2)}, u32[]{:S(2)}) %all-to-all-start.1) | async-done | bytes 98336 | tf_op jit(solution)/shard_map/all_to_all | solution.py:101
  98.2 9.8 %reshape_reshape.6 = bf16[128,2,8,8,3]{4,3,2,1,0:T(8,128)(2,1)} reshape(bf16[64,2,384]{2,1,0:T(2,128)(2,1)S(1)} %all-to-all-done.1) | data formatting | bytes 196608 | tf_op jit(solution)/shard_map/reshape;reshape | solution.py:164
  107.9 19.9 %fusion.1 = bf16[128,2,8,8,128]{4,0,3,2,1:T(8,128)(2,1)S(1)} fusion(bf16[3,3,3,3,128]{4,3,2,1,0:T(4,128)(2,1)S(1)} %copy-done.3, bf16[128,2,8,8,3]{4,3,2,1,0:T(8,128)(2,1)} %reshape_reshape.6), kind=kOutput, calls=%fused_computation.7 | convolution fusion | flops 142737408 | bytes 4313344 | tf_op jit(solution)/shard_map/conv_general_dilated | solution.py:23
  127.8 9.5 %multiply_convert_fusion.1 = bf16[128,2,4,4,256]{4,0,3,2,1:T(8,128)(2,1)S(1)} fusion(f32[256]{0:T(256)S(1)} %copy-done.5, f32[256]{0:T(256)S(1)} %copy-done.6, f32[128,256]{1,0:T(8,128)S(1)} %copy.120, f32[128,256]{1,0:T(8,128)S(1)} %copy.118, bf16[3,3,3,128,256]{4,3,2,1,0:T(8,128)(2,1)S(1)} %copy-done, f32[128]{0:T(128)S(1)} %copy-done.10, ...), kind=kOutput, calls=%fused_computation.9 | convolution fusion | flops 3077570560 | bytes 8457216 | tf_op jit(solution)/shard_map/conv_general_dilated | solution.py:23
  137.3 3.0 %copy.121 = bf16[128,2,4,4,256]{4,3,2,1,0:T(4,128)(2,1)} copy(bf16[128,2,4,4,256]{4,0,3,2,1:T(8,128)(2,1)S(1)} %multiply_convert_fusion.1) | data formatting | bytes 4194304 | tf_op jit(solution)/shard_map/convert_element_type | solution.py:81
  140.3 4.0 %reshape.85 = bf16[4096,256]{1,0:T(8,128)(2,1)} reshape(bf16[128,2,4,4,256]{4,3,2,1,0:T(4,128)(2,1)} %copy.121) | data formatting | bytes 4194304 | tf_op jit(solution)/shard_map/reshape | solution.py:172
  144.3 2.3 %fusion = bf16[4096,128]{1,0:T(8,128)(2,1)S(1)} fusion(bf16[4096,256]{1,0:T(8,128)(2,1)} %reshape.85, bf16[256,128]{1,0:T(8,128)(2,1)S(1)} %copy-done.2, f32[128]{0:T(128)S(1)} %copy-done.4), kind=kOutput, calls=%fused_computation.2 | convolution fusion | flops 269484032 | bytes 3211776 | tf_op jit(solution)/shard_map/dot_general | solution.py:173
  146.6 1.3 reshape.86
  147.9 2.7 %convolution_convert_fusion = bf16[128,4096]{1,0:T(8,128)(2,1)} fusion(bf16[128,4096]{1,0:T(8,128)(2,1)} %reshape.86, pred[128]{0:T(512)(128)(4,1)S(1)} %fusion.26, s32[128]{0:T(128)S(1)} %multiply_add_fusion.1), kind=kOutput, calls=%fused_computation.3 | convolution fusion | flops 135282688 | bytes 2097792 | tf_op jit(solution)/shard_map/dot_general | solution.py:95
  150.6 1.7 reshape.87
  152.3 32.9 %all_to_all.20 = bf16[64,2,4096]{2,1,0:T(2,128)(2,1)} all-to-all(bf16[64,2,4096]{2,1,0:T(2,128)(2,1)S(1)} %reshape.87), channel_id=1, replica_groups=mesh['slab'=4,'dev'=64] {'dev'}, dimensions={0} | all-to-all | bytes 2097152 | tf_op jit(solution)/shard_map/all_to_all | solution.py:101
  185.2 2.6 %reshape_reshape.7 = bf16[4096,128]{1,0:T(8,128)(2,1)} reshape(bf16[64,2,4096]{2,1,0:T(2,128)(2,1)} %all_to_all.20) | data formatting | bytes 2097152 | tf_op jit(solution)/shard_map/reshape;reshape | solution.py:180
  (58 shorter events, 0.9 us)
Async XLA Ops:
  0.0 22.7 %copy-start = (bf16[3,3,3,128,256]{4,3,2,1,0:T(8,128)(2,1)S(1)}, bf16[3,3,3,128,256]{4,3,2,1,0:T(8,128)(2,1)}, u32[]{:S(2)}) copy-start(bf16[3,3,3,128,256]{4,3,2,1,0:T(8,128)(2,1)} %param.19) | copy-start | bytes 5308420
  0.0 6.1 %copy-start.9 = (s32[48]{0:T(128)S(1)}, s32[48]{0:T(128)}, u32[]{:S(2)}) copy-start(s32[48]{0:T(128)} %param.13) | copy-start | bytes 580
  0.0 20.8 %copy-start.1 = (bf16[48,384]{1,0:T(8,128)(2,1)S(1)}, bf16[48,384]{1,0:T(8,128)(2,1)}, u32[]{:S(2)}) copy-start(bf16[48,384]{1,0:T(8,128)(2,1)} %param.12) | copy-start | bytes 110596
  0.0 20.4 %copy-start.8 = (s32[128,1]{0,1:T(1,128)S(1)}, s32[128,1]{0,1:T(1,128)}, u32[]{:S(2)}) copy-start(s32[128,1]{0,1:T(1,128)} %param.15) | copy-start | bytes 1540
  0.0 20.6 %copy-start.7 = (s32[48,1]{0,1:T(1,128)S(1)}, s32[48,1]{0,1:T(1,128)}, u32[]{:S(2)}) copy-start(s32[48,1]{0,1:T(1,128)} %param.14) | copy-start | bytes 580
  0.0 22.7 %copy-start.10 = (f32[128]{0:T(128)S(1)}, f32[128]{0:T(128)}, u32[]{:S(2)}) copy-start(f32[128]{0:T(128)} %param.18) | copy-start | bytes 1540
  0.0 22.7 %copy-start.11 = (f32[128]{0:T(128)S(1)}, f32[128]{0:T(128)}, u32[]{:S(2)}) copy-start(f32[128]{0:T(128)} %param.17) | copy-start | bytes 1540
  7.1 14.7 %collective-permute-start.3 = (f32[1,66]{1,0:T(1,128)S(1)}, f32[1,66]{1,0:T(1,128)S(1)}, u32[]{:S(2)}, u32[]{:S(2)}) collective-permute-start(f32[1,66]{1,0:T(1,128)S(1)} %maximum_bitcast_fusion.1), channel_id=1, source_target_pairs={{2,0},{3,1},{4,2},{5,3},{6,4},{7,5},{8,6},{9,7},{10,8},{11,9},{12,... | collective-permute-start | bytes 800 | tf_op jit(solution)/shard_map/ppermute | solution.py:45
  8.4 13.4 %collective-permute-start.2 = (f32[1,66]{1,0:T(1,128)S(1)}, f32[1,66]{1,0:T(1,128)S(1)}, u32[]{:S(2)}, u32[]{:S(2)}) collective-permute-start(f32[1,66]{1,0:T(1,128)S(1)} %maximum_bitcast_fusion.1), channel_id=1, source_target_pairs={{1,0},{2,1},{3,2},{4,3},{5,4},{6,5},{7,6},{8,7},{9,8},{10,9},{11,1... | collective-permute-start | bytes 800 | tf_op jit(solution)/shard_map/ppermute | solution.py:45
  14.2 7.7 %collective-permute-start.1 = (f32[1,66]{1,0:T(1,128)S(1)}, f32[1,66]{1,0:T(1,128)S(1)}, u32[]{:S(2)}, u32[]{:S(2)}) collective-permute-start(f32[1,66]{1,0:T(1,128)S(1)} %maximum_bitcast_fusion), channel_id=1, source_target_pairs={{0,2},{1,3},{2,4},{3,5},{4,6},{5,7},{6,8},{7,9},{8,10},{9,11},{10,... | collective-permute-start | bytes 800 | tf_op jit(solution)/shard_map/ppermute | solution.py:45
  18.4 3.4 %collective-permute-start = (f32[1,66]{1,0:T(1,128)S(1)}, f32[1,66]{1,0:T(1,128)S(1)}, u32[]{:S(2)}, u32[]{:S(2)}) collective-permute-start(f32[1,66]{1,0:T(1,128)S(1)} %maximum_bitcast_fusion), channel_id=1, source_target_pairs={{0,1},{1,2},{2,3},{3,4},{4,5},{5,6},{6,7},{7,8},{8,9},{9,10},{10,1... | collective-permute-start | bytes 800 | tf_op jit(solution)/shard_map/ppermute | solution.py:45
  28.3 31.2 %collective-permute-start.7 = (f32[1,66]{1,0:T(1,128)S(1)}, f32[1,66]{1,0:T(1,128)S(1)}, u32[]{:S(2)}, u32[]{:S(2)}) collective-permute-start(f32[1,66]{1,0:T(1,128)S(1)} %maximum_bitcast_fusion.3), channel_id=1, source_target_pairs={{2,0},{3,1},{4,2},{5,3},{6,4},{7,5},{8,6},{9,7},{10,8},{11,9},{12,... | collective-permute-start | bytes 800 | tf_op jit(solution)/shard_map/ppermute | solution.py:45
  29.6 29.9 %collective-permute-start.6 = (f32[1,66]{1,0:T(1,128)S(1)}, f32[1,66]{1,0:T(1,128)S(1)}, u32[]{:S(2)}, u32[]{:S(2)}) collective-permute-start(f32[1,66]{1,0:T(1,128)S(1)} %maximum_bitcast_fusion.3), channel_id=1, source_target_pairs={{1,0},{2,1},{3,2},{4,3},{5,4},{6,5},{7,6},{8,7},{9,8},{10,9},{11,1... | collective-permute-start | bytes 800 | tf_op jit(solution)/shard_map/ppermute | solution.py:45
  32.6 26.9 %collective-permute-start.5 = (f32[1,66]{1,0:T(1,128)S(1)}, f32[1,66]{1,0:T(1,128)S(1)}, u32[]{:S(2)}, u32[]{:S(2)}) collective-permute-start(f32[1,66]{1,0:T(1,128)S(1)} %maximum_bitcast_fusion.2), channel_id=1, source_target_pairs={{0,2},{1,3},{2,4},{3,5},{4,6},{5,7},{6,8},{7,9},{8,10},{9,11},{10,... | collective-permute-start | bytes 800 | tf_op jit(solution)/shard_map/ppermute | solution.py:45
  36.9 22.7 %collective-permute-start.4 = (f32[1,66]{1,0:T(1,128)S(1)}, f32[1,66]{1,0:T(1,128)S(1)}, u32[]{:S(2)}, u32[]{:S(2)}) collective-permute-start(f32[1,66]{1,0:T(1,128)S(1)} %maximum_bitcast_fusion.2), channel_id=1, source_target_pairs={{0,1},{1,2},{2,3},{3,4},{4,5},{5,6},{6,7},{7,8},{8,9},{9,10},{10,1... | collective-permute-start | bytes 800 | tf_op jit(solution)/shard_map/ppermute | solution.py:45
  41.1 27.7 %all-to-all-start.2 = ((f32[64,1,128]{2,1,0:T(1,128)}), f32[64,1,128]{2,1,0:T(1,128)S(1)}, u32[]{:S(2)}, u32[]{:S(2)}) async-start(f32[64,1,128]{2,1,0:T(1,128)} %reshape.92), calls=%async_computation.2 | async-start | bytes 65536 | tf_op jit(solution)/shard_map/all_to_all | solution.py:101
  68.8 14.6 %all-to-all-start = ((f32[64,2,65]{2,1,0:T(2,128)}), f32[64,2,65]{2,1,0:T(2,128)S(1)}, u32[]{:S(2)}, u32[]{:S(2)}) async-start(f32[64,2,65]{2,1,0:T(2,128)} %bitcast.18), calls=%async_computation | async-start | bytes 131072 | tf_op jit(solution)/shard_map/all_to_all | solution.py:101
  75.0 32.9 %copy-start.3 = (bf16[3,3,3,3,128]{4,3,2,1,0:T(4,128)(2,1)S(1)}, bf16[3,3,3,3,128]{4,3,2,1,0:T(4,128)(2,1)}, u32[]{:S(2)}) copy-start(bf16[3,3,3,3,128]{4,3,2,1,0:T(4,128)(2,1)} %param.16) | copy-start | bytes 62212
  83.4 14.7 %all-to-all-start.1 = ((bf16[64,2,384]{2,1,0:T(2,128)(2,1)}), bf16[64,2,384]{2,1,0:T(2,128)(2,1)S(1)}, u32[]{:S(2)}, u32[]{:S(2)}) async-start(bf16[64,2,384]{2,1,0:T(2,128)(2,1)} %reshape.82), calls=%async_computation.1 | async-start | bytes 196608 | tf_op jit(solution)/shard_map/all_to_all | solution.py:101
  107.9 19.9 %copy-start.5 = (f32[256]{0:T(256)S(1)}, f32[256]{0:T(256)}, u32[]{:S(2)}) copy-start(f32[256]{0:T(256)} %param.21) | copy-start | bytes 3076
  107.9 19.9 %copy-start.6 = (f32[256]{0:T(256)S(1)}, f32[256]{0:T(256)}, u32[]{:S(2)}) copy-start(f32[256]{0:T(256)} %param.20) | copy-start | bytes 3076
  140.3 4.0 %copy-start.2 = (bf16[256,128]{1,0:T(8,128)(2,1)S(1)}, bf16[256,128]{1,0:T(8,128)(2,1)}, u32[]{:S(2)}) copy-start(bf16[256,128]{1,0:T(8,128)(2,1)} %param.22) | copy-start | bytes 196612
  140.3 4.0 %copy-start.4 = (f32[128]{0:T(128)S(1)}, f32[128]{0:T(128)}, u32[]{:S(2)}) copy-start(f32[128]{0:T(128)} %param.23) | copy-start | bytes 1540

commit v3 on v1

--- a/solution.py
+++ b/solution.py
@@ -87,6 +87,11 @@
     return jnp.sum(earlier.astype(jnp.int32), axis=1)
 
 
+def route(values, place, slots):
+    pick = (jnp.arange(slots, dtype=jnp.int32)[:, None] == place[None, :]).astype(values.dtype)
+    return jnp.dot(pick, values, preferred_element_type=jnp.float32).astype(values.dtype)
+
+
 def encode(tiles, clips, weights):
     (
         conv_first,
@@ -150,10 +155,11 @@
     place = encoder * capacity + arrival_rank(encoder)
     target = owner * capacity + arrival_rank(owner)
 
-    tiles = pixels.reshape(pixels.shape[0], FR, HT, WT, 3)
+    how_many = pixels.shape[0]
+    tiles = pixels.reshape(how_many, FR, HT, WT, 3)
     latents = encode(tiles, tile_clip, weights)
 
-    outgoing = jnp.zeros((slots, LROWS, LAT), jnp.bfloat16).at[place].set(latents)
+    outgoing = route(latents.reshape(how_many, LROWS * LAT), place, slots)
     arrived = lax.all_to_all(
         outgoing.reshape(group_width, capacity, LROWS, LAT),
         "dev",
@@ -161,7 +167,7 @@
         concat_axis=0,
         tiled=True,
     ).reshape(slots, LROWS, LAT)
-    forward = jnp.zeros((slots, LROWS, LAT), jnp.bfloat16).at[target].set(arrived)
+    forward = route(arrived.reshape(slots, LROWS * LAT), target, slots)
     received = lax.all_to_all(
         forward.reshape(group_width, capacity, LROWS, LAT),
         "dev",

time: 145 us -> 130 us (0.90)
  local copies, waits for them, and re-layouts: 22.2 us -> 6.35 us
    scatter x2 -> x0, local copies, waits for them, and re-layouts: 15.2 us -> none  [the longest x1 9.72 us: per_device(): jnp.zeros((slots, LROWS, LAT), jnp.bfloat16).at[target].set(arrived)]
where the time goes in v3:
time: 130 us; the launch traced here: 129 us
  starting transfers between devices  38.2 us (29%)
  waiting for transfers between devices  35.6 us (27%)
  blocking collectives  34.5 us (27%)
  matrix products  10.1 us (8%)
  local copies, waits for them, and re-layouts  6.35 us (5%)
  other arithmetic  3.94 us (3%)
    all_to_all x1, blocking collectives, per_device(): lax.all_to_all(forward.reshape(group_width, capacity, LROWS, LAT), 'dev',...  34.5 us
    all_to_all x1, waiting for transfers between devices, per_device(): lax.all_to_all(outgoing.reshape(group_width, capacity, LROWS, LAT), 'dev'...  28.3 us
    ppermute x8, starting transfers between devices, shifted(): return lax.ppermute(x, AXES, perm)  24.1 us
    all_to_all x1, starting transfers between devices, per_device(): lax.all_to_all(outgoing.reshape(group_width, capacity, LROWS, LAT), 'dev'...  14.1 us
    conv_general_dilated x2, matrix products, conv_local(): lax.conv_general_dilated(inputs, kernel, (1, stride, stride), ((2, 0), (1...  7.74 us
    ppermute x8, waiting for transfers between devices, shifted(): return lax.ppermute(x, AXES, perm)  7.3 us
    unnamed x24, local copies, waits for them, and re-layouts  3.72 us
  transfers between devices with their start and end apart: 9, of which 5 were waited for; matrix products, arithmetic and copies ran while one was open for 1% of the time, Pallas kernels for 0%

profile of v3, /device:TPU:1, one launch (start us, length us, event | category | flops | bytes accessed | tf_op | source)
XLA Modules:
  0.0 129.2 jit_solution(13898272757243693226)
XLA Ops:
  0.0 1.0 copy.52
  1.0 0.0 copy-start.8
  1.0 0.1 reshape.61
  1.1 0.0 copy-start.5
  1.1 0.0 copy-start.6
  1.1 3.3 %convert_reduce_fusion = (f32[48,128]{1,0:T(8,128)S(1)}, f32[48,128]{1,0:T(8,128)S(1)}, bf16[48,2,8,8,128]{4,0,3,2,1:T(8,128)(2,1)}) fusion(bf16[48,2,8,8,3]{0,4,3,2,1:T(4,128)(2,1)S(1)} %reshape.61, bf16[3,3,3,3,128]{4,3,2,1,0:T(4,128)(2,1)} %param.16), kind=kOutput, calls=%fused_computation.4 | convolution fusion | flops 57446400 | bytes 1679616 | tf_op jit(solution)/shard_map/conv_general_dilated | solution.py:23
  4.5 0.1 copy.53
  4.6 0.1 copy.54
  4.8 0.1 pad.21.clone
  4.9 0.2 fusion.31
  5.1 0.6 fusion.71
  5.7 0.7 maximum_bitcast_fusion
  6.4 4.9 %collective-permute-start = (f32[1,66]{1,0:T(1,128)S(1)}, f32[1,66]{1,0:T(1,128)S(1)}, u32[]{:S(2)}, u32[]{:S(2)}) collective-permute-start(f32[1,66]{1,0:T(1,128)S(1)} %maximum_bitcast_fusion), channel_id=1, source_target_pairs={{0,1},{1,2},{2,3},{3,4},{4,5},{5,6},{6,7},{7,8},{8,9},{9,10},{10,1... | collective-permute-start | bytes 800 | tf_op jit(solution)/shard_map/ppermute | solution.py:45
  11.4 3.5 %collective-permute-start.1 = (f32[1,66]{1,0:T(1,128)S(1)}, f32[1,66]{1,0:T(1,128)S(1)}, u32[]{:S(2)}, u32[]{:S(2)}) collective-permute-start(f32[1,66]{1,0:T(1,128)S(1)} %maximum_bitcast_fusion), channel_id=1, source_target_pairs={{0,2},{1,3},{2,4},{3,5},{4,6},{5,7},{6,8},{7,9},{8,10},{9,11},{10,... | collective-permute-start | bytes 800 | tf_op jit(solution)/shard_map/ppermute | solution.py:45
  14.9 0.7 maximum_bitcast_fusion.1
  15.6 1.9 %collective-permute-start.2 = (f32[1,66]{1,0:T(1,128)S(1)}, f32[1,66]{1,0:T(1,128)S(1)}, u32[]{:S(2)}, u32[]{:S(2)}) collective-permute-start(f32[1,66]{1,0:T(1,128)S(1)} %maximum_bitcast_fusion.1), channel_id=1, source_target_pairs={{1,0},{2,1},{3,2},{4,3},{5,4},{6,5},{7,6},{8,7},{9,8},{10,9},{11,1... | collective-permute-start | bytes 800 | tf_op jit(solution)/shard_map/ppermute | solution.py:45
  17.5 1.3 %collective-permute-start.3 = (f32[1,66]{1,0:T(1,128)S(1)}, f32[1,66]{1,0:T(1,128)S(1)}, u32[]{:S(2)}, u32[]{:S(2)}) collective-permute-start(f32[1,66]{1,0:T(1,128)S(1)} %maximum_bitcast_fusion.1), channel_id=1, source_target_pairs={{2,0},{3,1},{4,2},{5,3},{6,4},{7,5},{8,6},{9,7},{10,8},{11,9},{12,... | collective-permute-start | bytes 800 | tf_op jit(solution)/shard_map/ppermute | solution.py:45
  18.8 0.2 convert_reduce_fusion.3
  19.0 0.1 copy.55
  19.1 1.4 %collective-permute-done.2 = f32[1,66]{1,0:T(1,128)S(1)} collective-permute-done((f32[1,66]{1,0:T(1,128)S(1)}, f32[1,66]{1,0:T(1,128)S(1)}, u32[]{:S(2)}, u32[]{:S(2)}) %collective-permute-start.2) | collective-permute-done | bytes 296 | tf_op jit(solution)/shard_map/ppermute | solution.py:45
  20.5 1.5 %collective-permute-done.3 = f32[1,66]{1,0:T(1,128)S(1)} collective-permute-done((f32[1,66]{1,0:T(1,128)S(1)}, f32[1,66]{1,0:T(1,128)S(1)}, u32[]{:S(2)}, u32[]{:S(2)}) %collective-permute-start.3) | collective-permute-done | bytes 296 | tf_op jit(solution)/shard_map/ppermute | solution.py:45
  22.0 0.1 slice_reduce_fusion.1
  22.1 0.3 convolution_add_fusion.2
  22.5 0.1 copy.57
  22.6 0.1 copy.58
  22.7 0.0 copy-done.5
  22.7 0.0 copy-start.2
  22.7 0.0 copy-start.3
  22.7 4.4 %convert_reduce_fusion.1 = (f32[48,256]{1,0:T(8,128)S(1)}, f32[48,256]{1,0:T(8,128)S(1)}, bf16[48,2,4,4,256]{4,0,3,2,1:T(8,128)(2,1)S(1)}) fusion(bf16[3,3,3,128,256]{4,3,2,1,0:T(8,128)(2,1)S(1)} %copy-done, bf16[48,2,8,8,128]{4,0,3,2,1:T(8,128)(2,1)} %get-tuple-element.19, f32[128]{0:T(128)S(1)} %copy-done.5, f32[128]{0:T(128)S(1)} %copy-done.6, ...), kind=kOutput, calls=%fused_computation.19 | convolution fusion | flops 1151705088 | bytes 4277248 | tf_op jit(solution)/shard_map/conv_general_dilated | solution.py:23
  27.1 0.1 copy.59
  27.2 0.1 copy.60
  27.3 0.1 bitcast_reduce_fusion
  27.4 0.2 fusion.36
  27.7 0.7 maximum_bitcast_fusion.2
  28.4 4.6 %collective-permute-start.4 = (f32[1,66]{1,0:T(1,128)S(1)}, f32[1,66]{1,0:T(1,128)S(1)}, u32[]{:S(2)}, u32[]{:S(2)}) collective-permute-start(f32[1,66]{1,0:T(1,128)S(1)} %maximum_bitcast_fusion.2), channel_id=1, source_target_pairs={{0,1},{1,2},{2,3},{3,4},{4,5},{5,6},{6,7},{7,8},{8,9},{9,10},{10,1... | collective-permute-start | bytes 800 | tf_op jit(solution)/shard_map/ppermute | solution.py:45
  33.0 4.7 %collective-permute-start.5 = (f32[1,66]{1,0:T(1,128)S(1)}, f32[1,66]{1,0:T(1,128)S(1)}, u32[]{:S(2)}, u32[]{:S(2)}) collective-permute-start(f32[1,66]{1,0:T(1,128)S(1)} %maximum_bitcast_fusion.2), channel_id=1, source_target_pairs={{0,2},{1,3},{2,4},{3,5},{4,6},{5,7},{6,8},{7,9},{8,10},{9,11},{10,... | collective-permute-start | bytes 800 | tf_op jit(solution)/shard_map/ppermute | solution.py:45
  37.6 0.7 maximum_bitcast_fusion.3
  38.3 1.9 %collective-permute-start.6 = (f32[1,66]{1,0:T(1,128)S(1)}, f32[1,66]{1,0:T(1,128)S(1)}, u32[]{:S(2)}, u32[]{:S(2)}) collective-permute-start(f32[1,66]{1,0:T(1,128)S(1)} %maximum_bitcast_fusion.3), channel_id=1, source_target_pairs={{1,0},{2,1},{3,2},{4,3},{5,4},{6,5},{7,6},{8,7},{9,8},{10,9},{11,1... | collective-permute-start | bytes 800 | tf_op jit(solution)/shard_map/ppermute | solution.py:45
  40.2 1.3 %collective-permute-start.7 = (f32[1,66]{1,0:T(1,128)S(1)}, f32[1,66]{1,0:T(1,128)S(1)}, u32[]{:S(2)}, u32[]{:S(2)}) collective-permute-start(f32[1,66]{1,0:T(1,128)S(1)} %maximum_bitcast_fusion.3), channel_id=1, source_target_pairs={{2,0},{3,1},{4,2},{5,3},{6,4},{7,5},{8,6},{9,7},{10,8},{11,9},{12,... | collective-permute-start | bytes 800 | tf_op jit(solution)/shard_map/ppermute | solution.py:45
  41.5 0.1 copy.61
  41.7 1.5 %collective-permute-done.6 = f32[1,66]{1,0:T(1,128)S(1)} collective-permute-done((f32[1,66]{1,0:T(1,128)S(1)}, f32[1,66]{1,0:T(1,128)S(1)}, u32[]{:S(2)}, u32[]{:S(2)}) %collective-permute-start.6) | collective-permute-done | bytes 296 | tf_op jit(solution)/shard_map/ppermute | solution.py:45
  43.2 2.8 %collective-permute-done.7 = f32[1,66]{1,0:T(1,128)S(1)} collective-permute-done((f32[1,66]{1,0:T(1,128)S(1)}, f32[1,66]{1,0:T(1,128)S(1)}, u32[]{:S(2)}, u32[]{:S(2)}) %collective-permute-start.7) | collective-permute-done | bytes 296 | tf_op jit(solution)/shard_map/ppermute | solution.py:45
  46.1 0.1 slice_reduce_fusion
  46.2 0.3 convolution_add_fusion.1
  46.5 0.1 copy.63
  46.6 0.1 copy.64
  46.7 0.6 fusion.20
  47.3 0.0 copy-start.1
  47.3 0.0 copy-start.4
  47.3 0.4 copy.65
  47.7 0.2 reshape.62
  47.9 0.2 copy-done.1
  48.1 0.4 fusion.10
  48.5 0.2 reshape_reshape.6
  48.7 0.4 fusion.26
  49.1 0.0 copy-start.9
  49.1 1.2 copy.68
  50.3 14.1 %all-to-all-start = ((bf16[64,2,32,128]{3,2,1,0:T(8,128)(2,1)}), bf16[64,2,32,128]{3,2,1,0:T(8,128)(2,1)S(1)}, u32[]{:S(2)}, u32[]{:S(2)}) async-start(bf16[64,2,32,128]{3,2,1,0:T(8,128)(2,1)} %bitcast.60), calls=%async_computation | async-start | bytes 2097152 | tf_op jit(solution)/shard_map/all_to_all | solution.py:163
  64.4 0.2 convert_reduce_fusion.2
  64.6 28.3 %all-to-all-done = bf16[64,2,32,128]{3,2,1,0:T(8,128)(2,1)S(1)} async-done(((bf16[64,2,32,128]{3,2,1,0:T(8,128)(2,1)}), bf16[64,2,32,128]{3,2,1,0:T(8,128)(2,1)S(1)}, u32[]{:S(2)}, u32[]{:S(2)}) %all-to-all-start) | async-done | bytes 1048608 | tf_op jit(solution)/shard_map/all_to_all | solution.py:163
  92.9 0.5 fusion.27
  93.4 0.2 copy.70
  93.7 34.5 %all_to_all.10 = bf16[64,2,32,128]{3,2,1,0:T(8,128)(2,1)S(1)} all-to-all(bf16[64,2,32,128]{3,2,1,0:T(8,128)(2,1)S(1)} %bitcast.61), channel_id=1, replica_groups=mesh['slab'=4,'dev'=64] {'dev'}, dimensions={0} | all-to-all | bytes 2097152 | tf_op jit(solution)/shard_map/all_to_all | solution.py:171
  128.2 1.0 copy.76
  (31 shorter events, 0.3 us)
Async XLA Ops:
  0.0 22.7 %copy-start = (bf16[3,3,3,128,256]{4,3,2,1,0:T(8,128)(2,1)S(1)}, bf16[3,3,3,128,256]{4,3,2,1,0:T(8,128)(2,1)}, u32[]{:S(2)}) copy-start(bf16[3,3,3,128,256]{4,3,2,1,0:T(8,128)(2,1)} %param.19) | copy-start | bytes 5308420
  0.0 4.8 %copy-start.7 = (s32[48]{0:T(128)S(1)}, s32[48]{0:T(128)}, u32[]{:S(2)}) copy-start(s32[48]{0:T(128)} %param.13) | copy-start | bytes 580
  1.0 17.8 %copy-start.8 = (s32[48,1]{0,1:T(1,128)S(1)}, s32[48,1]{0,1:T(1,128)}, u32[]{:S(2)}) copy-start(s32[48,1]{0,1:T(1,128)} %param.14) | copy-start | bytes 580
  1.1 21.6 %copy-start.5 = (f32[128]{0:T(128)S(1)}, f32[128]{0:T(128)}, u32[]{:S(2)}) copy-start(f32[128]{0:T(128)} %param.18) | copy-start | bytes 1540
  1.1 21.5 %copy-start.6 = (f32[128]{0:T(128)S(1)}, f32[128]{0:T(128)}, u32[]{:S(2)}) copy-start(f32[128]{0:T(128)} %param.17) | copy-start | bytes 1540
  6.4 12.6 %collective-permute-start = (f32[1,66]{1,0:T(1,128)S(1)}, f32[1,66]{1,0:T(1,128)S(1)}, u32[]{:S(2)}, u32[]{:S(2)}) collective-permute-start(f32[1,66]{1,0:T(1,128)S(1)} %maximum_bitcast_fusion), channel_id=1, source_target_pairs={{0,1},{1,2},{2,3},{3,4},{4,5},{5,6},{6,7},{7,8},{8,9},{9,10},{10,1... | collective-permute-start | bytes 800 | tf_op jit(solution)/shard_map/ppermute | solution.py:45
  11.4 7.7 %collective-permute-start.1 = (f32[1,66]{1,0:T(1,128)S(1)}, f32[1,66]{1,0:T(1,128)S(1)}, u32[]{:S(2)}, u32[]{:S(2)}) collective-permute-start(f32[1,66]{1,0:T(1,128)S(1)} %maximum_bitcast_fusion), channel_id=1, source_target_pairs={{0,2},{1,3},{2,4},{3,5},{4,6},{5,7},{6,8},{7,9},{8,10},{9,11},{10,... | collective-permute-start | bytes 800 | tf_op jit(solution)/shard_map/ppermute | solution.py:45
  15.6 4.9 %collective-permute-start.2 = (f32[1,66]{1,0:T(1,128)S(1)}, f32[1,66]{1,0:T(1,128)S(1)}, u32[]{:S(2)}, u32[]{:S(2)}) collective-permute-start(f32[1,66]{1,0:T(1,128)S(1)} %maximum_bitcast_fusion.1), channel_id=1, source_target_pairs={{1,0},{2,1},{3,2},{4,3},{5,4},{6,5},{7,6},{8,7},{9,8},{10,9},{11,1... | collective-permute-start | bytes 800 | tf_op jit(solution)/shard_map/ppermute | solution.py:45
  17.5 4.5 %collective-permute-start.3 = (f32[1,66]{1,0:T(1,128)S(1)}, f32[1,66]{1,0:T(1,128)S(1)}, u32[]{:S(2)}, u32[]{:S(2)}) collective-permute-start(f32[1,66]{1,0:T(1,128)S(1)} %maximum_bitcast_fusion.1), channel_id=1, source_target_pairs={{2,0},{3,1},{4,2},{5,3},{6,4},{7,5},{8,6},{9,7},{10,8},{11,9},{12,... | collective-permute-start | bytes 800 | tf_op jit(solution)/shard_map/ppermute | solution.py:45
  22.7 24.0 %copy-start.2 = (f32[256]{0:T(256)S(1)}, f32[256]{0:T(256)}, u32[]{:S(2)}) copy-start(f32[256]{0:T(256)} %param.21) | copy-start | bytes 3076
  22.7 24.0 %copy-start.3 = (f32[256]{0:T(256)S(1)}, f32[256]{0:T(256)}, u32[]{:S(2)}) copy-start(f32[256]{0:T(256)} %param.20) | copy-start | bytes 3076
  28.4 13.3 %collective-permute-start.4 = (f32[1,66]{1,0:T(1,128)S(1)}, f32[1,66]{1,0:T(1,128)S(1)}, u32[]{:S(2)}, u32[]{:S(2)}) collective-permute-start(f32[1,66]{1,0:T(1,128)S(1)} %maximum_bitcast_fusion.2), channel_id=1, source_target_pairs={{0,1},{1,2},{2,3},{3,4},{4,5},{5,6},{6,7},{7,8},{8,9},{9,10},{10,1... | collective-permute-start | bytes 800 | tf_op jit(solution)/shard_map/ppermute | solution.py:45
  33.0 8.7 %collective-permute-start.5 = (f32[1,66]{1,0:T(1,128)S(1)}, f32[1,66]{1,0:T(1,128)S(1)}, u32[]{:S(2)}, u32[]{:S(2)}) collective-permute-start(f32[1,66]{1,0:T(1,128)S(1)} %maximum_bitcast_fusion.2), channel_id=1, source_target_pairs={{0,2},{1,3},{2,4},{3,5},{4,6},{5,7},{6,8},{7,9},{8,10},{9,11},{10,... | collective-permute-start | bytes 800 | tf_op jit(solution)/shard_map/ppermute | solution.py:45
  38.3 4.9 %collective-permute-start.6 = (f32[1,66]{1,0:T(1,128)S(1)}, f32[1,66]{1,0:T(1,128)S(1)}, u32[]{:S(2)}, u32[]{:S(2)}) collective-permute-start(f32[1,66]{1,0:T(1,128)S(1)} %maximum_bitcast_fusion.3), channel_id=1, source_target_pairs={{1,0},{2,1},{3,2},{4,3},{5,4},{6,5},{7,6},{8,7},{9,8},{10,9},{11,1... | collective-permute-start | bytes 800 | tf_op jit(solution)/shard_map/ppermute | solution.py:45
  40.2 5.8 %collective-permute-start.7 = (f32[1,66]{1,0:T(1,128)S(1)}, f32[1,66]{1,0:T(1,128)S(1)}, u32[]{:S(2)}, u32[]{:S(2)}) collective-permute-start(f32[1,66]{1,0:T(1,128)S(1)} %maximum_bitcast_fusion.3), channel_id=1, source_target_pairs={{2,0},{3,1},{4,2},{5,3},{6,4},{7,5},{8,6},{9,7},{10,8},{11,9},{12,... | collective-permute-start | bytes 800 | tf_op jit(solution)/shard_map/ppermute | solution.py:45
  47.3 0.8 copy-start.1
  47.3 0.8 copy-start.4
  49.1 15.3 %copy-start.9 = (s32[128,1]{0,1:T(1,128)S(1)}, s32[128,1]{0,1:T(1,128)}, u32[]{:S(2)}) copy-start(s32[128,1]{0,1:T(1,128)} %param.15) | copy-start | bytes 1540
  50.3 42.6 %all-to-all-start = ((bf16[64,2,32,128]{3,2,1,0:T(8,128)(2,1)}), bf16[64,2,32,128]{3,2,1,0:T(8,128)(2,1)S(1)}, u32[]{:S(2)}, u32[]{:S(2)}) async-start(bf16[64,2,32,128]{3,2,1,0:T(8,128)(2,1)} %bitcast.60), calls=%async_computation | async-start | bytes 2097152 | tf_op jit(solution)/shard_map/all_to_all | solution.py:163

commit v4 on v2

--- a/solution.py
+++ b/solution.py
@@ -148,31 +148,31 @@
     tiles = pixels.reshape(how_many, FR, HT, WT, 3)
     hidden, (sums, squares) = first_conv(tiles, conv_first)
     totals = clip_totals(tile_clip, jnp.concatenate([sums, squares, ones], axis=1))
+    slot_pixels, totals = lax.optimization_barrier((slot_pixels, totals))
     means_a, scales_a = finish_stats(totals, FR * HT * WT * (C1 // GROUPS))
-    slot_a = to_encoders(
-        route(jnp.concatenate([means_a, scales_a], axis=1), place, slots), group_width, capacity
-    )
     down, (sums, squares) = second_conv(hidden, means_a, scales_a, gain_first, bias_first, conv_down)
+    slot_tiles = slot_pixels.reshape(slots, FR, HT, WT, 3)
+    slot_hidden, _ = first_conv(slot_tiles, conv_first)
     totals = clip_totals(tile_clip, jnp.concatenate([sums, squares, ones], axis=1))
+    slot_hidden, totals = lax.optimization_barrier((slot_hidden, totals))
     means_b, scales_b = finish_stats(totals, LROWS * (C2 // GROUPS))
-    slot_b = to_encoders(
-        route(jnp.concatenate([means_b, scales_b, ones], axis=1), place, slots),
+    slot_stats = to_encoders(
+        route(jnp.concatenate([means_a, scales_a, means_b, scales_b, ones], axis=1), place, slots),
         group_width,
         capacity,
     )
 
-    slot_tiles = slot_pixels.reshape(slots, FR, HT, WT, 3)
-    slot_hidden, _ = first_conv(slot_tiles, conv_first)
+    g = GROUPS
     slot_down, _ = second_conv(
-        slot_hidden, slot_a[:, :GROUPS], slot_a[:, GROUPS:], gain_first, bias_first, conv_down
+        slot_hidden, slot_stats[:, :g], slot_stats[:, g : 2 * g], gain_first, bias_first, conv_down
     )
     active = normalize(
-        slot_down, slot_b[:, :GROUPS], slot_b[:, GROUPS : 2 * GROUPS], gain_second, bias_second
+        slot_down, slot_stats[:, 2 * g : 3 * g], slot_stats[:, 3 * g : 4 * g], gain_second, bias_second
     )
     flat = active.reshape(-1, C2)
     latent = jnp.dot(flat, project, preferred_element_type=jnp.float32) + project_bias
     latent = latent.astype(jnp.bfloat16).reshape(slots, LROWS * LAT)
-    live = slot_b[:, 2 * GROUPS :] > 0.5
+    live = slot_stats[:, 4 * g :] > 0.5
     latent = jnp.where(live, latent, jnp.zeros_like(latent))
 
     forward = route(latent, target, slots)

time: 189 us -> 151 us (0.80)
  matrix products: 44.3 us -> 28.7 us
  local copies, waits for them, and re-layouts: 28 us -> 17.8 us
  waiting for transfers between devices: 25.6 us -> 19.7 us
  starting transfers between devices: 51.5 us -> 45.8 us
    conv_general_dilated x4, matrix products: 37.1 us -> 22.3 us  [conv_local(): lax.conv_general_dilated(inputs, kernel, (1, stride, stride), ((2, 0), (1...]
    another operation x1 -> x0, local copies, waits for them, and re-layouts: 9.76 us -> none  [per_device(): slot_tiles = slot_pixels.reshape(slots, FR, HT, WT, 3)]
    all_to_all x3 -> x2, waiting for transfers between devices: 25.6 us -> 19.7 us  [to_encoders(): lax.all_to_all(values.reshape((group_width, capacity) + shape[1:]), 'dev'...]
    all_to_all x3 -> x2, starting transfers between devices: 27.5 us -> 22 us  [to_encoders(): lax.all_to_all(values.reshape((group_width, capacity) + shape[1:]), 'dev'...]
  transfers between devices with their start and end apart: 11 -> 10, of which waited for: 3 -> 2; matrix products, arithmetic and copies ran while one was open for 4% -> 5% of each run, Pallas kernels for 0% -> 0%
where the time goes in v4:
time: 151 us; the launch traced here: 150 us
  starting transfers between devices  45.8 us (30%)
  blocking collectives  33.3 us (22%)
  matrix products  28.7 us (19%)
  waiting for transfers between devices  19.7 us (13%)
  local copies, waits for them, and re-layouts  17.8 us (12%)
  other arithmetic  4.26 us (3%)
    all_to_all x1, blocking collectives, to_encoders(): lax.all_to_all(values.reshape((group_width, capacity) + shape[1:]), 'dev'...  33.3 us
    ppermute x8, starting transfers between devices, shifted(): return lax.ppermute(x, AXES, perm)  23.8 us
    conv_general_dilated x4, matrix products, conv_local(): lax.conv_general_dilated(inputs, kernel, (1, stride, stride), ((2, 0), (1...  22.3 us
    all_to_all x2, starting transfers between devices, to_encoders(): lax.all_to_all(values.reshape((group_width, capacity) + shape[1:]), 'dev'...  22 us
    all_to_all x2, waiting for transfers between devices, to_encoders(): lax.all_to_all(values.reshape((group_width, capacity) + shape[1:]), 'dev'...  19.7 us
    reshape x1, local copies, waits for them, and re-layouts, per_device(): flat = active.reshape(-1, C2)  4.01 us
    reshape x3, local copies, waits for them, and re-layouts, to_encoders(): values.reshape((group_width, capacity) + shape[1:])  3.15 us
  transfers between devices with their start and end apart: 10, of which 2 were waited for; matrix products, arithmetic and copies ran while one was open for 5% of the time, Pallas kernels for 0%

profile of v4, /device:TPU:1, one launch (start us, length us, event | category | flops | bytes accessed | tf_op | source)
XLA Modules:
  0.0 150.2 jit_solution(11370449192878178423)
XLA Ops:
  0.1 0.8 convert_element_type.65
  0.8 0.6 fusion.56
  1.4 0.9 copy.95
  2.3 0.1 reshape.81
  2.4 3.3 %convert_reduce_fusion = (f32[48,128]{1,0:T(8,128)S(1)}, f32[48,128]{1,0:T(8,128)S(1)}, bf16[48,2,8,8,128]{4,0,3,2,1:T(8,128)(2,1)}) fusion(bf16[48,2,8,8,3]{0,4,3,2,1:T(4,128)(2,1)S(1)} %reshape.81, bf16[3,3,3,3,128]{4,3,2,1,0:T(4,128)(2,1)} %param.16), kind=kOutput, calls=%fused_computation.6 | convolution fusion | flops 57446400 | bytes 1679616 | tf_op jit(solution)/shard_map/conv_general_dilated | solution.py:23
  5.7 0.1 copy.96
  5.8 0.1 copy.97
  6.1 0.2 fusion.24
  6.3 0.7 maximum_bitcast_fusion.1
  7.0 1.3 collective-permute-start.3
  8.3 5.1 %collective-permute-start.2 = (f32[1,66]{1,0:T(1,128)S(1)}, f32[1,66]{1,0:T(1,128)S(1)}, u32[]{:S(2)}, u32[]{:S(2)}) collective-permute-start(f32[1,66]{1,0:T(1,128)S(1)} %maximum_bitcast_fusion.1), channel_id=1, source_target_pairs={{1,0},{2,1},{3,2},{4,3},{5,4},{6,5},{7,6},{8,7},{9,8},{10,9},{11,1... | collective-permute-start | bytes 800 | tf_op jit(solution)/shard_map/ppermute | solution.py:45
  13.4 0.7 maximum_bitcast_fusion
  14.1 4.3 %collective-permute-start.1 = (f32[1,66]{1,0:T(1,128)S(1)}, f32[1,66]{1,0:T(1,128)S(1)}, u32[]{:S(2)}, u32[]{:S(2)}) collective-permute-start(f32[1,66]{1,0:T(1,128)S(1)} %maximum_bitcast_fusion), channel_id=1, source_target_pairs={{0,2},{1,3},{2,4},{3,5},{4,6},{5,7},{6,8},{7,9},{8,10},{9,11},{10,... | collective-permute-start | bytes 800 | tf_op jit(solution)/shard_map/ppermute | solution.py:45
  18.3 2.0 %collective-permute-start = (f32[1,66]{1,0:T(1,128)S(1)}, f32[1,66]{1,0:T(1,128)S(1)}, u32[]{:S(2)}, u32[]{:S(2)}) collective-permute-start(f32[1,66]{1,0:T(1,128)S(1)} %maximum_bitcast_fusion), channel_id=1, source_target_pairs={{0,1},{1,2},{2,3},{3,4},{4,5},{5,6},{6,7},{7,8},{8,9},{9,10},{10,1... | collective-permute-start | bytes 800 | tf_op jit(solution)/shard_map/ppermute | solution.py:45
  20.4 0.2 convert_reduce_fusion.3
  20.6 0.2 convolution_convert_fusion.3
  20.7 0.7 reshape.79
  21.4 14.2 %all-to-all-start = ((bf16[64,2,384]{2,1,0:T(2,128)(2,1)}), bf16[64,2,384]{2,1,0:T(2,128)(2,1)S(1)}, u32[]{:S(2)}, u32[]{:S(2)}) async-start(bf16[64,2,384]{2,1,0:T(2,128)(2,1)} %reshape.79), calls=%async_computation | async-start | bytes 196608 | tf_op jit(solution)/shard_map/all_to_all | solution.py:101
  35.6 0.2 convert_reduce_fusion.2
  35.8 0.1 copy.98
  35.9 0.1 slice_reduce_fusion.1
  36.1 0.3 convolution_add_fusion.2
  36.4 9.4 %all-to-all-done = bf16[64,2,384]{2,1,0:T(2,128)(2,1)S(1)} async-done(((bf16[64,2,384]{2,1,0:T(2,128)(2,1)}), bf16[64,2,384]{2,1,0:T(2,128)(2,1)S(1)}, u32[]{:S(2)}, u32[]{:S(2)}) %all-to-all-start) | async-done | bytes 98336 | tf_op jit(solution)/shard_map/all_to_all | solution.py:101
  45.9 0.1 copy.101
  46.0 0.1 copy.102
  46.1 4.4 %convert_reduce_fusion.1 = (f32[48,256]{1,0:T(8,128)S(1)}, f32[48,256]{1,0:T(8,128)S(1)}) fusion(bf16[3,3,3,128,256]{4,3,2,1,0:T(8,128)(2,1)S(1)} %copy-done, bf16[48,2,8,8,128]{4,0,3,2,1:T(8,128)(2,1)} %get-tuple-element.31, f32[128]{0:T(128)S(1)} %copy-done.10, f32[128]{0:T(128)S(1)} %copy-done.11, f32[48,128]{1,0:T(8,128)S(1)} %copy.102, ...), kind=kOutput, calls=%fused_computation.21 | convolution fusion | flops 1151705088 | bytes 3490816 | tf_op jit(solution)/shard_map/conv_general_dilated | solution.py:23
  50.5 0.1 copy.103
  50.6 0.1 copy.104
  50.7 0.1 bitcast_reduce_fusion
  50.8 0.2 fusion.25
  51.0 0.7 maximum_bitcast_fusion.3
  51.7 1.3 collective-permute-start.7
  53.0 2.3 %collective-permute-start.6 = (f32[1,66]{1,0:T(1,128)S(1)}, f32[1,66]{1,0:T(1,128)S(1)}, u32[]{:S(2)}, u32[]{:S(2)}) collective-permute-start(f32[1,66]{1,0:T(1,128)S(1)} %maximum_bitcast_fusion.3), channel_id=1, source_target_pairs={{1,0},{2,1},{3,2},{4,3},{5,4},{6,5},{7,6},{8,7},{9,8},{10,9},{11,1... | collective-permute-start | bytes 800 | tf_op jit(solution)/shard_map/ppermute | solution.py:45
  55.3 0.7 maximum_bitcast_fusion.2
  56.0 4.3 %collective-permute-start.5 = (f32[1,66]{1,0:T(1,128)S(1)}, f32[1,66]{1,0:T(1,128)S(1)}, u32[]{:S(2)}, u32[]{:S(2)}) collective-permute-start(f32[1,66]{1,0:T(1,128)S(1)} %maximum_bitcast_fusion.2), channel_id=1, source_target_pairs={{0,2},{1,3},{2,4},{3,5},{4,6},{5,7},{6,8},{7,9},{8,10},{9,11},{10,... | collective-permute-start | bytes 800 | tf_op jit(solution)/shard_map/ppermute | solution.py:45
  60.2 3.3 %collective-permute-start.4 = (f32[1,66]{1,0:T(1,128)S(1)}, f32[1,66]{1,0:T(1,128)S(1)}, u32[]{:S(2)}, u32[]{:S(2)}) collective-permute-start(f32[1,66]{1,0:T(1,128)S(1)} %maximum_bitcast_fusion.2), channel_id=1, source_target_pairs={{0,1},{1,2},{2,3},{3,4},{4,5},{5,6},{6,7},{7,8},{8,9},{9,10},{10,1... | collective-permute-start | bytes 800 | tf_op jit(solution)/shard_map/ppermute | solution.py:45
  63.5 0.1 copy.100
  63.7 3.8 %convolution_convert_fusion.1 = bf16[128,2,8,8,128]{4,0,3,2,1:T(8,128)(2,1)} fusion(bf16[128,2,8,8,3]{0,4,3,2,1:T(4,128)(2,1)S(1)} %reshape.82, bf16[3,3,3,3,128]{4,3,2,1,0:T(4,128)(2,1)S(1)} %copy-done.3), kind=kOutput, calls=%fused_computation.19 | convolution fusion | flops 144834560 | bytes 4313344 | tf_op jit(solution)/shard_map/conv_general_dilated | solution.py:23
  67.5 0.1 copy.105
  67.7 0.1 slice_reduce_fusion
  67.8 0.3 convolution_add_fusion.1
  68.2 0.2 fusion.21
  68.4 0.7 reshape.83
  69.2 7.8 %all-to-all-start.1 = ((f32[64,2,129]{2,1,0:T(2,128)}), f32[64,2,129]{2,1,0:T(2,128)S(1)}, u32[]{:S(2)}, u32[]{:S(2)}) async-start(f32[64,2,129]{2,1,0:T(2,128)} %reshape.83), calls=%async_computation.1 | async-start | bytes 262144 | tf_op jit(solution)/shard_map/all_to_all | solution.py:101
  77.0 10.3 %all-to-all-done.1 = f32[64,2,129]{2,1,0:T(2,128)S(1)} async-done(((f32[64,2,129]{2,1,0:T(2,128)}), f32[64,2,129]{2,1,0:T(2,128)S(1)}, u32[]{:S(2)}, u32[]{:S(2)}) %all-to-all-start.1) | async-done | bytes 66080 | tf_op jit(solution)/shard_map/all_to_all | solution.py:101
  87.3 0.1 reshape.84
  87.4 0.1 fusion.23
  87.5 0.1 fusion.55
  87.7 0.1 copy.114
  87.8 0.1 copy.112
  87.9 0.1 copy.110
  88.0 0.1 copy.111
  88.1 0.1 copy.109
  88.2 0.1 copy.113
  88.3 0.1 copy.115
  88.5 10.8 %multiply_convert_fusion.1 = bf16[128,2,4,4,256]{4,0,3,2,1:T(8,128)(2,1)S(1)} fusion(f32[256]{0:T(256)S(1)} %copy-done.5, f32[256]{0:T(256)S(1)} %copy-done.6, f32[128,256]{1,0:T(8,128)S(1)} %copy.115, f32[128,256]{1,0:T(8,128)S(1)} %copy.113, bf16[3,3,3,128,256]{4,3,2,1,0:T(8,128)(2,1)S(1)} %copy-done, ...), kind=kOutput, calls=%fused_computation.7 | convolution fusion | flops 3077570560 | bytes 8457216 | tf_op jit(solution)/shard_map/conv_general_dilated | solution.py:23
  99.2 3.0 %copy.116 = bf16[128,2,4,4,256]{4,3,2,1,0:T(4,128)(2,1)} copy(bf16[128,2,4,4,256]{4,0,3,2,1:T(8,128)(2,1)S(1)} %multiply_convert_fusion.1) | data formatting | bytes 4194304 | tf_op jit(solution)/shard_map/convert_element_type | solution.py:81
  102.2 4.0 %reshape.85 = bf16[4096,256]{1,0:T(8,128)(2,1)} reshape(bf16[128,2,4,4,256]{4,3,2,1,0:T(4,128)(2,1)} %copy.116) | data formatting | bytes 4194304 | tf_op jit(solution)/shard_map/reshape | solution.py:172
  106.2 2.3 %fusion = bf16[4096,128]{1,0:T(8,128)(2,1)S(1)} fusion(bf16[4096,256]{1,0:T(8,128)(2,1)} %reshape.85, bf16[256,128]{1,0:T(8,128)(2,1)S(1)} %copy-done.2, f32[128]{0:T(128)S(1)} %copy-done.4), kind=kOutput, calls=%fused_computation.2 | convolution fusion | flops 269484032 | bytes 3211776 | tf_op jit(solution)/shard_map/dot_general | solution.py:173
  108.5 1.3 reshape.86
  109.8 2.7 %convolution_convert_fusion = bf16[128,4096]{1,0:T(8,128)(2,1)} fusion(bf16[128,4096]{1,0:T(8,128)(2,1)} %reshape.86, pred[128]{0:T(512)(128)(4,1)S(1)} %fusion.23, s32[128]{0:T(128)S(1)} %multiply_add_fusion.1), kind=kOutput, calls=%fused_computation.3 | convolution fusion | flops 135282688 | bytes 2097792 | tf_op jit(solution)/shard_map/dot_general | solution.py:95
  112.5 1.7 %reshape.87 = bf16[64,2,4096]{2,1,0:T(2,128)(2,1)S(1)} reshape(bf16[128,4096]{1,0:T(8,128)(2,1)} %convolution_convert_fusion) | data formatting | bytes 2097152 | tf_op jit(solution)/shard_map/reshape | solution.py:102
  114.3 33.3 %all_to_all.15 = bf16[64,2,4096]{2,1,0:T(2,128)(2,1)} all-to-all(bf16[64,2,4096]{2,1,0:T(2,128)(2,1)S(1)} %reshape.87), channel_id=1, replica_groups=mesh['slab'=4,'dev'=64] {'dev'}, dimensions={0} | all-to-all | bytes 2097152 | tf_op jit(solution)/shard_map/all_to_all | solution.py:101
  147.6 2.6 %reshape_reshape.3 = bf16[4096,128]{1,0:T(8,128)(2,1)} reshape(bf16[64,2,4096]{2,1,0:T(2,128)(2,1)} %all_to_all.15) | data formatting | bytes 2097152 | tf_op jit(solution)/shard_map/reshape;reshape | solution.py:180
  (57 shorter events, 0.6 us)
Async XLA Ops:
  0.0 46.0 %copy-start = (bf16[3,3,3,128,256]{4,3,2,1,0:T(8,128)(2,1)S(1)}, bf16[3,3,3,128,256]{4,3,2,1,0:T(8,128)(2,1)}, u32[]{:S(2)}) copy-start(bf16[3,3,3,128,256]{4,3,2,1,0:T(8,128)(2,1)} %param.19) | copy-start | bytes 5308420
  0.0 6.1 %copy-start.8 = (s32[48]{0:T(128)S(1)}, s32[48]{0:T(128)}, u32[]{:S(2)}) copy-start(s32[48]{0:T(128)} %param.13) | copy-start | bytes 580
  0.0 20.6 %copy-start.1 = (bf16[48,384]{1,0:T(8,128)(2,1)S(1)}, bf16[48,384]{1,0:T(8,128)(2,1)}, u32[]{:S(2)}) copy-start(bf16[48,384]{1,0:T(8,128)(2,1)} %param.12) | copy-start | bytes 110596
  0.0 20.4 %copy-start.7 = (s32[48,1]{0,1:T(1,128)S(1)}, s32[48,1]{0,1:T(1,128)}, u32[]{:S(2)}) copy-start(s32[48,1]{0,1:T(1,128)} %param.14) | copy-start | bytes 580
  0.0 35.6 %copy-start.9 = (s32[128,1]{0,1:T(1,128)S(1)}, s32[128,1]{0,1:T(1,128)}, u32[]{:S(2)}) copy-start(s32[128,1]{0,1:T(1,128)} %param.15) | copy-start | bytes 1540
  0.0 46.0 %copy-start.10 = (f32[128]{0:T(128)S(1)}, f32[128]{0:T(128)}, u32[]{:S(2)}) copy-start(f32[128]{0:T(128)} %param.18) | copy-start | bytes 1540
  0.0 46.0 %copy-start.11 = (f32[128]{0:T(128)S(1)}, f32[128]{0:T(128)}, u32[]{:S(2)}) copy-start(f32[128]{0:T(128)} %param.17) | copy-start | bytes 1540
  7.0 28.9 %collective-permute-start.3 = (f32[1,66]{1,0:T(1,128)S(1)}, f32[1,66]{1,0:T(1,128)S(1)}, u32[]{:S(2)}, u32[]{:S(2)}) collective-permute-start(f32[1,66]{1,0:T(1,128)S(1)} %maximum_bitcast_fusion.1), channel_id=1, source_target_pairs={{2,0},{3,1},{4,2},{5,3},{6,4},{7,5},{8,6},{9,7},{10,8},{11,9},{12,... | collective-permute-start | bytes 800 | tf_op jit(solution)/shard_map/ppermute | solution.py:45
  8.3 27.6 %collective-permute-start.2 = (f32[1,66]{1,0:T(1,128)S(1)}, f32[1,66]{1,0:T(1,128)S(1)}, u32[]{:S(2)}, u32[]{:S(2)}) collective-permute-start(f32[1,66]{1,0:T(1,128)S(1)} %maximum_bitcast_fusion.1), channel_id=1, source_target_pairs={{1,0},{2,1},{3,2},{4,3},{5,4},{6,5},{7,6},{8,7},{9,8},{10,9},{11,1... | collective-permute-start | bytes 800 | tf_op jit(solution)/shard_map/ppermute | solution.py:45
  14.1 21.8 %collective-permute-start.1 = (f32[1,66]{1,0:T(1,128)S(1)}, f32[1,66]{1,0:T(1,128)S(1)}, u32[]{:S(2)}, u32[]{:S(2)}) collective-permute-start(f32[1,66]{1,0:T(1,128)S(1)} %maximum_bitcast_fusion), channel_id=1, source_target_pairs={{0,2},{1,3},{2,4},{3,5},{4,6},{5,7},{6,8},{7,9},{8,10},{9,11},{10,... | collective-permute-start | bytes 800 | tf_op jit(solution)/shard_map/ppermute | solution.py:45
  18.3 17.6 %collective-permute-start = (f32[1,66]{1,0:T(1,128)S(1)}, f32[1,66]{1,0:T(1,128)S(1)}, u32[]{:S(2)}, u32[]{:S(2)}) collective-permute-start(f32[1,66]{1,0:T(1,128)S(1)} %maximum_bitcast_fusion), channel_id=1, source_target_pairs={{0,1},{1,2},{2,3},{3,4},{4,5},{5,6},{6,7},{7,8},{8,9},{9,10},{10,1... | collective-permute-start | bytes 800 | tf_op jit(solution)/shard_map/ppermute | solution.py:45
  21.4 24.3 %all-to-all-start = ((bf16[64,2,384]{2,1,0:T(2,128)(2,1)}), bf16[64,2,384]{2,1,0:T(2,128)(2,1)S(1)}, u32[]{:S(2)}, u32[]{:S(2)}) async-start(bf16[64,2,384]{2,1,0:T(2,128)(2,1)} %reshape.79), calls=%async_computation | async-start | bytes 196608 | tf_op jit(solution)/shard_map/all_to_all | solution.py:101
  46.1 17.6 %copy-start.3 = (bf16[3,3,3,3,128]{4,3,2,1,0:T(4,128)(2,1)S(1)}, bf16[3,3,3,3,128]{4,3,2,1,0:T(4,128)(2,1)}, u32[]{:S(2)}) copy-start(bf16[3,3,3,3,128]{4,3,2,1,0:T(4,128)(2,1)} %param.16) | copy-start | bytes 62212
  51.7 15.9 %collective-permute-start.7 = (f32[1,66]{1,0:T(1,128)S(1)}, f32[1,66]{1,0:T(1,128)S(1)}, u32[]{:S(2)}, u32[]{:S(2)}) collective-permute-start(f32[1,66]{1,0:T(1,128)S(1)} %maximum_bitcast_fusion.3), channel_id=1, source_target_pairs={{2,0},{3,1},{4,2},{5,3},{6,4},{7,5},{8,6},{9,7},{10,8},{11,9},{12,... | collective-permute-start | bytes 800 | tf_op jit(solution)/shard_map/ppermute | solution.py:45
  53.0 14.6 %collective-permute-start.6 = (f32[1,66]{1,0:T(1,128)S(1)}, f32[1,66]{1,0:T(1,128)S(1)}, u32[]{:S(2)}, u32[]{:S(2)}) collective-permute-start(f32[1,66]{1,0:T(1,128)S(1)} %maximum_bitcast_fusion.3), channel_id=1, source_target_pairs={{1,0},{2,1},{3,2},{4,3},{5,4},{6,5},{7,6},{8,7},{9,8},{10,9},{11,1... | collective-permute-start | bytes 800 | tf_op jit(solution)/shard_map/ppermute | solution.py:45
  56.0 11.7 %collective-permute-start.5 = (f32[1,66]{1,0:T(1,128)S(1)}, f32[1,66]{1,0:T(1,128)S(1)}, u32[]{:S(2)}, u32[]{:S(2)}) collective-permute-start(f32[1,66]{1,0:T(1,128)S(1)} %maximum_bitcast_fusion.2), channel_id=1, source_target_pairs={{0,2},{1,3},{2,4},{3,5},{4,6},{5,7},{6,8},{7,9},{8,10},{9,11},{10,... | collective-permute-start | bytes 800 | tf_op jit(solution)/shard_map/ppermute | solution.py:45
  60.2 7.4 %collective-permute-start.4 = (f32[1,66]{1,0:T(1,128)S(1)}, f32[1,66]{1,0:T(1,128)S(1)}, u32[]{:S(2)}, u32[]{:S(2)}) collective-permute-start(f32[1,66]{1,0:T(1,128)S(1)} %maximum_bitcast_fusion.2), channel_id=1, source_target_pairs={{0,1},{1,2},{2,3},{3,4},{4,5},{5,6},{6,7},{7,8},{8,9},{9,10},{10,1... | collective-permute-start | bytes 800 | tf_op jit(solution)/shard_map/ppermute | solution.py:45
  63.7 24.7 %copy-start.5 = (f32[256]{0:T(256)S(1)}, f32[256]{0:T(256)}, u32[]{:S(2)}) copy-start(f32[256]{0:T(256)} %param.21) | copy-start | bytes 3076
  63.7 24.7 %copy-start.6 = (f32[256]{0:T(256)S(1)}, f32[256]{0:T(256)}, u32[]{:S(2)}) copy-start(f32[256]{0:T(256)} %param.20) | copy-start | bytes 3076
  69.2 18.2 %all-to-all-start.1 = ((f32[64,2,129]{2,1,0:T(2,128)}), f32[64,2,129]{2,1,0:T(2,128)S(1)}, u32[]{:S(2)}, u32[]{:S(2)}) async-start(f32[64,2,129]{2,1,0:T(2,128)} %reshape.83), calls=%async_computation.1 | async-start | bytes 262144 | tf_op jit(solution)/shard_map/all_to_all | solution.py:101
  102.2 4.0 %copy-start.2 = (bf16[256,128]{1,0:T(8,128)(2,1)S(1)}, bf16[256,128]{1,0:T(8,128)(2,1)}, u32[]{:S(2)}) copy-start(bf16[256,128]{1,0:T(8,128)(2,1)} %param.22) | copy-start | bytes 196612
  102.2 4.0 %copy-start.4 = (f32[128]{0:T(128)S(1)}, f32[128]{0:T(128)}, u32[]{:S(2)}) copy-start(f32[128]{0:T(128)} %param.23) | copy-start | bytes 1540

commit v5 on v3

--- a/solution.py
+++ b/solution.py
@@ -159,6 +159,7 @@
     tiles = pixels.reshape(how_many, FR, HT, WT, 3)
     latents = encode(tiles, tile_clip, weights)
 
+    latents, target = lax.optimization_barrier((latents, target))
     outgoing = route(latents.reshape(how_many, LROWS * LAT), place, slots)
     arrived = lax.all_to_all(
         outgoing.reshape(group_width, capacity, LROWS, LAT),

time: 130 us -> 128 us (0.985)
  blocking collectives: 34.5 us -> 76.9 us
  waiting for transfers between devices: 35.6 us -> 7.1 us
  starting transfers between devices: 38.2 us -> 24.1 us
    all_to_all x0 -> x1, blocking collectives: none -> 42.4 us  [per_device(): lax.all_to_all(outgoing.reshape(group_width, capacity, LROWS, LAT), 'dev'...]
    all_to_all x1 -> x0, waiting for transfers between devices: 28.3 us -> none  [per_device(): lax.all_to_all(outgoing.reshape(group_width, capacity, LROWS, LAT), 'dev'...]
    all_to_all x1 -> x0, starting transfers between devices: 14.1 us -> none  [per_device(): lax.all_to_all(outgoing.reshape(group_width, capacity, LROWS, LAT), 'dev'...]
  transfers between devices with their start and end apart: 9 -> 8, of which waited for: 5 -> 4; matrix products, arithmetic and copies ran while one was open for 1% -> 1% of each run, Pallas kernels for 0% -> 0%
where the time goes in v5:
time: 128 us
  blocking collectives  76.9 us (60%)
  starting transfers between devices  24.1 us (19%)
  matrix products  10 us (8%)
  waiting for transfers between devices  7.1 us (6%)
  local copies, waits for them, and re-layouts  5.24 us (4%)
  other arithmetic  3.93 us (3%)
    all_to_all x1, blocking collectives, per_device(): lax.all_to_all(outgoing.reshape(group_width, capacity, LROWS, LAT), 'dev'...  42.4 us
    all_to_all x1, blocking collectives, per_device(): lax.all_to_all(forward.reshape(group_width, capacity, LROWS, LAT), 'dev',...  34.5 us
    ppermute x8, starting transfers between devices, shifted(): return lax.ppermute(x, AXES, perm)  24.1 us
    conv_general_dilated x2, matrix products, conv_local(): lax.conv_general_dilated(inputs, kernel, (1, stride, stride), ((2, 0), (1...  7.72 us
    ppermute x8, waiting for transfers between devices, shifted(): return lax.ppermute(x, AXES, perm)  7.1 us
    unnamed x24, local copies, waits for them, and re-layouts  2.78 us
  transfers between devices with their start and end apart: 8, of which 4 were waited for; matrix products, arithmetic and copies ran while one was open for 1% of the time, Pallas kernels for 0%

profile of v5, /device:TPU:1, one launch (start us, length us, event | category | flops | bytes accessed | tf_op | source)
XLA Modules:
  0.0 127.8 jit_solution(6266674086692658858)
XLA Ops:
  0.0 1.0 copy.52
  1.0 0.0 copy-start.5
  1.0 0.0 copy-start.9
  1.1 0.1 reshape.60
  1.1 0.0 copy-start.6
  1.1 0.0 copy-start.7
  1.2 3.3 %convert_reduce_fusion = (f32[48,128]{1,0:T(8,128)S(1)}, f32[48,128]{1,0:T(8,128)S(1)}, bf16[48,2,8,8,128]{4,0,3,2,1:T(8,128)(2,1)}) fusion(bf16[48,2,8,8,3]{0,4,3,2,1:T(4,128)(2,1)S(1)} %reshape.60, bf16[3,3,3,3,128]{4,3,2,1,0:T(4,128)(2,1)} %param.16), kind=kOutput, calls=%fused_computation.4 | convolution fusion | flops 57446400 | bytes 1679616 | tf_op jit(solution)/shard_map/conv_general_dilated | solution.py:23
  4.5 0.1 copy.53
  4.6 0.1 copy.54
  4.8 0.1 pad.21.clone
  4.9 0.2 fusion.33
  5.1 0.6 fusion.73
  5.7 0.7 maximum_bitcast_fusion
  6.4 4.9 %collective-permute-start = (f32[1,66]{1,0:T(1,128)S(1)}, f32[1,66]{1,0:T(1,128)S(1)}, u32[]{:S(2)}, u32[]{:S(2)}) collective-permute-start(f32[1,66]{1,0:T(1,128)S(1)} %maximum_bitcast_fusion), channel_id=1, source_target_pairs={{0,1},{1,2},{2,3},{3,4},{4,5},{5,6},{6,7},{7,8},{8,9},{9,10},{10,1... | collective-permute-start | bytes 800 | tf_op jit(solution)/shard_map/ppermute | solution.py:45
  11.3 3.5 %collective-permute-start.1 = (f32[1,66]{1,0:T(1,128)S(1)}, f32[1,66]{1,0:T(1,128)S(1)}, u32[]{:S(2)}, u32[]{:S(2)}) collective-permute-start(f32[1,66]{1,0:T(1,128)S(1)} %maximum_bitcast_fusion), channel_id=1, source_target_pairs={{0,2},{1,3},{2,4},{3,5},{4,6},{5,7},{6,8},{7,9},{8,10},{9,11},{10,... | collective-permute-start | bytes 800 | tf_op jit(solution)/shard_map/ppermute | solution.py:45
  14.9 0.7 maximum_bitcast_fusion.1
  15.6 1.9 %collective-permute-start.2 = (f32[1,66]{1,0:T(1,128)S(1)}, f32[1,66]{1,0:T(1,128)S(1)}, u32[]{:S(2)}, u32[]{:S(2)}) collective-permute-start(f32[1,66]{1,0:T(1,128)S(1)} %maximum_bitcast_fusion.1), channel_id=1, source_target_pairs={{1,0},{2,1},{3,2},{4,3},{5,4},{6,5},{7,6},{8,7},{9,8},{10,9},{11,1... | collective-permute-start | bytes 800 | tf_op jit(solution)/shard_map/ppermute | solution.py:45
  17.5 1.3 %collective-permute-start.3 = (f32[1,66]{1,0:T(1,128)S(1)}, f32[1,66]{1,0:T(1,128)S(1)}, u32[]{:S(2)}, u32[]{:S(2)}) collective-permute-start(f32[1,66]{1,0:T(1,128)S(1)} %maximum_bitcast_fusion.1), channel_id=1, source_target_pairs={{2,0},{3,1},{4,2},{5,3},{6,4},{7,5},{8,6},{9,7},{10,8},{11,9},{12,... | collective-permute-start | bytes 800 | tf_op jit(solution)/shard_map/ppermute | solution.py:45
  18.8 0.2 convert_reduce_fusion.2
  19.0 0.2 convert_reduce_fusion.3
  19.2 0.1 copy.55
  19.3 0.0 collective-permute-done
  19.3 0.0 collective-permute-done.1
  19.3 1.2 collective-permute-done.2
  20.5 1.5 %collective-permute-done.3 = f32[1,66]{1,0:T(1,128)S(1)} collective-permute-done((f32[1,66]{1,0:T(1,128)S(1)}, f32[1,66]{1,0:T(1,128)S(1)}, u32[]{:S(2)}, u32[]{:S(2)}) %collective-permute-start.3) | collective-permute-done | bytes 296 | tf_op jit(solution)/shard_map/ppermute | solution.py:45
  22.0 0.1 slice_reduce_fusion.1
  22.1 0.3 convolution_add_fusion.2
  22.5 0.1 copy.57
  22.6 0.1 copy.58
  22.6 0.0 copy-done.6
  22.7 0.0 copy-start.2
  22.7 0.0 copy-start.3
  22.7 4.4 %convert_reduce_fusion.1 = (f32[48,256]{1,0:T(8,128)S(1)}, f32[48,256]{1,0:T(8,128)S(1)}, bf16[48,2,4,4,256]{4,0,3,2,1:T(8,128)(2,1)S(1)}) fusion(bf16[3,3,3,128,256]{4,3,2,1,0:T(8,128)(2,1)S(1)} %copy-done, bf16[48,2,8,8,128]{4,0,3,2,1:T(8,128)(2,1)} %get-tuple-element.23, f32[128]{0:T(128)S(1)} %copy-done.6, f32[128]{0:T(128)S(1)} %copy-done.7, ...), kind=kOutput, calls=%fused_computation.19 | convolution fusion | flops 1151705088 | bytes 4277248 | tf_op jit(solution)/shard_map/conv_general_dilated | solution.py:23
  27.1 0.1 copy.59
  27.2 0.1 copy.60
  27.3 0.1 bitcast_reduce_fusion
  27.4 0.2 fusion.38
  27.6 0.7 maximum_bitcast_fusion.2
  28.4 4.6 %collective-permute-start.4 = (f32[1,66]{1,0:T(1,128)S(1)}, f32[1,66]{1,0:T(1,128)S(1)}, u32[]{:S(2)}, u32[]{:S(2)}) collective-permute-start(f32[1,66]{1,0:T(1,128)S(1)} %maximum_bitcast_fusion.2), channel_id=1, source_target_pairs={{0,1},{1,2},{2,3},{3,4},{4,5},{5,6},{6,7},{7,8},{8,9},{9,10},{10,1... | collective-permute-start | bytes 800 | tf_op jit(solution)/shard_map/ppermute | solution.py:45
  33.0 4.7 %collective-permute-start.5 = (f32[1,66]{1,0:T(1,128)S(1)}, f32[1,66]{1,0:T(1,128)S(1)}, u32[]{:S(2)}, u32[]{:S(2)}) collective-permute-start(f32[1,66]{1,0:T(1,128)S(1)} %maximum_bitcast_fusion.2), channel_id=1, source_target_pairs={{0,2},{1,3},{2,4},{3,5},{4,6},{5,7},{6,8},{7,9},{8,10},{9,11},{10,... | collective-permute-start | bytes 800 | tf_op jit(solution)/shard_map/ppermute | solution.py:45
  37.6 0.7 maximum_bitcast_fusion.3
  38.3 1.9 %collective-permute-start.6 = (f32[1,66]{1,0:T(1,128)S(1)}, f32[1,66]{1,0:T(1,128)S(1)}, u32[]{:S(2)}, u32[]{:S(2)}) collective-permute-start(f32[1,66]{1,0:T(1,128)S(1)} %maximum_bitcast_fusion.3), channel_id=1, source_target_pairs={{1,0},{2,1},{3,2},{4,3},{5,4},{6,5},{7,6},{8,7},{9,8},{10,9},{11,1... | collective-permute-start | bytes 800 | tf_op jit(solution)/shard_map/ppermute | solution.py:45
  40.2 1.3 %collective-permute-start.7 = (f32[1,66]{1,0:T(1,128)S(1)}, f32[1,66]{1,0:T(1,128)S(1)}, u32[]{:S(2)}, u32[]{:S(2)}) collective-permute-start(f32[1,66]{1,0:T(1,128)S(1)} %maximum_bitcast_fusion.3), channel_id=1, source_target_pairs={{2,0},{3,1},{4,2},{5,3},{6,4},{7,5},{8,6},{9,7},{10,8},{11,9},{12,... | collective-permute-start | bytes 800 | tf_op jit(solution)/shard_map/ppermute | solution.py:45
  41.5 0.1 copy.61
  41.6 1.5 %collective-permute-done.6 = f32[1,66]{1,0:T(1,128)S(1)} collective-permute-done((f32[1,66]{1,0:T(1,128)S(1)}, f32[1,66]{1,0:T(1,128)S(1)}, u32[]{:S(2)}, u32[]{:S(2)}) %collective-permute-start.6) | collective-permute-done | bytes 296 | tf_op jit(solution)/shard_map/ppermute | solution.py:45
  43.2 2.8 %collective-permute-done.7 = f32[1,66]{1,0:T(1,128)S(1)} collective-permute-done((f32[1,66]{1,0:T(1,128)S(1)}, f32[1,66]{1,0:T(1,128)S(1)}, u32[]{:S(2)}, u32[]{:S(2)}) %collective-permute-start.7) | collective-permute-done | bytes 296 | tf_op jit(solution)/shard_map/ppermute | solution.py:45
  46.0 0.1 slice_reduce_fusion
  46.2 0.3 convolution_add_fusion.1
  46.5 0.1 copy.63
  46.6 0.1 copy.64
  46.7 0.6 fusion.20
  47.3 0.0 copy-start.1
  47.3 0.0 copy-start.4
  47.3 0.4 copy.65
  47.7 0.2 reshape.61
  47.9 0.2 copy-done.1
  48.1 0.4 fusion.10
  48.5 0.4 fusion.26
  48.9 0.2 copy.69
  49.2 42.4 %all_to_all.10 = bf16[64,2,32,128]{3,2,1,0:T(8,128)(2,1)S(1)} all-to-all(bf16[64,2,32,128]{3,2,1,0:T(8,128)(2,1)S(1)} %bitcast.64), channel_id=1, replica_groups=mesh['slab'=4,'dev'=64] {'dev'}, dimensions={0} | all-to-all | bytes 2097152 | tf_op jit(solution)/shard_map/all_to_all | solution.py:164
  91.6 0.5 fusion.27
  92.1 0.2 copy.71
  92.3 34.5 %all_to_all.11 = bf16[64,2,32,128]{3,2,1,0:T(8,128)(2,1)S(1)} all-to-all(bf16[64,2,32,128]{3,2,1,0:T(8,128)(2,1)S(1)} %bitcast.65), channel_id=1, replica_groups=mesh['slab'=4,'dev'=64] {'dev'}, dimensions={0} | all-to-all | bytes 2097152 | tf_op jit(solution)/shard_map/all_to_all | solution.py:172
  126.9 1.0 copy.81
  (29 shorter events, 0.3 us)
Async XLA Ops:
  0.0 22.6 %copy-start = (bf16[3,3,3,128,256]{4,3,2,1,0:T(8,128)(2,1)S(1)}, bf16[3,3,3,128,256]{4,3,2,1,0:T(8,128)(2,1)}, u32[]{:S(2)}) copy-start(bf16[3,3,3,128,256]{4,3,2,1,0:T(8,128)(2,1)} %param.19) | copy-start | bytes 5308420
  0.0 4.8 %copy-start.8 = (s32[48]{0:T(128)S(1)}, s32[48]{0:T(128)}, u32[]{:S(2)}) copy-start(s32[48]{0:T(128)} %param.13) | copy-start | bytes 580
  1.0 17.8 %copy-start.5 = (s32[128,1]{0,1:T(1,128)S(1)}, s32[128,1]{0,1:T(1,128)}, u32[]{:S(2)}) copy-start(s32[128,1]{0,1:T(1,128)} %param.15) | copy-start | bytes 1540
  1.0 17.9 %copy-start.9 = (s32[48,1]{0,1:T(1,128)S(1)}, s32[48,1]{0,1:T(1,128)}, u32[]{:S(2)}) copy-start(s32[48,1]{0,1:T(1,128)} %param.14) | copy-start | bytes 580
  1.1 21.5 %copy-start.6 = (f32[128]{0:T(128)S(1)}, f32[128]{0:T(128)}, u32[]{:S(2)}) copy-start(f32[128]{0:T(128)} %param.18) | copy-start | bytes 1540
  1.1 21.5 %copy-start.7 = (f32[128]{0:T(128)S(1)}, f32[128]{0:T(128)}, u32[]{:S(2)}) copy-start(f32[128]{0:T(128)} %param.17) | copy-start | bytes 1540
  6.4 12.8 %collective-permute-start = (f32[1,66]{1,0:T(1,128)S(1)}, f32[1,66]{1,0:T(1,128)S(1)}, u32[]{:S(2)}, u32[]{:S(2)}) collective-permute-start(f32[1,66]{1,0:T(1,128)S(1)} %maximum_bitcast_fusion), channel_id=1, source_target_pairs={{0,1},{1,2},{2,3},{3,4},{4,5},{5,6},{6,7},{7,8},{8,9},{9,10},{10,1... | collective-permute-start | bytes 800 | tf_op jit(solution)/shard_map/ppermute | solution.py:45
  11.3 7.9 %collective-permute-start.1 = (f32[1,66]{1,0:T(1,128)S(1)}, f32[1,66]{1,0:T(1,128)S(1)}, u32[]{:S(2)}, u32[]{:S(2)}) collective-permute-start(f32[1,66]{1,0:T(1,128)S(1)} %maximum_bitcast_fusion), channel_id=1, source_target_pairs={{0,2},{1,3},{2,4},{3,5},{4,6},{5,7},{6,8},{7,9},{8,10},{9,11},{10,... | collective-permute-start | bytes 800 | tf_op jit(solution)/shard_map/ppermute | solution.py:45
  15.6 4.9 %collective-permute-start.2 = (f32[1,66]{1,0:T(1,128)S(1)}, f32[1,66]{1,0:T(1,128)S(1)}, u32[]{:S(2)}, u32[]{:S(2)}) collective-permute-start(f32[1,66]{1,0:T(1,128)S(1)} %maximum_bitcast_fusion.1), channel_id=1, source_target_pairs={{1,0},{2,1},{3,2},{4,3},{5,4},{6,5},{7,6},{8,7},{9,8},{10,9},{11,1... | collective-permute-start | bytes 800 | tf_op jit(solution)/shard_map/ppermute | solution.py:45
  17.5 4.5 %collective-permute-start.3 = (f32[1,66]{1,0:T(1,128)S(1)}, f32[1,66]{1,0:T(1,128)S(1)}, u32[]{:S(2)}, u32[]{:S(2)}) collective-permute-start(f32[1,66]{1,0:T(1,128)S(1)} %maximum_bitcast_fusion.1), channel_id=1, source_target_pairs={{2,0},{3,1},{4,2},{5,3},{6,4},{7,5},{8,6},{9,7},{10,8},{11,9},{12,... | collective-permute-start | bytes 800 | tf_op jit(solution)/shard_map/ppermute | solution.py:45
  22.7 24.0 %copy-start.2 = (f32[256]{0:T(256)S(1)}, f32[256]{0:T(256)}, u32[]{:S(2)}) copy-start(f32[256]{0:T(256)} %param.21) | copy-start | bytes 3076
  22.7 24.0 %copy-start.3 = (f32[256]{0:T(256)S(1)}, f32[256]{0:T(256)}, u32[]{:S(2)}) copy-start(f32[256]{0:T(256)} %param.20) | copy-start | bytes 3076
  28.4 13.3 %collective-permute-start.4 = (f32[1,66]{1,0:T(1,128)S(1)}, f32[1,66]{1,0:T(1,128)S(1)}, u32[]{:S(2)}, u32[]{:S(2)}) collective-permute-start(f32[1,66]{1,0:T(1,128)S(1)} %maximum_bitcast_fusion.2), channel_id=1, source_target_pairs={{0,1},{1,2},{2,3},{3,4},{4,5},{5,6},{6,7},{7,8},{8,9},{9,10},{10,1... | collective-permute-start | bytes 800 | tf_op jit(solution)/shard_map/ppermute | solution.py:45
  33.0 8.7 %collective-permute-start.5 = (f32[1,66]{1,0:T(1,128)S(1)}, f32[1,66]{1,0:T(1,128)S(1)}, u32[]{:S(2)}, u32[]{:S(2)}) collective-permute-start(f32[1,66]{1,0:T(1,128)S(1)} %maximum_bitcast_fusion.2), channel_id=1, source_target_pairs={{0,2},{1,3},{2,4},{3,5},{4,6},{5,7},{6,8},{7,9},{8,10},{9,11},{10,... | collective-permute-start | bytes 800 | tf_op jit(solution)/shard_map/ppermute | solution.py:45
  38.3 4.9 %collective-permute-start.6 = (f32[1,66]{1,0:T(1,128)S(1)}, f32[1,66]{1,0:T(1,128)S(1)}, u32[]{:S(2)}, u32[]{:S(2)}) collective-permute-start(f32[1,66]{1,0:T(1,128)S(1)} %maximum_bitcast_fusion.3), channel_id=1, source_target_pairs={{1,0},{2,1},{3,2},{4,3},{5,4},{6,5},{7,6},{8,7},{9,8},{10,9},{11,1... | collective-permute-start | bytes 800 | tf_op jit(solution)/shard_map/ppermute | solution.py:45
  40.2 5.8 %collective-permute-start.7 = (f32[1,66]{1,0:T(1,128)S(1)}, f32[1,66]{1,0:T(1,128)S(1)}, u32[]{:S(2)}, u32[]{:S(2)}) collective-permute-start(f32[1,66]{1,0:T(1,128)S(1)} %maximum_bitcast_fusion.3), channel_id=1, source_target_pairs={{2,0},{3,1},{4,2},{5,3},{6,4},{7,5},{8,6},{9,7},{10,8},{11,9},{12,... | collective-permute-start | bytes 800 | tf_op jit(solution)/shard_map/ppermute | solution.py:45
  47.3 0.8 copy-start.1
  47.3 0.8 copy-start.4

commit v6 on v5

--- a/solution.py
+++ b/solution.py
@@ -50,17 +50,19 @@
     member = (clips[:, None] == clips[None, :]).astype(jnp.float32)
     own = jnp.dot(member, stats, precision=precise)
     clip_f = clips.astype(jnp.float32)
-    to_right = jnp.concatenate([clip_f[-1:], own[-1]])[None, :]
-    to_left = jnp.concatenate([clip_f[:1], own[0]])[None, :]
-    received = jnp.concatenate(
-        [
-            shifted(to_right, 1, n),
-            shifted(to_right, 2, n),
-            shifted(to_left, -1, n),
-            shifted(to_left, -2, n),
-        ],
-        axis=0,
-    )
+    to_right = jnp.concatenate([clip_f[-1:], own[-1]])
+    to_left = jnp.concatenate([clip_f[:1], own[0]])
+    mine = jnp.stack([to_left, to_right])
+    partner = lax.ppermute(mine, AXES, [(i, i ^ 1) for i in range(n)])
+    odd = (lax.axis_index(AXES) % 2) == 1
+    pair = jnp.where(odd, jnp.concatenate([partner, mine]), jnp.concatenate([mine, partner]))
+    from_left = shifted(pair, 2, n)
+    from_right = shifted(pair, -2, n)
+    left_near = jnp.where(odd, partner[1], from_left[3])
+    left_far = jnp.where(odd, from_left[3], from_left[1])
+    right_near = jnp.where(odd, from_right[0], partner[0])
+    right_far = jnp.where(odd, from_right[2], from_right[0])
+    received = jnp.stack([left_near, left_far, right_near, right_far])
     match = (clip_f[:, None] == received[None, :, 0]).astype(jnp.float32)
     return own + jnp.dot(match, received[:, 1:], precision=precise)
 

time: 128 us -> 120 us (0.938)
  starting transfers between devices: 24.1 us -> 12.9 us
  waiting for transfers between devices: 7.1 us -> 8.61 us
    ppermute x8 -> x4, starting transfers between devices: 24.1 us -> 7.96 us  [shifted(): return lax.ppermute(x, AXES, perm)]
    ppermute x0 -> x2, starting transfers between devices: none -> 4.93 us  [clip_totals(): partner = lax.ppermute(mine, AXES, [(i, i ^ 1) for i in range(n)])]
    broadcast_in_dim x4 -> x0, other arithmetic: 2.8 us -> none  [the longest x2 1.44 us: clip_totals(): to_right = jnp.concatenate([clip_f[-1:], own[-1]])[None, :]]
    another operation x0 -> x7, other arithmetic: none -> 2.77 us  [the longest x5 2.75 us: clip_totals(): mine = jnp.stack([to_left, to_right])]
    ppermute x8 -> x4, waiting for transfers between devices: 7.1 us -> 7.34 us  [shifted(): return lax.ppermute(x, AXES, perm)]
  transfers between devices with their start and end apart: 8 -> 6, of which waited for: 4 -> 4; matrix products, arithmetic and copies ran while one was open for 1% -> 0% of each run, Pallas kernels for 0% -> 0%
where the time goes in v6:
time: 120 us; the launch traced here: 119 us
  blocking collectives  78.1 us (65%)
  starting transfers between devices  12.9 us (11%)
  matrix products  10.1 us (8%)
  waiting for transfers between devices  8.61 us (7%)
  local copies, waits for them, and re-layouts  5.26 us (4%)
  other arithmetic  3.92 us (3%)
    all_to_all x1, blocking collectives, per_device(): lax.all_to_all(outgoing.reshape(group_width, capacity, LROWS, LAT), 'dev'...  43.6 us
    all_to_all x1, blocking collectives, per_device(): lax.all_to_all(forward.reshape(group_width, capacity, LROWS, LAT), 'dev',...  34.5 us
    ppermute x4, starting transfers between devices, shifted(): return lax.ppermute(x, AXES, perm)  7.96 us
    conv_general_dilated x2, matrix products, conv_local(): lax.conv_general_dilated(inputs, kernel, (1, stride, stride), ((2, 0), (1...  7.74 us
    ppermute x4, waiting for transfers between devices, shifted(): return lax.ppermute(x, AXES, perm)  7.34 us
    ppermute x2, starting transfers between devices, clip_totals(): partner = lax.ppermute(mine, AXES, [(i, i ^ 1) for i in range(n)])  4.93 us
    unnamed x24, local copies, waits for them, and re-layouts  2.78 us
    another operation x5, other arithmetic, clip_totals(): mine = jnp.stack([to_left, to_right])  2.75 us
  transfers between devices with their start and end apart: 6, of which 4 were waited for; matrix products, arithmetic and copies ran while one was open for 0% of the time, Pallas kernels for 0%

profile of v6, /device:TPU:1, one launch (start us, length us, event | category | flops | bytes accessed | tf_op | source)
XLA Modules:
  0.0 119.3 jit_solution(11811000829472351603)
XLA Ops:
  0.0 1.0 copy.52
  1.0 0.0 copy-start.5
  1.0 0.1 reshape.60
  1.1 0.0 copy-start.6
  1.1 0.0 copy-start.7
  1.1 3.3 %convert_reduce_fusion = (f32[48,128]{1,0:T(8,128)S(1)}, f32[48,128]{1,0:T(8,128)S(1)}, bf16[48,2,8,8,128]{4,0,3,2,1:T(8,128)(2,1)}) fusion(bf16[48,2,8,8,3]{0,4,3,2,1:T(4,128)(2,1)S(1)} %reshape.60, bf16[3,3,3,3,128]{4,3,2,1,0:T(4,128)(2,1)} %param.16), kind=kOutput, calls=%fused_computation.4 | convolution fusion | flops 57446400 | bytes 1679616 | tf_op jit(solution)/shard_map/conv_general_dilated | solution.py:23
  4.5 0.1 copy.53
  4.6 0.1 copy.54
  4.8 0.0 copy-done.8
  4.8 0.1 pad.37.clone
  4.9 0.2 fusion.33
  5.1 0.6 fusion.73
  5.7 1.3 %maximum_bitcast_fusion = (f32[1,66]{1,0:T(1,128)S(1)}, f32[1,66]{1,0:T(1,128)S(1)}) fusion(f32[65]{0:T(128)S(1)} %get-tuple-element.19, f32[1]{0:T(128)} %get-tuple-element.33, f32[65]{0:T(128)S(1)} %get-tuple-element.20, f32[1]{0:T(128)} %get-tuple-element.34), kind=kLoop, calls=%fused_computation.115 | loop fusion | flops 132 | bytes 1056 | tf_op jit(solution)/shard_map/stack | solution.py:55
  7.1 3.3 %collective-permute-start = (f32[2,66]{1,0:T(2,128)S(1)}, f32[2,66]{1,0:T(2,128)S(1)}, u32[]{:S(2)}, u32[]{:S(2)}) collective-permute-start(f32[2,66]{1,0:T(2,128)S(1)} %pad_maximum_fusion.2), channel_id=1, source_target_pairs={{0,1},{1,0},{2,3},{3,2},{4,5},{5,4},{6,7},{7,6},{8,9},{9,8},{10,11... | collective-permute-start | bytes 1592 | tf_op jit(solution)/shard_map/ppermute | solution.py:56
  10.4 0.2 convert_reduce_fusion.2
  10.6 0.6 collective-permute-done
  11.2 1.8 %collective-permute-start.1 = (f32[4,66]{1,0:T(4,128)S(1)}, f32[4,66]{1,0:T(4,128)S(1)}, u32[]{:S(2)}, u32[]{:S(2)}) collective-permute-start(f32[4,66]{1,0:T(4,128)S(1)} %maximum_select_fusion), channel_id=1, source_target_pairs={{0,2},{1,3},{2,4},{3,5},{4,6},{5,7},{6,8},{7,9},{8,10},{9,11},{10,... | collective-permute-start | bytes 3176 | tf_op jit(solution)/shard_map/ppermute | solution.py:45
  13.0 1.3 %collective-permute-start.2 = (f32[4,66]{1,0:T(4,128)S(1)}, f32[4,66]{1,0:T(4,128)S(1)}, u32[]{:S(2)}, u32[]{:S(2)}) collective-permute-start(f32[4,66]{1,0:T(4,128)S(1)} %maximum_select_fusion), channel_id=1, source_target_pairs={{2,0},{3,1},{4,2},{5,3},{6,4},{7,5},{8,6},{9,7},{10,8},{11,9},{12,... | collective-permute-start | bytes 3176 | tf_op jit(solution)/shard_map/ppermute | solution.py:45
  14.4 0.1 copy.55
  14.4 0.0 collective-permute-done.1
  14.4 3.1 %collective-permute-done.2 = f32[4,66]{1,0:T(4,128)S(1)} collective-permute-done((f32[4,66]{1,0:T(4,128)S(1)}, f32[4,66]{1,0:T(4,128)S(1)}, u32[]{:S(2)}, u32[]{:S(2)}) %collective-permute-start.2) | collective-permute-done | bytes 1088 | tf_op jit(solution)/shard_map/ppermute | solution.py:45
  17.6 0.1 slice_reduce_fusion.1
  17.7 0.3 convolution_add_fusion.2
  18.1 0.1 copy.57
  18.2 0.1 copy.58
  18.2 0.0 copy-done.6
  18.2 0.0 copy-done.7
  18.3 0.0 copy-start.9
  18.3 0.0 copy-start.2
  18.3 0.0 copy-start.3
  18.3 4.4 %convert_reduce_fusion.1 = (f32[48,256]{1,0:T(8,128)S(1)}, f32[48,256]{1,0:T(8,128)S(1)}, bf16[48,2,4,4,256]{4,0,3,2,1:T(8,128)(2,1)S(1)}) fusion(bf16[3,3,3,128,256]{4,3,2,1,0:T(8,128)(2,1)S(1)} %copy-done, bf16[48,2,8,8,128]{4,0,3,2,1:T(8,128)(2,1)} %get-tuple-element.35, f32[128]{0:T(128)S(1)} %copy-done.6, f32[128]{0:T(128)S(1)} %copy-done.7, ...), kind=kOutput, calls=%fused_computation.19 | convolution fusion | flops 1151705088 | bytes 4277248 | tf_op jit(solution)/shard_map/conv_general_dilated | solution.py:23
  22.7 0.1 copy.60
  22.8 0.1 copy.59
  23.0 0.2 fusion.38
  23.2 0.7 maximum_bitcast_fusion.2
  24.0 0.7 maximum_bitcast_fusion.3
  24.6 1.6 %collective-permute-start.3 = (f32[2,66]{1,0:T(2,128)S(1)}, f32[2,66]{1,0:T(2,128)S(1)}, u32[]{:S(2)}, u32[]{:S(2)}) collective-permute-start(f32[2,66]{1,0:T(2,128)S(1)} %pad_maximum_fusion.3), channel_id=1, source_target_pairs={{0,1},{1,0},{2,3},{3,2},{4,5},{5,4},{6,7},{7,6},{8,9},{9,8},{10,11... | collective-permute-start | bytes 1592 | tf_op jit(solution)/shard_map/ppermute | solution.py:56
  26.3 0.0 copy-done.9
  26.3 0.2 convert_reduce_fusion.3
  26.5 0.6 collective-permute-done.3
  27.1 3.5 %collective-permute-start.4 = (f32[4,66]{1,0:T(4,128)S(1)}, f32[4,66]{1,0:T(4,128)S(1)}, u32[]{:S(2)}, u32[]{:S(2)}) collective-permute-start(f32[4,66]{1,0:T(4,128)S(1)} %maximum_select_fusion.1), channel_id=1, source_target_pairs={{0,2},{1,3},{2,4},{3,5},{4,6},{5,7},{6,8},{7,9},{8,10},{9,11},{10,... | collective-permute-start | bytes 3176 | tf_op jit(solution)/shard_map/ppermute | solution.py:45
  30.7 1.3 %collective-permute-start.5 = (f32[4,66]{1,0:T(4,128)S(1)}, f32[4,66]{1,0:T(4,128)S(1)}, u32[]{:S(2)}, u32[]{:S(2)}) collective-permute-start(f32[4,66]{1,0:T(4,128)S(1)} %maximum_select_fusion.1), channel_id=1, source_target_pairs={{2,0},{3,1},{4,2},{5,3},{6,4},{7,5},{8,6},{9,7},{10,8},{11,9},{12,... | collective-permute-start | bytes 3176 | tf_op jit(solution)/shard_map/ppermute | solution.py:45
  32.0 0.1 copy.61
  32.1 0.0 collective-permute-done.4
  32.1 4.2 %collective-permute-done.5 = f32[4,66]{1,0:T(4,128)S(1)} collective-permute-done((f32[4,66]{1,0:T(4,128)S(1)}, f32[4,66]{1,0:T(4,128)S(1)}, u32[]{:S(2)}, u32[]{:S(2)}) %collective-permute-start.5) | collective-permute-done | bytes 1088 | tf_op jit(solution)/shard_map/ppermute | solution.py:45
  36.3 0.1 slice_reduce_fusion
  36.5 0.3 convolution_add_fusion.1
  36.8 0.1 copy.63
  36.9 0.1 copy.64
  37.0 0.0 copy-done.2
  37.0 0.6 fusion.20
  37.6 0.0 copy-start.1
  37.6 0.0 copy-start.4
  37.6 0.4 copy.65
  38.0 0.2 reshape.61
  38.2 0.2 copy-done.1
  38.4 0.4 fusion.10
  38.8 0.4 fusion.26
  39.2 0.2 copy.69
  39.5 43.6 %all_to_all.10 = bf16[64,2,32,128]{3,2,1,0:T(8,128)(2,1)S(1)} all-to-all(bf16[64,2,32,128]{3,2,1,0:T(8,128)(2,1)S(1)} %bitcast.64), channel_id=1, replica_groups=mesh['slab'=4,'dev'=64] {'dev'}, dimensions={0} | all-to-all | bytes 2097152 | tf_op jit(solution)/shard_map/all_to_all | solution.py:166
  83.0 0.5 fusion.27
  83.5 0.2 copy.71
  83.8 34.5 %all_to_all.11 = bf16[64,2,32,128]{3,2,1,0:T(8,128)(2,1)S(1)} all-to-all(bf16[64,2,32,128]{3,2,1,0:T(8,128)(2,1)S(1)} %bitcast.65), channel_id=1, replica_groups=mesh['slab'=4,'dev'=64] {'dev'}, dimensions={0} | all-to-all | bytes 2097152 | tf_op jit(solution)/shard_map/all_to_all | solution.py:174
  118.3 1.0 copy.81
  (31 shorter events, 0.4 us)
Async XLA Ops:
  0.0 18.2 %copy-start = (bf16[3,3,3,128,256]{4,3,2,1,0:T(8,128)(2,1)S(1)}, bf16[3,3,3,128,256]{4,3,2,1,0:T(8,128)(2,1)}, u32[]{:S(2)}) copy-start(bf16[3,3,3,128,256]{4,3,2,1,0:T(8,128)(2,1)} %param.19) | copy-start | bytes 5308420
  0.0 4.8 %copy-start.8 = (s32[48]{0:T(128)S(1)}, s32[48]{0:T(128)}, u32[]{:S(2)}) copy-start(s32[48]{0:T(128)} %param.13) | copy-start | bytes 580
  1.0 9.3 %copy-start.5 = (s32[128,1]{0,1:T(1,128)S(1)}, s32[128,1]{0,1:T(1,128)}, u32[]{:S(2)}) copy-start(s32[128,1]{0,1:T(1,128)} %param.15) | copy-start | bytes 1540
  1.1 17.1 %copy-start.6 = (f32[128]{0:T(128)S(1)}, f32[128]{0:T(128)}, u32[]{:S(2)}) copy-start(f32[128]{0:T(128)} %param.18) | copy-start | bytes 1540
  1.1 17.1 %copy-start.7 = (f32[128]{0:T(128)S(1)}, f32[128]{0:T(128)}, u32[]{:S(2)}) copy-start(f32[128]{0:T(128)} %param.17) | copy-start | bytes 1540
  7.1 4.1 %collective-permute-start = (f32[2,66]{1,0:T(2,128)S(1)}, f32[2,66]{1,0:T(2,128)S(1)}, u32[]{:S(2)}, u32[]{:S(2)}) collective-permute-start(f32[2,66]{1,0:T(2,128)S(1)} %pad_maximum_fusion.2), channel_id=1, source_target_pairs={{0,1},{1,0},{2,3},{3,2},{4,5},{5,4},{6,7},{7,6},{8,9},{9,8},{10,11... | collective-permute-start | bytes 1592 | tf_op jit(solution)/shard_map/ppermute | solution.py:56
  11.2 3.2 %collective-permute-start.1 = (f32[4,66]{1,0:T(4,128)S(1)}, f32[4,66]{1,0:T(4,128)S(1)}, u32[]{:S(2)}, u32[]{:S(2)}) collective-permute-start(f32[4,66]{1,0:T(4,128)S(1)} %maximum_select_fusion), channel_id=1, source_target_pairs={{0,2},{1,3},{2,4},{3,5},{4,6},{5,7},{6,8},{7,9},{8,10},{9,11},{10,... | collective-permute-start | bytes 3176 | tf_op jit(solution)/shard_map/ppermute | solution.py:45
  13.0 4.5 %collective-permute-start.2 = (f32[4,66]{1,0:T(4,128)S(1)}, f32[4,66]{1,0:T(4,128)S(1)}, u32[]{:S(2)}, u32[]{:S(2)}) collective-permute-start(f32[4,66]{1,0:T(4,128)S(1)} %maximum_select_fusion), channel_id=1, source_target_pairs={{2,0},{3,1},{4,2},{5,3},{6,4},{7,5},{8,6},{9,7},{10,8},{11,9},{12,... | collective-permute-start | bytes 3176 | tf_op jit(solution)/shard_map/ppermute | solution.py:45
  18.3 8.0 %copy-start.9 = (s32[48,1]{0,1:T(1,128)S(1)}, s32[48,1]{0,1:T(1,128)}, u32[]{:S(2)}) copy-start(s32[48,1]{0,1:T(1,128)} %param.14) | copy-start | bytes 580
  18.3 18.7 %copy-start.2 = (f32[256]{0:T(256)S(1)}, f32[256]{0:T(256)}, u32[]{:S(2)}) copy-start(f32[256]{0:T(256)} %param.21) | copy-start | bytes 3076
  18.3 18.7 %copy-start.3 = (f32[256]{0:T(256)S(1)}, f32[256]{0:T(256)}, u32[]{:S(2)}) copy-start(f32[256]{0:T(256)} %param.20) | copy-start | bytes 3076
  24.6 2.5 %collective-permute-start.3 = (f32[2,66]{1,0:T(2,128)S(1)}, f32[2,66]{1,0:T(2,128)S(1)}, u32[]{:S(2)}, u32[]{:S(2)}) collective-permute-start(f32[2,66]{1,0:T(2,128)S(1)} %pad_maximum_fusion.3), channel_id=1, source_target_pairs={{0,1},{1,0},{2,3},{3,2},{4,5},{5,4},{6,7},{7,6},{8,9},{9,8},{10,11... | collective-permute-start | bytes 1592 | tf_op jit(solution)/shard_map/ppermute | solution.py:56
  27.1 5.0 %collective-permute-start.4 = (f32[4,66]{1,0:T(4,128)S(1)}, f32[4,66]{1,0:T(4,128)S(1)}, u32[]{:S(2)}, u32[]{:S(2)}) collective-permute-start(f32[4,66]{1,0:T(4,128)S(1)} %maximum_select_fusion.1), channel_id=1, source_target_pairs={{0,2},{1,3},{2,4},{3,5},{4,6},{5,7},{6,8},{7,9},{8,10},{9,11},{10,... | collective-permute-start | bytes 3176 | tf_op jit(solution)/shard_map/ppermute | solution.py:45
  30.7 5.6 %collective-permute-start.5 = (f32[4,66]{1,0:T(4,128)S(1)}, f32[4,66]{1,0:T(4,128)S(1)}, u32[]{:S(2)}, u32[]{:S(2)}) collective-permute-start(f32[4,66]{1,0:T(4,128)S(1)} %maximum_select_fusion.1), channel_id=1, source_target_pairs={{2,0},{3,1},{4,2},{5,3},{6,4},{7,5},{8,6},{9,7},{10,8},{11,9},{12,... | collective-permute-start | bytes 3176 | tf_op jit(solution)/shard_map/ppermute | solution.py:45
  37.6 0.8 copy-start.1
  37.6 0.8 copy-start.4

commit v7 on v6

--- a/solution.py
+++ b/solution.py
@@ -47,12 +47,11 @@
 
 def clip_totals(clips, stats):
     n = lax.axis_size("slab") * lax.axis_size("dev")
-    member = (clips[:, None] == clips[None, :]).astype(jnp.float32)
-    own = jnp.dot(member, stats, precision=precise)
+    ends = jnp.stack([clips[0], clips[-1]])
+    edge = (ends[:, None] == clips[None, :]).astype(jnp.float32)
+    edge_sums = jnp.dot(edge, stats, precision=precise)
+    mine = jnp.concatenate([ends.astype(jnp.float32)[:, None], edge_sums], axis=1)
     clip_f = clips.astype(jnp.float32)
-    to_right = jnp.concatenate([clip_f[-1:], own[-1]])
-    to_left = jnp.concatenate([clip_f[:1], own[0]])
-    mine = jnp.stack([to_left, to_right])
     partner = lax.ppermute(mine, AXES, [(i, i ^ 1) for i in range(n)])
     odd = (lax.axis_index(AXES) % 2) == 1
     pair = jnp.where(odd, jnp.concatenate([partner, mine]), jnp.concatenate([mine, partner]))
@@ -63,6 +62,8 @@
     right_near = jnp.where(odd, from_right[0], partner[0])
     right_far = jnp.where(odd, from_right[2], from_right[0])
     received = jnp.stack([left_near, left_far, right_near, right_far])
+    member = (clips[:, None] == clips[None, :]).astype(jnp.float32)
+    own = jnp.dot(member, stats, precision=precise)
     match = (clip_f[:, None] == received[None, :, 0]).astype(jnp.float32)
     return own + jnp.dot(match, received[:, 1:], precision=precise)
 

time: 120 us -> 120 us (level)
    another operation x5 -> x1, other arithmetic: 2.75 us -> 1.33 us  [clip_totals(): ends = jnp.stack([clips[0], clips[-1]])]
    convert_element_type x0 -> x1, other arithmetic: none -> 1.26 us  [clip_totals(): ends.astype(jnp.float32)[:, None]]
  transfers between devices with their start and end apart: 6 -> 6, of which waited for: 4 -> 4; matrix products, arithmetic and copies ran while one was open for 0% -> 1% of each run, Pallas kernels for 0% -> 0%
where the time goes in v7:
time: 120 us
  blocking collectives  78.1 us (65%)
  starting transfers between devices  12.9 us (11%)
  matrix products  10.5 us (9%)
  waiting for transfers between devices  8.27 us (7%)
  local copies, waits for them, and re-layouts  5.71 us (5%)
  other arithmetic  4.05 us (3%)
    all_to_all x1, blocking collectives, per_device(): lax.all_to_all(outgoing.reshape(group_width, capacity, LROWS, LAT), 'dev'...  43.6 us
    all_to_all x1, blocking collectives, per_device(): lax.all_to_all(forward.reshape(group_width, capacity, LROWS, LAT), 'dev',...  34.5 us
    ppermute x4, starting transfers between devices, shifted(): return lax.ppermute(x, AXES, perm)  7.94 us
    conv_general_dilated x2, matrix products, conv_local(): lax.conv_general_dilated(inputs, kernel, (1, stride, stride), ((2, 0), (1...  7.74 us
    ppermute x4, waiting for transfers between devices, shifted(): return lax.ppermute(x, AXES, perm)  7.09 us
    ppermute x2, starting transfers between devices, clip_totals(): partner = lax.ppermute(mine, AXES, [(i, i ^ 1) for i in range(n)])  4.93 us
    unnamed x24, local copies, waits for them, and re-layouts  2.64 us
  transfers between devices with their start and end apart: 6, of which 4 were waited for; matrix products, arithmetic and copies ran while one was open for 1% of the time, Pallas kernels for 0%

profile of v7, /device:TPU:1, one launch (start us, length us, event | category | flops | bytes accessed | tf_op | source)
XLA Modules:
  0.0 119.9 jit_solution(12897402368947282137)
XLA Ops:
  0.0 1.4 %fusion.83 = (s32[1]{0:T(128)}, s32[1]{0:T(128)}) fusion(s32[48]{0:T(128)} %param.13), kind=kLoop, calls=%fused_computation.132 | loop fusion | bytes 16 | tf_op jit(solution)/shard_map/slice | solution.py:50
  1.4 0.9 copy.52
  2.3 0.0 copy-start.2
  2.3 0.1 reshape.90
  2.4 0.0 copy-start.6
  2.4 0.0 copy-start.9
  2.4 0.0 copy-start.7
  2.4 0.0 copy-start.8
  2.4 3.3 %convert_reduce_fusion = (f32[48,128]{1,0:T(8,128)S(1)}, f32[48,128]{1,0:T(8,128)S(1)}, bf16[48,2,8,8,128]{4,0,3,2,1:T(8,128)(2,1)}) fusion(bf16[48,2,8,8,3]{0,4,3,2,1:T(4,128)(2,1)S(1)} %reshape.90, bf16[3,3,3,3,128]{4,3,2,1,0:T(4,128)(2,1)} %param.16), kind=kOutput, calls=%fused_computation.4 | convolution fusion | flops 57446400 | bytes 1679616 | tf_op jit(solution)/shard_map/conv_general_dilated | solution.py:23
  5.8 0.1 copy.53
  5.9 0.1 copy.54
  6.1 1.3 %pad_add_fusion = s32[2]{0:T(128)S(1)} fusion(s32[1]{0:T(128)} %get-tuple-element.30, s32[1]{0:T(128)} %get-tuple-element.29), kind=kLoop, calls=%fused_computation.120 | loop fusion | flops 2 | bytes 16 | tf_op jit(solution)/shard_map/stack | solution.py:50
  7.4 0.1 pad.33.clone
  7.5 1.3 %add_convert_fusion = f32[2,1]{1,0:T(2,128)S(1)} fusion(s32[1,1]{1,0:T(1,128)} %bitcast.3, s32[1,1]{1,0:T(1,128)} %bitcast.2), kind=kLoop, calls=%fused_computation.105 | loop fusion | flops 4 | bytes 16 | tf_op jit(solution)/shard_map/convert_element_type | solution.py:53
  8.8 0.2 fusion.40
  8.9 0.1 pad_maximum_fusion.6
  9.0 3.3 %collective-permute-start = (f32[2,66]{1,0:T(2,128)S(1)}, f32[2,66]{1,0:T(2,128)S(1)}, u32[]{:S(2)}, u32[]{:S(2)}) collective-permute-start(f32[2,66]{1,0:T(2,128)S(1)} %pad_maximum_fusion.6), channel_id=1, source_target_pairs={{0,1},{1,0},{2,3},{3,2},{4,5},{5,4},{6,7},{7,6},{8,9},{9,8},{10,11... | collective-permute-start | bytes 1592 | tf_op jit(solution)/shard_map/ppermute | solution.py:55
  12.3 0.2 fusion.37
  12.6 0.2 convert_reduce_fusion.2
  12.8 0.4 collective-permute-done
  13.1 0.1 fusion.65
  13.2 1.8 %collective-permute-start.1 = (f32[4,66]{1,0:T(4,128)S(1)}, f32[4,66]{1,0:T(4,128)S(1)}, u32[]{:S(2)}, u32[]{:S(2)}) collective-permute-start(f32[4,66]{1,0:T(4,128)S(1)} %fusion.65), channel_id=1, source_target_pairs={{0,2},{1,3},{2,4},{3,5},{4,6},{5,7},{6,8},{7,9},{8,10},{9,11},{10,... | collective-permute-start | bytes 3176 | tf_op jit(solution)/shard_map/ppermute | solution.py:45
  15.0 1.3 %collective-permute-start.2 = (f32[4,66]{1,0:T(4,128)S(1)}, f32[4,66]{1,0:T(4,128)S(1)}, u32[]{:S(2)}, u32[]{:S(2)}) collective-permute-start(f32[4,66]{1,0:T(4,128)S(1)} %fusion.65), channel_id=1, source_target_pairs={{2,0},{3,1},{4,2},{5,3},{6,4},{7,5},{8,6},{9,7},{10,8},{11,9},{12,... | collective-permute-start | bytes 3176 | tf_op jit(solution)/shard_map/ppermute | solution.py:45
  16.3 0.2 convert_reduce_fusion.3
  16.5 3.0 %collective-permute-done.2 = f32[4,66]{1,0:T(4,128)S(1)} collective-permute-done((f32[4,66]{1,0:T(4,128)S(1)}, f32[4,66]{1,0:T(4,128)S(1)}, u32[]{:S(2)}, u32[]{:S(2)}) %collective-permute-start.2) | collective-permute-done | bytes 1088 | tf_op jit(solution)/shard_map/ppermute | solution.py:45
  19.6 0.1 slice_reduce_fusion.1
  19.7 0.3 convolution_add_fusion.2
  20.0 0.1 copy.57
  20.1 0.1 copy.58
  20.2 0.0 copy-done.7
  20.2 0.0 copy-start.3
  20.3 0.0 copy-start.4
  20.3 4.4 %convert_reduce_fusion.1 = (f32[48,256]{1,0:T(8,128)S(1)}, f32[48,256]{1,0:T(8,128)S(1)}, bf16[48,2,4,4,256]{4,0,3,2,1:T(8,128)(2,1)S(1)}) fusion(bf16[3,3,3,128,256]{4,3,2,1,0:T(8,128)(2,1)S(1)} %copy-done, bf16[48,2,8,8,128]{4,0,3,2,1:T(8,128)(2,1)} %get-tuple-element.31, f32[128]{0:T(128)S(1)} %copy-done.7, f32[128]{0:T(128)S(1)} %copy-done.8, ...), kind=kOutput, calls=%fused_computation.19 | convolution fusion | flops 1151705088 | bytes 4277248 | tf_op jit(solution)/shard_map/conv_general_dilated | solution.py:23
  24.7 0.1 copy.59
  24.8 0.1 copy.60
  24.9 0.1 bitcast_reduce_fusion
  25.0 0.2 fusion.39
  25.1 0.1 pad_maximum_fusion.7
  25.2 1.7 %collective-permute-start.3 = (f32[2,66]{1,0:T(2,128)S(1)}, f32[2,66]{1,0:T(2,128)S(1)}, u32[]{:S(2)}, u32[]{:S(2)}) collective-permute-start(f32[2,66]{1,0:T(2,128)S(1)} %pad_maximum_fusion.7), channel_id=1, source_target_pairs={{0,1},{1,0},{2,3},{3,2},{4,5},{5,4},{6,7},{7,6},{8,9},{9,8},{10,11... | collective-permute-start | bytes 1592 | tf_op jit(solution)/shard_map/ppermute | solution.py:55
  26.9 0.8 collective-permute-done.3
  27.7 0.1 fusion.67
  27.8 3.5 %collective-permute-start.4 = (f32[4,66]{1,0:T(4,128)S(1)}, f32[4,66]{1,0:T(4,128)S(1)}, u32[]{:S(2)}, u32[]{:S(2)}) collective-permute-start(f32[4,66]{1,0:T(4,128)S(1)} %fusion.67), channel_id=1, source_target_pairs={{0,2},{1,3},{2,4},{3,5},{4,6},{5,7},{6,8},{7,9},{8,10},{9,11},{10,... | collective-permute-start | bytes 3176 | tf_op jit(solution)/shard_map/ppermute | solution.py:45
  31.3 1.3 %collective-permute-start.5 = (f32[4,66]{1,0:T(4,128)S(1)}, f32[4,66]{1,0:T(4,128)S(1)}, u32[]{:S(2)}, u32[]{:S(2)}) collective-permute-start(f32[4,66]{1,0:T(4,128)S(1)} %fusion.67), channel_id=1, source_target_pairs={{2,0},{3,1},{4,2},{5,3},{6,4},{7,5},{8,6},{9,7},{10,8},{11,9},{12,... | collective-permute-start | bytes 3176 | tf_op jit(solution)/shard_map/ppermute | solution.py:45
  32.6 0.2 fusion.35
  32.9 4.1 %collective-permute-done.5 = f32[4,66]{1,0:T(4,128)S(1)} collective-permute-done((f32[4,66]{1,0:T(4,128)S(1)}, f32[4,66]{1,0:T(4,128)S(1)}, u32[]{:S(2)}, u32[]{:S(2)}) %collective-permute-start.5) | collective-permute-done | bytes 1088 | tf_op jit(solution)/shard_map/ppermute | solution.py:45
  37.0 0.1 slice_reduce_fusion
  37.1 0.3 convolution_add_fusion.1
  37.4 0.1 copy.63
  37.5 0.1 copy.64
  37.6 0.0 copy-done.3
  37.6 0.6 fusion.20
  38.2 0.0 copy-start.1
  38.2 0.0 copy-start.5
  38.2 0.4 copy.65
  38.6 0.2 reshape.91
  38.8 0.2 copy-done.1
  39.0 0.4 fusion.10
  39.4 0.4 fusion.26
  39.8 0.2 copy.71
  40.1 43.6 %all_to_all.10 = bf16[64,2,32,128]{3,2,1,0:T(8,128)(2,1)S(1)} all-to-all(bf16[64,2,32,128]{3,2,1,0:T(8,128)(2,1)S(1)} %bitcast.50), channel_id=1, replica_groups=mesh['slab'=4,'dev'=64] {'dev'}, dimensions={0} | all-to-all | bytes 2097152 | tf_op jit(solution)/shard_map/all_to_all | solution.py:167
  83.7 0.5 fusion.27
  84.2 0.2 copy.73
  84.4 34.5 %all_to_all.11 = bf16[64,2,32,128]{3,2,1,0:T(8,128)(2,1)S(1)} all-to-all(bf16[64,2,32,128]{3,2,1,0:T(8,128)(2,1)S(1)} %bitcast.51), channel_id=1, replica_groups=mesh['slab'=4,'dev'=64] {'dev'}, dimensions={0} | all-to-all | bytes 2097152 | tf_op jit(solution)/shard_map/all_to_all | solution.py:175
  118.9 1.0 copy.83
  (27 shorter events, 0.3 us)
Async XLA Ops:
  0.0 20.2 %copy-start = (bf16[3,3,3,128,256]{4,3,2,1,0:T(8,128)(2,1)S(1)}, bf16[3,3,3,128,256]{4,3,2,1,0:T(8,128)(2,1)}, u32[]{:S(2)}) copy-start(bf16[3,3,3,128,256]{4,3,2,1,0:T(8,128)(2,1)} %param.19) | copy-start | bytes 5308420
  2.3 6.5 %copy-start.2 = (s32[48]{0:T(128)S(1)}, s32[48]{0:T(128)}, u32[]{:S(2)}) copy-start(s32[48]{0:T(128)} %param.13) | copy-start | bytes 580
  2.4 10.2 %copy-start.6 = (s32[128,1]{0,1:T(1,128)S(1)}, s32[128,1]{0,1:T(1,128)}, u32[]{:S(2)}) copy-start(s32[128,1]{0,1:T(1,128)} %param.15) | copy-start | bytes 1540
  2.4 13.9 %copy-start.9 = (s32[48,1]{0,1:T(1,128)S(1)}, s32[48,1]{0,1:T(1,128)}, u32[]{:S(2)}) copy-start(s32[48,1]{0,1:T(1,128)} %param.14) | copy-start | bytes 580
  2.4 17.8 %copy-start.7 = (f32[128]{0:T(128)S(1)}, f32[128]{0:T(128)}, u32[]{:S(2)}) copy-start(f32[128]{0:T(128)} %param.18) | copy-start | bytes 1540
  2.4 17.8 %copy-start.8 = (f32[128]{0:T(128)S(1)}, f32[128]{0:T(128)}, u32[]{:S(2)}) copy-start(f32[128]{0:T(128)} %param.17) | copy-start | bytes 1540
  9.0 4.1 %collective-permute-start = (f32[2,66]{1,0:T(2,128)S(1)}, f32[2,66]{1,0:T(2,128)S(1)}, u32[]{:S(2)}, u32[]{:S(2)}) collective-permute-start(f32[2,66]{1,0:T(2,128)S(1)} %pad_maximum_fusion.6), channel_id=1, source_target_pairs={{0,1},{1,0},{2,3},{3,2},{4,5},{5,4},{6,7},{7,6},{8,9},{9,8},{10,11... | collective-permute-start | bytes 1592 | tf_op jit(solution)/shard_map/ppermute | solution.py:55
  13.2 3.3 %collective-permute-start.1 = (f32[4,66]{1,0:T(4,128)S(1)}, f32[4,66]{1,0:T(4,128)S(1)}, u32[]{:S(2)}, u32[]{:S(2)}) collective-permute-start(f32[4,66]{1,0:T(4,128)S(1)} %fusion.65), channel_id=1, source_target_pairs={{0,2},{1,3},{2,4},{3,5},{4,6},{5,7},{6,8},{7,9},{8,10},{9,11},{10,... | collective-permute-start | bytes 3176 | tf_op jit(solution)/shard_map/ppermute | solution.py:45
  15.0 4.5 %collective-permute-start.2 = (f32[4,66]{1,0:T(4,128)S(1)}, f32[4,66]{1,0:T(4,128)S(1)}, u32[]{:S(2)}, u32[]{:S(2)}) collective-permute-start(f32[4,66]{1,0:T(4,128)S(1)} %fusion.65), channel_id=1, source_target_pairs={{2,0},{3,1},{4,2},{5,3},{6,4},{7,5},{8,6},{9,7},{10,8},{11,9},{12,... | collective-permute-start | bytes 3176 | tf_op jit(solution)/shard_map/ppermute | solution.py:45
  20.2 17.4 %copy-start.3 = (f32[256]{0:T(256)S(1)}, f32[256]{0:T(256)}, u32[]{:S(2)}) copy-start(f32[256]{0:T(256)} %param.21) | copy-start | bytes 3076
  20.3 17.4 %copy-start.4 = (f32[256]{0:T(256)S(1)}, f32[256]{0:T(256)}, u32[]{:S(2)}) copy-start(f32[256]{0:T(256)} %param.20) | copy-start | bytes 3076
  25.2 2.5 %collective-permute-start.3 = (f32[2,66]{1,0:T(2,128)S(1)}, f32[2,66]{1,0:T(2,128)S(1)}, u32[]{:S(2)}, u32[]{:S(2)}) collective-permute-start(f32[2,66]{1,0:T(2,128)S(1)} %pad_maximum_fusion.7), channel_id=1, source_target_pairs={{0,1},{1,0},{2,3},{3,2},{4,5},{5,4},{6,7},{7,6},{8,9},{9,8},{10,11... | collective-permute-start | bytes 1592 | tf_op jit(solution)/shard_map/ppermute | solution.py:55
  27.8 5.1 %collective-permute-start.4 = (f32[4,66]{1,0:T(4,128)S(1)}, f32[4,66]{1,0:T(4,128)S(1)}, u32[]{:S(2)}, u32[]{:S(2)}) collective-permute-start(f32[4,66]{1,0:T(4,128)S(1)} %fusion.67), channel_id=1, source_target_pairs={{0,2},{1,3},{2,4},{3,5},{4,6},{5,7},{6,8},{7,9},{8,10},{9,11},{10,... | collective-permute-start | bytes 3176 | tf_op jit(solution)/shard_map/ppermute | solution.py:45
  31.3 5.6 %collective-permute-start.5 = (f32[4,66]{1,0:T(4,128)S(1)}, f32[4,66]{1,0:T(4,128)S(1)}, u32[]{:S(2)}, u32[]{:S(2)}) collective-permute-start(f32[4,66]{1,0:T(4,128)S(1)} %fusion.67), channel_id=1, source_target_pairs={{2,0},{3,1},{4,2},{5,3},{6,4},{7,5},{8,6},{9,7},{10,8},{11,9},{12,... | collective-permute-start | bytes 3176 | tf_op jit(solution)/shard_map/ppermute | solution.py:45
  38.2 0.8 copy-start.1
  38.2 0.8 copy-start.5

commit v8 on v6

--- a/solution.py
+++ b/solution.py
@@ -53,15 +53,15 @@
     to_right = jnp.concatenate([clip_f[-1:], own[-1]])
     to_left = jnp.concatenate([clip_f[:1], own[0]])
     mine = jnp.stack([to_left, to_right])
-    partner = lax.ppermute(mine, AXES, [(i, i ^ 1) for i in range(n)])
+    from_left = shifted(mine, 2, n)
+    from_right = shifted(mine, -2, n)
+    bundle = jnp.concatenate([mine, from_left, from_right])
+    partner = lax.ppermute(bundle, AXES, [(i, i ^ 1) for i in range(n)])
     odd = (lax.axis_index(AXES) % 2) == 1
-    pair = jnp.where(odd, jnp.concatenate([partner, mine]), jnp.concatenate([mine, partner]))
-    from_left = shifted(pair, 2, n)
-    from_right = shifted(pair, -2, n)
-    left_near = jnp.where(odd, partner[1], from_left[3])
-    left_far = jnp.where(odd, from_left[3], from_left[1])
-    right_near = jnp.where(odd, from_right[0], partner[0])
-    right_far = jnp.where(odd, from_right[2], from_right[0])
+    left_near = jnp.where(odd, partner[1], partner[3])
+    left_far = from_left[1]
+    right_near = jnp.where(odd, partner[4], partner[0])
+    right_far = from_right[0]
     received = jnp.stack([left_near, left_far, right_near, right_far])
     match = (clip_f[:, None] == received[None, :, 0]).astype(jnp.float32)
     return own + jnp.dot(match, received[:, 1:], precision=precise)

time: 120 us -> 120 us (level)
    ppermute x4, starting transfers between devices: 7.96 us -> 10.5 us  [shifted(): return lax.ppermute(x, AXES, perm)]
    ppermute x2, starting transfers between devices: 4.93 us -> 3.58 us  [clip_totals(): partner = lax.ppermute(bundle, AXES, [(i, i ^ 1) for i in range(n)])]
where the time goes in v8:
time: 120 us; the launch traced here: 119 us
  blocking collectives  76.9 us (64%)
  starting transfers between devices  14.1 us (12%)
  matrix products  10.1 us (8%)
  waiting for transfers between devices  8.56 us (7%)
  local copies, waits for them, and re-layouts  5.27 us (4%)
  other arithmetic  3.92 us (3%)
    all_to_all x1, blocking collectives, per_device(): lax.all_to_all(outgoing.reshape(group_width, capacity, LROWS, LAT), 'dev'...  42.4 us
    all_to_all x1, blocking collectives, per_device(): lax.all_to_all(forward.reshape(group_width, capacity, LROWS, LAT), 'dev',...  34.5 us
    ppermute x4, starting transfers between devices, shifted(): return lax.ppermute(x, AXES, perm)  10.5 us
    conv_general_dilated x2, matrix products, conv_local(): lax.conv_general_dilated(inputs, kernel, (1, stride, stride), ((2, 0), (1...  7.74 us
    ppermute x4, waiting for transfers between devices, shifted(): return lax.ppermute(x, AXES, perm)  7.14 us
    ppermute x2, starting transfers between devices, clip_totals(): partner = lax.ppermute(bundle, AXES, [(i, i ^ 1) for i in range(n)])  3.58 us
    unnamed x24, local copies, waits for them, and re-layouts  2.78 us
    another operation x5, other arithmetic, clip_totals(): mine = jnp.stack([to_left, to_right])  2.75 us
  transfers between devices with their start and end apart: 6, of which 4 were waited for; matrix products, arithmetic and copies ran while one was open for 0% of the time, Pallas kernels for 0%

profile of v8, /device:TPU:1, one launch (start us, length us, event | category | flops | bytes accessed | tf_op | source)
XLA Modules:
  0.0 119.3 jit_solution(4831077674866203015)
XLA Ops:
  0.0 0.0 copy-start
  0.0 1.0 copy.52
  1.0 0.0 copy-start.5
  1.0 0.1 reshape.60
  1.1 0.0 copy-start.6
  1.1 0.0 copy-start.7
  1.1 3.3 %convert_reduce_fusion = (f32[48,128]{1,0:T(8,128)S(1)}, f32[48,128]{1,0:T(8,128)S(1)}, bf16[48,2,8,8,128]{4,0,3,2,1:T(8,128)(2,1)}) fusion(bf16[48,2,8,8,3]{0,4,3,2,1:T(4,128)(2,1)S(1)} %reshape.60, bf16[3,3,3,3,128]{4,3,2,1,0:T(4,128)(2,1)} %param.16), kind=kOutput, calls=%fused_computation.4 | convolution fusion | flops 57446400 | bytes 1679616 | tf_op jit(solution)/shard_map/conv_general_dilated | solution.py:23
  4.5 0.1 copy.53
  4.6 0.1 copy.54
  4.8 0.0 copy-done.8
  4.8 0.1 pad.33.clone
  4.9 0.2 fusion.33
  5.1 0.6 fusion.73
  5.7 1.3 %maximum_bitcast_fusion = (f32[1,66]{1,0:T(1,128)S(1)}, f32[1,66]{1,0:T(1,128)S(1)}) fusion(f32[65]{0:T(128)S(1)} %get-tuple-element.19, f32[1]{0:T(128)} %get-tuple-element.25, f32[65]{0:T(128)S(1)} %get-tuple-element.20, f32[1]{0:T(128)} %get-tuple-element.26), kind=kLoop, calls=%fused_computation.111 | loop fusion | flops 132 | bytes 1056 | tf_op jit(solution)/shard_map/stack | solution.py:55
  7.1 4.4 %collective-permute-start = (f32[2,66]{1,0:T(2,128)S(1)}, f32[2,66]{1,0:T(2,128)S(1)}, u32[]{:S(2)}, u32[]{:S(2)}) collective-permute-start(f32[2,66]{1,0:T(2,128)S(1)} %pad_maximum_fusion.4), channel_id=1, source_target_pairs={{0,2},{1,3},{2,4},{3,5},{4,6},{5,7},{6,8},{7,9},{8,10},{9,11},{10,... | collective-permute-start | bytes 1592 | tf_op jit(solution)/shard_map/ppermute | solution.py:45
  11.4 1.3 %collective-permute-start.1 = (f32[2,66]{1,0:T(2,128)S(1)}, f32[2,66]{1,0:T(2,128)S(1)}, u32[]{:S(2)}, u32[]{:S(2)}) collective-permute-start(f32[2,66]{1,0:T(2,128)S(1)} %pad_maximum_fusion.4), channel_id=1, source_target_pairs={{2,0},{3,1},{4,2},{5,3},{6,4},{7,5},{8,6},{9,7},{10,8},{11,9},{12,... | collective-permute-start | bytes 1592 | tf_op jit(solution)/shard_map/ppermute | solution.py:45
  12.8 0.2 convert_reduce_fusion.2
  12.9 0.0 collective-permute-done
  12.9 3.0 %collective-permute-done.1 = f32[2,66]{1,0:T(2,128)S(1)} collective-permute-done((f32[2,66]{1,0:T(2,128)S(1)}, f32[2,66]{1,0:T(2,128)S(1)}, u32[]{:S(2)}, u32[]{:S(2)}) %collective-permute-start.1) | collective-permute-done | bytes 560 | tf_op jit(solution)/shard_map/ppermute | solution.py:45
  16.0 2.0 %collective-permute-start.2 = (f32[6,66]{1,0:T(8,128)S(1)}, f32[6,66]{1,0:T(8,128)S(1)}, u32[]{:S(2)}, u32[]{:S(2)}) collective-permute-start(f32[6,66]{1,0:T(8,128)S(1)} %pad_maximum_fusion), channel_id=1, source_target_pairs={{0,1},{1,0},{2,3},{3,2},{4,5},{5,4},{6,7},{7,6},{8,9},{9,8},{10,11... | collective-permute-start | bytes 4760 | tf_op jit(solution)/shard_map/ppermute | solution.py:59
  18.0 0.1 copy.55
  18.1 0.7 collective-permute-done.2
  18.8 0.1 slice_reduce_fusion.1
  18.9 0.3 convolution_add_fusion.2
  19.3 0.1 copy.57
  19.4 0.1 copy.58
  19.5 0.0 copy-done.6
  19.5 0.0 copy-start.9
  19.5 0.0 copy-start.2
  19.5 0.0 copy-start.3
  19.5 4.4 %convert_reduce_fusion.1 = (f32[48,256]{1,0:T(8,128)S(1)}, f32[48,256]{1,0:T(8,128)S(1)}, bf16[48,2,4,4,256]{4,0,3,2,1:T(8,128)(2,1)S(1)}) fusion(bf16[3,3,3,128,256]{4,3,2,1,0:T(8,128)(2,1)S(1)} %copy-done, bf16[48,2,8,8,128]{4,0,3,2,1:T(8,128)(2,1)} %get-tuple-element.27, f32[128]{0:T(128)S(1)} %copy-done.6, f32[128]{0:T(128)S(1)} %copy-done.7, ...), kind=kOutput, calls=%fused_computation.19 | convolution fusion | flops 1151705088 | bytes 4277248 | tf_op jit(solution)/shard_map/conv_general_dilated | solution.py:23
  23.9 0.1 copy.60
  24.1 0.1 copy.59
  24.2 0.2 fusion.38
  24.5 0.7 maximum_bitcast_fusion.2
  25.2 0.7 maximum_bitcast_fusion.3
  25.9 3.5 %collective-permute-start.3 = (f32[2,66]{1,0:T(2,128)S(1)}, f32[2,66]{1,0:T(2,128)S(1)}, u32[]{:S(2)}, u32[]{:S(2)}) collective-permute-start(f32[2,66]{1,0:T(2,128)S(1)} %pad_maximum_fusion.5), channel_id=1, source_target_pairs={{0,2},{1,3},{2,4},{3,5},{4,6},{5,7},{6,8},{7,9},{8,10},{9,11},{10,... | collective-permute-start | bytes 1592 | tf_op jit(solution)/shard_map/ppermute | solution.py:45
  29.4 1.3 %collective-permute-start.4 = (f32[2,66]{1,0:T(2,128)S(1)}, f32[2,66]{1,0:T(2,128)S(1)}, u32[]{:S(2)}, u32[]{:S(2)}) collective-permute-start(f32[2,66]{1,0:T(2,128)S(1)} %pad_maximum_fusion.5), channel_id=1, source_target_pairs={{2,0},{3,1},{4,2},{5,3},{6,4},{7,5},{8,6},{9,7},{10,8},{11,9},{12,... | collective-permute-start | bytes 1592 | tf_op jit(solution)/shard_map/ppermute | solution.py:45
  30.7 0.0 copy-done.9
  30.7 0.2 convert_reduce_fusion.3
  30.9 0.0 collective-permute-done.3
  30.9 4.1 %collective-permute-done.4 = f32[2,66]{1,0:T(2,128)S(1)} collective-permute-done((f32[2,66]{1,0:T(2,128)S(1)}, f32[2,66]{1,0:T(2,128)S(1)}, u32[]{:S(2)}, u32[]{:S(2)}) %collective-permute-start.4) | collective-permute-done | bytes 560 | tf_op jit(solution)/shard_map/ppermute | solution.py:45
  35.1 1.6 %collective-permute-start.5 = (f32[6,66]{1,0:T(8,128)S(1)}, f32[6,66]{1,0:T(8,128)S(1)}, u32[]{:S(2)}, u32[]{:S(2)}) collective-permute-start(f32[6,66]{1,0:T(8,128)S(1)} %pad_maximum_fusion.1), channel_id=1, source_target_pairs={{0,1},{1,0},{2,3},{3,2},{4,5},{5,4},{6,7},{7,6},{8,9},{9,8},{10,11... | collective-permute-start | bytes 4760 | tf_op jit(solution)/shard_map/ppermute | solution.py:59
  36.6 0.1 copy.61
  36.7 0.7 collective-permute-done.5
  37.5 0.1 slice_reduce_fusion
  37.6 0.3 convolution_add_fusion.1
  38.0 0.1 copy.63
  38.1 0.1 copy.64
  38.1 0.0 copy-done.2
  38.1 0.5 fusion.20
  38.7 0.0 copy-start.1
  38.7 0.0 copy-start.4
  38.7 0.4 copy.65
  39.1 0.2 reshape.61
  39.3 0.2 copy-done.1
  39.5 0.4 fusion.10
  39.9 0.4 fusion.26
  40.4 0.2 copy.69
  40.6 42.4 %all_to_all.10 = bf16[64,2,32,128]{3,2,1,0:T(8,128)(2,1)S(1)} all-to-all(bf16[64,2,32,128]{3,2,1,0:T(8,128)(2,1)S(1)} %bitcast.64), channel_id=1, replica_groups=mesh['slab'=4,'dev'=64] {'dev'}, dimensions={0} | all-to-all | bytes 2097152 | tf_op jit(solution)/shard_map/all_to_all | solution.py:166
  83.0 0.5 fusion.27
  83.5 0.2 copy.71
  83.8 34.5 %all_to_all.11 = bf16[64,2,32,128]{3,2,1,0:T(8,128)(2,1)S(1)} all-to-all(bf16[64,2,32,128]{3,2,1,0:T(8,128)(2,1)S(1)} %bitcast.65), channel_id=1, replica_groups=mesh['slab'=4,'dev'=64] {'dev'}, dimensions={0} | all-to-all | bytes 2097152 | tf_op jit(solution)/shard_map/all_to_all | solution.py:174
  118.3 1.0 copy.81
  (35 shorter events, 0.4 us)
Async XLA Ops:
  0.0 19.4 %copy-start = (bf16[3,3,3,128,256]{4,3,2,1,0:T(8,128)(2,1)S(1)}, bf16[3,3,3,128,256]{4,3,2,1,0:T(8,128)(2,1)}, u32[]{:S(2)}) copy-start(bf16[3,3,3,128,256]{4,3,2,1,0:T(8,128)(2,1)} %param.19) | copy-start | bytes 5308420
  0.0 4.8 %copy-start.8 = (s32[48]{0:T(128)S(1)}, s32[48]{0:T(128)}, u32[]{:S(2)}) copy-start(s32[48]{0:T(128)} %param.13) | copy-start | bytes 580
  1.0 11.7 %copy-start.5 = (s32[128,1]{0,1:T(1,128)S(1)}, s32[128,1]{0,1:T(1,128)}, u32[]{:S(2)}) copy-start(s32[128,1]{0,1:T(1,128)} %param.15) | copy-start | bytes 1540
  1.1 18.3 %copy-start.6 = (f32[128]{0:T(128)S(1)}, f32[128]{0:T(128)}, u32[]{:S(2)}) copy-start(f32[128]{0:T(128)} %param.18) | copy-start | bytes 1540
  1.1 18.3 %copy-start.7 = (f32[128]{0:T(128)S(1)}, f32[128]{0:T(128)}, u32[]{:S(2)}) copy-start(f32[128]{0:T(128)} %param.17) | copy-start | bytes 1540
  7.1 5.9 %collective-permute-start = (f32[2,66]{1,0:T(2,128)S(1)}, f32[2,66]{1,0:T(2,128)S(1)}, u32[]{:S(2)}, u32[]{:S(2)}) collective-permute-start(f32[2,66]{1,0:T(2,128)S(1)} %pad_maximum_fusion.4), channel_id=1, source_target_pairs={{0,2},{1,3},{2,4},{3,5},{4,6},{5,7},{6,8},{7,9},{8,10},{9,11},{10,... | collective-permute-start | bytes 1592 | tf_op jit(solution)/shard_map/ppermute | solution.py:45
  11.4 4.5 %collective-permute-start.1 = (f32[2,66]{1,0:T(2,128)S(1)}, f32[2,66]{1,0:T(2,128)S(1)}, u32[]{:S(2)}, u32[]{:S(2)}) collective-permute-start(f32[2,66]{1,0:T(2,128)S(1)} %pad_maximum_fusion.4), channel_id=1, source_target_pairs={{2,0},{3,1},{4,2},{5,3},{6,4},{7,5},{8,6},{9,7},{10,8},{11,9},{12,... | collective-permute-start | bytes 1592 | tf_op jit(solution)/shard_map/ppermute | solution.py:45
  16.0 2.8 %collective-permute-start.2 = (f32[6,66]{1,0:T(8,128)S(1)}, f32[6,66]{1,0:T(8,128)S(1)}, u32[]{:S(2)}, u32[]{:S(2)}) collective-permute-start(f32[6,66]{1,0:T(8,128)S(1)} %pad_maximum_fusion), channel_id=1, source_target_pairs={{0,1},{1,0},{2,3},{3,2},{4,5},{5,4},{6,7},{7,6},{8,9},{9,8},{10,11... | collective-permute-start | bytes 4760 | tf_op jit(solution)/shard_map/ppermute | solution.py:59
  19.5 11.2 %copy-start.9 = (s32[48,1]{0,1:T(1,128)S(1)}, s32[48,1]{0,1:T(1,128)}, u32[]{:S(2)}) copy-start(s32[48,1]{0,1:T(1,128)} %param.14) | copy-start | bytes 580
  19.5 18.6 %copy-start.2 = (f32[256]{0:T(256)S(1)}, f32[256]{0:T(256)}, u32[]{:S(2)}) copy-start(f32[256]{0:T(256)} %param.21) | copy-start | bytes 3076
  19.5 18.6 %copy-start.3 = (f32[256]{0:T(256)S(1)}, f32[256]{0:T(256)}, u32[]{:S(2)}) copy-start(f32[256]{0:T(256)} %param.20) | copy-start | bytes 3076
  25.9 5.0 %collective-permute-start.3 = (f32[2,66]{1,0:T(2,128)S(1)}, f32[2,66]{1,0:T(2,128)S(1)}, u32[]{:S(2)}, u32[]{:S(2)}) collective-permute-start(f32[2,66]{1,0:T(2,128)S(1)} %pad_maximum_fusion.5), channel_id=1, source_target_pairs={{0,2},{1,3},{2,4},{3,5},{4,6},{5,7},{6,8},{7,9},{8,10},{9,11},{10,... | collective-permute-start | bytes 1592 | tf_op jit(solution)/shard_map/ppermute | solution.py:45
  29.4 5.6 %collective-permute-start.4 = (f32[2,66]{1,0:T(2,128)S(1)}, f32[2,66]{1,0:T(2,128)S(1)}, u32[]{:S(2)}, u32[]{:S(2)}) collective-permute-start(f32[2,66]{1,0:T(2,128)S(1)} %pad_maximum_fusion.5), channel_id=1, source_target_pairs={{2,0},{3,1},{4,2},{5,3},{6,4},{7,5},{8,6},{9,7},{10,8},{11,9},{12,... | collective-permute-start | bytes 1592 | tf_op jit(solution)/shard_map/ppermute | solution.py:45
  35.1 2.4 %collective-permute-start.5 = (f32[6,66]{1,0:T(8,128)S(1)}, f32[6,66]{1,0:T(8,128)S(1)}, u32[]{:S(2)}, u32[]{:S(2)}) collective-permute-start(f32[6,66]{1,0:T(8,128)S(1)} %pad_maximum_fusion.1), channel_id=1, source_target_pairs={{0,1},{1,0},{2,3},{3,2},{4,5},{5,4},{6,7},{7,6},{8,9},{9,8},{10,11... | collective-permute-start | bytes 4760 | tf_op jit(solution)/shard_map/ppermute | solution.py:59
  38.7 0.8 copy-start.1
  38.7 0.8 copy-start.4

commit v9 on v8

--- a/solution.py
+++ b/solution.py
@@ -47,11 +47,11 @@
 
 def clip_totals(clips, stats):
     n = lax.axis_size("slab") * lax.axis_size("dev")
-    member = (clips[:, None] == clips[None, :]).astype(jnp.float32)
-    own = jnp.dot(member, stats, precision=precise)
     clip_f = clips.astype(jnp.float32)
-    to_right = jnp.concatenate([clip_f[-1:], own[-1]])
-    to_left = jnp.concatenate([clip_f[:1], own[0]])
+    first = jnp.sum(jnp.where((clips == clips[0])[:, None], stats, 0.0), axis=0)
+    last = jnp.sum(jnp.where((clips == clips[-1])[:, None], stats, 0.0), axis=0)
+    to_right = jnp.concatenate([clip_f[-1:], last])
+    to_left = jnp.concatenate([clip_f[:1], first])
     mine = jnp.stack([to_left, to_right])
     from_left = shifted(mine, 2, n)
     from_right = shifted(mine, -2, n)
@@ -63,6 +63,8 @@
     right_near = jnp.where(odd, partner[4], partner[0])
     right_far = from_right[0]
     received = jnp.stack([left_near, left_far, right_near, right_far])
+    member = (clips[:, None] == clips[None, :]).astype(jnp.float32)
+    own = jnp.dot(member, stats, precision=precise)
     match = (clip_f[:, None] == received[None, :, 0]).astype(jnp.float32)
     return own + jnp.dot(match, received[:, 1:], precision=precise)
 

time: 120 us -> 123 us (1.025)
  other arithmetic: 3.92 us -> 6.24 us
    slice x1 -> x2, local copies, waits for them, and re-layouts: 0.61 us -> 1.99 us  [the longest x1 1.38 us: clip_totals(): last = jnp.sum(jnp.where((clips == clips[-1])[:, None], stats, 0.0), axis=0)]
    eq x0 -> x1, other arithmetic: none -> 1.25 us  [clip_totals(): last = jnp.sum(jnp.where((clips == clips[-1])[:, None], stats, 0.0), axis=0)]
  transfers between devices with their start and end apart: 6 -> 6, of which waited for: 4 -> 4; matrix products, arithmetic and copies ran while one was open for 0% -> 1% of each run, Pallas kernels for 0% -> 0%
where the time goes in v9:
time: 123 us; the launch traced here: 122 us
  blocking collectives  76.9 us (63%)
  starting transfers between devices  14.1 us (11%)
  matrix products  10.1 us (8%)
  waiting for transfers between devices  8.23 us (7%)
  local copies, waits for them, and re-layouts  6.3 us (5%)
  other arithmetic  6.24 us (5%)
    all_to_all x1, blocking collectives, per_device(): lax.all_to_all(outgoing.reshape(group_width, capacity, LROWS, LAT), 'dev'...  42.4 us
    all_to_all x1, blocking collectives, per_device(): lax.all_to_all(forward.reshape(group_width, capacity, LROWS, LAT), 'dev',...  34.5 us
    ppermute x4, starting transfers between devices, shifted(): return lax.ppermute(x, AXES, perm)  10.5 us
    conv_general_dilated x2, matrix products, conv_local(): lax.conv_general_dilated(inputs, kernel, (1, stride, stride), ((2, 0), (1...  7.75 us
    ppermute x4, waiting for transfers between devices, shifted(): return lax.ppermute(x, AXES, perm)  7.06 us
    ppermute x2, starting transfers between devices, clip_totals(): partner = lax.ppermute(bundle, AXES, [(i, i ^ 1) for i in range(n)])  3.58 us
    another operation x5, other arithmetic, clip_totals(): mine = jnp.stack([to_left, to_right])  2.8 us
    unnamed x24, local copies, waits for them, and re-layouts  2.64 us
  transfers between devices with their start and end apart: 6, of which 4 were waited for; matrix products, arithmetic and copies ran while one was open for 1% of the time, Pallas kernels for 0%

profile of v9, /device:TPU:1, one launch (start us, length us, event | category | flops | bytes accessed | tf_op | source)
XLA Modules:
  0.0 122.3 jit_solution(17401105585150086176)
XLA Ops:
  0.0 1.4 %fusion.66 = (s32[1]{0:T(128)}, s32[1]{0:T(128)}) fusion(s32[48]{0:T(128)} %param.13), kind=kLoop, calls=%fused_computation.117 | loop fusion | bytes 16 | tf_op jit(solution)/shard_map/slice | solution.py:52
  1.4 0.7 convert_element_type.47
  2.0 0.9 copy.52
  2.9 0.0 copy-start.2
  2.9 0.1 reshape.62
  3.0 0.0 copy-start.6
  3.0 0.0 copy-start.9
  3.0 0.0 copy-start.7
  3.1 0.0 copy-start.8
  3.1 3.3 %convert_reduce_fusion = (f32[48,128]{1,0:T(8,128)S(1)}, f32[48,128]{1,0:T(8,128)S(1)}, bf16[48,2,8,8,128]{4,0,3,2,1:T(8,128)(2,1)}) fusion(bf16[48,2,8,8,3]{0,4,3,2,1:T(4,128)(2,1)S(1)} %reshape.62, bf16[3,3,3,3,128]{4,3,2,1,0:T(4,128)(2,1)} %param.16), kind=kOutput, calls=%fused_computation.4 | convolution fusion | flops 57446400 | bytes 1679616 | tf_op jit(solution)/shard_map/conv_general_dilated | solution.py:23
  6.4 0.1 copy.53
  6.5 0.1 copy.54
  6.7 0.6 fusion.65
  7.3 1.3 %broadcast_compare_fusion = (pred[48]{0:T(512)(128)(4,1)S(1)}, pred[48]{0:T(512)(128)(4,1)S(1)}) fusion(s32[48]{0:T(128)S(1)} %copy-done.2, s32[]{:T(128)} %bitcast.4, s32[]{:T(128)} %bitcast.2), kind=kLoop, calls=%fused_computation.111 | loop fusion | flops 96 | bytes 296 | tf_op jit(solution)/shard_map/eq | solution.py:52
  8.6 0.1 pad.33.clone
  8.7 0.2 select_reduce_fusion.3
  8.8 1.4 %maximum_bitcast_fusion = (f32[1,66]{1,0:T(1,128)S(1)}, f32[1,66]{1,0:T(1,128)S(1)}) fusion(f32[65]{0:T(128)S(1)} %get-tuple-element.15, f32[1]{0:T(128)} %get-tuple-element.25, f32[65]{0:T(128)S(1)} %get-tuple-element.16, f32[1]{0:T(128)} %get-tuple-element.26), kind=kLoop, calls=%fused_computation.105 | loop fusion | flops 132 | bytes 1056 | tf_op jit(solution)/shard_map/stack | solution.py:55
  10.2 4.4 %collective-permute-start = (f32[2,66]{1,0:T(2,128)S(1)}, f32[2,66]{1,0:T(2,128)S(1)}, u32[]{:S(2)}, u32[]{:S(2)}) collective-permute-start(f32[2,66]{1,0:T(2,128)S(1)} %pad_maximum_fusion.4), channel_id=1, source_target_pairs={{0,2},{1,3},{2,4},{3,5},{4,6},{5,7},{6,8},{7,9},{8,10},{9,11},{10,... | collective-permute-start | bytes 1592 | tf_op jit(solution)/shard_map/ppermute | solution.py:45
  14.6 1.3 %collective-permute-start.1 = (f32[2,66]{1,0:T(2,128)S(1)}, f32[2,66]{1,0:T(2,128)S(1)}, u32[]{:S(2)}, u32[]{:S(2)}) collective-permute-start(f32[2,66]{1,0:T(2,128)S(1)} %pad_maximum_fusion.4), channel_id=1, source_target_pairs={{2,0},{3,1},{4,2},{5,3},{6,4},{7,5},{8,6},{9,7},{10,8},{11,9},{12,... | collective-permute-start | bytes 1592 | tf_op jit(solution)/shard_map/ppermute | solution.py:45
  15.9 0.2 fusion.37
  16.1 0.2 convert_reduce_fusion.2
  16.3 0.0 collective-permute-done
  16.3 2.8 %collective-permute-done.1 = f32[2,66]{1,0:T(2,128)S(1)} collective-permute-done((f32[2,66]{1,0:T(2,128)S(1)}, f32[2,66]{1,0:T(2,128)S(1)}, u32[]{:S(2)}, u32[]{:S(2)}) %collective-permute-start.1) | collective-permute-done | bytes 560 | tf_op jit(solution)/shard_map/ppermute | solution.py:45
  19.1 2.0 %collective-permute-start.2 = (f32[6,66]{1,0:T(8,128)S(1)}, f32[6,66]{1,0:T(8,128)S(1)}, u32[]{:S(2)}, u32[]{:S(2)}) collective-permute-start(f32[6,66]{1,0:T(8,128)S(1)} %pad_maximum_fusion), channel_id=1, source_target_pairs={{0,1},{1,0},{2,3},{3,2},{4,5},{5,4},{6,7},{7,6},{8,9},{9,8},{10,11... | collective-permute-start | bytes 4760 | tf_op jit(solution)/shard_map/ppermute | solution.py:59
  21.1 0.2 convert_reduce_fusion.3
  21.3 0.6 collective-permute-done.2
  21.9 0.1 slice_reduce_fusion.1
  22.1 0.3 convolution_add_fusion.2
  22.4 0.1 copy.57
  22.5 0.1 copy.58
  22.6 0.0 copy-done.7
  22.6 0.0 copy-start.3
  22.6 0.0 copy-start.4
  22.6 4.4 %convert_reduce_fusion.1 = (f32[48,256]{1,0:T(8,128)S(1)}, f32[48,256]{1,0:T(8,128)S(1)}, bf16[48,2,4,4,256]{4,0,3,2,1:T(8,128)(2,1)S(1)}) fusion(bf16[3,3,3,128,256]{4,3,2,1,0:T(8,128)(2,1)S(1)} %copy-done, bf16[48,2,8,8,128]{4,0,3,2,1:T(8,128)(2,1)} %get-tuple-element.31, f32[128]{0:T(128)S(1)} %copy-done.7, f32[128]{0:T(128)S(1)} %copy-done.8, ...), kind=kOutput, calls=%fused_computation.19 | convolution fusion | flops 1151705088 | bytes 4277248 | tf_op jit(solution)/shard_map/conv_general_dilated | solution.py:23
  27.0 0.1 copy.60
  27.2 0.1 copy.59
  27.3 0.2 select_reduce_fusion.1
  27.5 0.7 maximum_bitcast_fusion.2
  28.2 0.7 maximum_bitcast_fusion.3
  29.0 3.5 %collective-permute-start.3 = (f32[2,66]{1,0:T(2,128)S(1)}, f32[2,66]{1,0:T(2,128)S(1)}, u32[]{:S(2)}, u32[]{:S(2)}) collective-permute-start(f32[2,66]{1,0:T(2,128)S(1)} %pad_maximum_fusion.5), channel_id=1, source_target_pairs={{0,2},{1,3},{2,4},{3,5},{4,6},{5,7},{6,8},{7,9},{8,10},{9,11},{10,... | collective-permute-start | bytes 1592 | tf_op jit(solution)/shard_map/ppermute | solution.py:45
  32.5 1.3 %collective-permute-start.4 = (f32[2,66]{1,0:T(2,128)S(1)}, f32[2,66]{1,0:T(2,128)S(1)}, u32[]{:S(2)}, u32[]{:S(2)}) collective-permute-start(f32[2,66]{1,0:T(2,128)S(1)} %pad_maximum_fusion.5), channel_id=1, source_target_pairs={{2,0},{3,1},{4,2},{5,3},{6,4},{7,5},{8,6},{9,7},{10,8},{11,9},{12,... | collective-permute-start | bytes 1592 | tf_op jit(solution)/shard_map/ppermute | solution.py:45
  33.8 0.0 collective-permute-done.3
  33.8 4.3 %collective-permute-done.4 = f32[2,66]{1,0:T(2,128)S(1)} collective-permute-done((f32[2,66]{1,0:T(2,128)S(1)}, f32[2,66]{1,0:T(2,128)S(1)}, u32[]{:S(2)}, u32[]{:S(2)}) %collective-permute-start.4) | collective-permute-done | bytes 560 | tf_op jit(solution)/shard_map/ppermute | solution.py:45
  38.1 1.6 %collective-permute-start.5 = (f32[6,66]{1,0:T(8,128)S(1)}, f32[6,66]{1,0:T(8,128)S(1)}, u32[]{:S(2)}, u32[]{:S(2)}) collective-permute-start(f32[6,66]{1,0:T(8,128)S(1)} %pad_maximum_fusion.1), channel_id=1, source_target_pairs={{0,1},{1,0},{2,3},{3,2},{4,5},{5,4},{6,7},{7,6},{8,9},{9,8},{10,11... | collective-permute-start | bytes 4760 | tf_op jit(solution)/shard_map/ppermute | solution.py:59
  39.7 0.2 fusion.35
  40.0 0.6 collective-permute-done.5
  40.6 0.1 slice_reduce_fusion
  40.7 0.3 convolution_add_fusion.1
  41.0 0.1 copy.63
  41.1 0.1 copy.64
  41.2 0.5 fusion.20
  41.8 0.0 copy-start.1
  41.8 0.0 copy-start.5
  41.8 0.4 copy.65
  42.2 0.2 reshape.63
  42.4 0.2 copy-done.1
  42.6 0.4 fusion.10
  43.0 0.4 fusion.26
  43.4 0.2 copy.71
  43.7 42.4 %all_to_all.10 = bf16[64,2,32,128]{3,2,1,0:T(8,128)(2,1)S(1)} all-to-all(bf16[64,2,32,128]{3,2,1,0:T(8,128)(2,1)S(1)} %bitcast.58), channel_id=1, replica_groups=mesh['slab'=4,'dev'=64] {'dev'}, dimensions={0} | all-to-all | bytes 2097152 | tf_op jit(solution)/shard_map/all_to_all | solution.py:168
  86.1 0.5 fusion.27
  86.6 0.2 copy.73
  86.8 34.5 %all_to_all.11 = bf16[64,2,32,128]{3,2,1,0:T(8,128)(2,1)S(1)} all-to-all(bf16[64,2,32,128]{3,2,1,0:T(8,128)(2,1)S(1)} %bitcast.59), channel_id=1, replica_groups=mesh['slab'=4,'dev'=64] {'dev'}, dimensions={0} | all-to-all | bytes 2097152 | tf_op jit(solution)/shard_map/all_to_all | solution.py:176
  121.4 1.0 copy.83
  (35 shorter events, 0.4 us)
Async XLA Ops:
  0.0 22.6 %copy-start = (bf16[3,3,3,128,256]{4,3,2,1,0:T(8,128)(2,1)S(1)}, bf16[3,3,3,128,256]{4,3,2,1,0:T(8,128)(2,1)}, u32[]{:S(2)}) copy-start(bf16[3,3,3,128,256]{4,3,2,1,0:T(8,128)(2,1)} %param.19) | copy-start | bytes 5308420
  2.9 4.4 %copy-start.2 = (s32[48]{0:T(128)S(1)}, s32[48]{0:T(128)}, u32[]{:S(2)}) copy-start(s32[48]{0:T(128)} %param.13) | copy-start | bytes 580
  3.0 13.1 %copy-start.6 = (s32[128,1]{0,1:T(1,128)S(1)}, s32[128,1]{0,1:T(1,128)}, u32[]{:S(2)}) copy-start(s32[128,1]{0,1:T(1,128)} %param.15) | copy-start | bytes 1540
  3.0 18.1 %copy-start.9 = (s32[48,1]{0,1:T(1,128)S(1)}, s32[48,1]{0,1:T(1,128)}, u32[]{:S(2)}) copy-start(s32[48,1]{0,1:T(1,128)} %param.14) | copy-start | bytes 580
  3.0 19.6 %copy-start.7 = (f32[128]{0:T(128)S(1)}, f32[128]{0:T(128)}, u32[]{:S(2)}) copy-start(f32[128]{0:T(128)} %param.18) | copy-start | bytes 1540
  3.1 19.6 %copy-start.8 = (f32[128]{0:T(128)S(1)}, f32[128]{0:T(128)}, u32[]{:S(2)}) copy-start(f32[128]{0:T(128)} %param.17) | copy-start | bytes 1540
  10.2 6.1 %collective-permute-start = (f32[2,66]{1,0:T(2,128)S(1)}, f32[2,66]{1,0:T(2,128)S(1)}, u32[]{:S(2)}, u32[]{:S(2)}) collective-permute-start(f32[2,66]{1,0:T(2,128)S(1)} %pad_maximum_fusion.4), channel_id=1, source_target_pairs={{0,2},{1,3},{2,4},{3,5},{4,6},{5,7},{6,8},{7,9},{8,10},{9,11},{10,... | collective-permute-start | bytes 1592 | tf_op jit(solution)/shard_map/ppermute | solution.py:45
  14.6 4.5 %collective-permute-start.1 = (f32[2,66]{1,0:T(2,128)S(1)}, f32[2,66]{1,0:T(2,128)S(1)}, u32[]{:S(2)}, u32[]{:S(2)}) collective-permute-start(f32[2,66]{1,0:T(2,128)S(1)} %pad_maximum_fusion.4), channel_id=1, source_target_pairs={{2,0},{3,1},{4,2},{5,3},{6,4},{7,5},{8,6},{9,7},{10,8},{11,9},{12,... | collective-permute-start | bytes 1592 | tf_op jit(solution)/shard_map/ppermute | solution.py:45
  19.1 2.8 %collective-permute-start.2 = (f32[6,66]{1,0:T(8,128)S(1)}, f32[6,66]{1,0:T(8,128)S(1)}, u32[]{:S(2)}, u32[]{:S(2)}) collective-permute-start(f32[6,66]{1,0:T(8,128)S(1)} %pad_maximum_fusion), channel_id=1, source_target_pairs={{0,1},{1,0},{2,3},{3,2},{4,5},{5,4},{6,7},{7,6},{8,9},{9,8},{10,11... | collective-permute-start | bytes 4760 | tf_op jit(solution)/shard_map/ppermute | solution.py:59
  22.6 18.6 %copy-start.3 = (f32[256]{0:T(256)S(1)}, f32[256]{0:T(256)}, u32[]{:S(2)}) copy-start(f32[256]{0:T(256)} %param.21) | copy-start | bytes 3076
  22.6 18.6 %copy-start.4 = (f32[256]{0:T(256)S(1)}, f32[256]{0:T(256)}, u32[]{:S(2)}) copy-start(f32[256]{0:T(256)} %param.20) | copy-start | bytes 3076
  29.0 4.9 %collective-permute-start.3 = (f32[2,66]{1,0:T(2,128)S(1)}, f32[2,66]{1,0:T(2,128)S(1)}, u32[]{:S(2)}, u32[]{:S(2)}) collective-permute-start(f32[2,66]{1,0:T(2,128)S(1)} %pad_maximum_fusion.5), channel_id=1, source_target_pairs={{0,2},{1,3},{2,4},{3,5},{4,6},{5,7},{6,8},{7,9},{8,10},{9,11},{10,... | collective-permute-start | bytes 1592 | tf_op jit(solution)/shard_map/ppermute | solution.py:45
  32.5 5.6 %collective-permute-start.4 = (f32[2,66]{1,0:T(2,128)S(1)}, f32[2,66]{1,0:T(2,128)S(1)}, u32[]{:S(2)}, u32[]{:S(2)}) collective-permute-start(f32[2,66]{1,0:T(2,128)S(1)} %pad_maximum_fusion.5), channel_id=1, source_target_pairs={{2,0},{3,1},{4,2},{5,3},{6,4},{7,5},{8,6},{9,7},{10,8},{11,9},{12,... | collective-permute-start | bytes 1592 | tf_op jit(solution)/shard_map/ppermute | solution.py:45
  38.1 2.4 %collective-permute-start.5 = (f32[6,66]{1,0:T(8,128)S(1)}, f32[6,66]{1,0:T(8,128)S(1)}, u32[]{:S(2)}, u32[]{:S(2)}) collective-permute-start(f32[6,66]{1,0:T(8,128)S(1)} %pad_maximum_fusion.1), channel_id=1, source_target_pairs={{0,1},{1,0},{2,3},{3,2},{4,5},{5,4},{6,7},{7,6},{8,9},{9,8},{10,11... | collective-permute-start | bytes 4760 | tf_op jit(solution)/shard_map/ppermute | solution.py:59
  41.8 0.8 copy-start.1
  41.8 0.8 copy-start.5

commit v10 on v8

--- a/solution.py
+++ b/solution.py
@@ -53,14 +53,15 @@
     to_right = jnp.concatenate([clip_f[-1:], own[-1]])
     to_left = jnp.concatenate([clip_f[:1], own[0]])
     mine = jnp.stack([to_left, to_right])
+    odd = (lax.axis_index(AXES) % 2) == 1
+    partner = lax.ppermute(mine, AXES, [(i, i ^ 1) for i in range(n)])
+    cross_pairs = [(i, i + 1) for i in range(1, n - 1, 2)] + [(i, i - 1) for i in range(2, n, 2)]
+    across = lax.ppermute(mine, AXES, cross_pairs)
     from_left = shifted(mine, 2, n)
     from_right = shifted(mine, -2, n)
-    bundle = jnp.concatenate([mine, from_left, from_right])
-    partner = lax.ppermute(bundle, AXES, [(i, i ^ 1) for i in range(n)])
-    odd = (lax.axis_index(AXES) % 2) == 1
-    left_near = jnp.where(odd, partner[1], partner[3])
+    left_near = jnp.where(odd, partner[1], across[1])
     left_far = from_left[1]
-    right_near = jnp.where(odd, partner[4], partner[0])
+    right_near = jnp.where(odd, across[0], partner[0])
     right_far = from_right[0]
     received = jnp.stack([left_near, left_far, right_near, right_far])
     match = (clip_f[:, None] == received[None, :, 0]).astype(jnp.float32)

time: 120 us -> 134 us (1.12)
  blocking collectives: 76.9 us -> 87.4 us
  starting transfers between devices: 14.1 us -> 19.7 us
  waiting for transfers between devices: 8.56 us -> 6.62 us
    all_to_all x1, blocking collectives: 42.4 us -> 52.8 us  [per_device(): lax.all_to_all(outgoing.reshape(group_width, capacity, LROWS, LAT), 'dev'...]
    ppermute x2 -> x4, starting transfers between devices: 3.58 us -> 10.4 us  [the longest x2 5.42 us: clip_totals(): across = lax.ppermute(mine, AXES, cross_pairs)]
    ppermute x2 -> x4, waiting for transfers between devices: 1.41 us -> 0.01 us  [the longest x2 0.01 us: clip_totals(): partner = lax.ppermute(mine, AXES, [(i, i ^ 1) for i in range(n)])]
  transfers between devices with their start and end apart: 6 -> 8, of which waited for: 4 -> 2; matrix products, arithmetic and copies ran while one was open for 0% -> 0% of each run, Pallas kernels for 0% -> 0%
where the time goes in v10:
time: 134 us; the launch traced here: 133 us
  blocking collectives  87.4 us (65%)
  starting transfers between devices  19.7 us (15%)
  matrix products  10 us (7%)
  waiting for transfers between devices  6.62 us (5%)
  local copies, waits for them, and re-layouts  5.27 us (4%)
  other arithmetic  3.9 us (3%)
    all_to_all x1, blocking collectives, per_device(): lax.all_to_all(outgoing.reshape(group_width, capacity, LROWS, LAT), 'dev'...  52.8 us
    all_to_all x1, blocking collectives, per_device(): lax.all_to_all(forward.reshape(group_width, capacity, LROWS, LAT), 'dev',...  34.5 us
    ppermute x4, starting transfers between devices, shifted(): return lax.ppermute(x, AXES, perm)  9.31 us
    conv_general_dilated x2, matrix products, conv_local(): lax.conv_general_dilated(inputs, kernel, (1, stride, stride), ((2, 0), (1...  7.72 us
    ppermute x4, waiting for transfers between devices, shifted(): return lax.ppermute(x, AXES, perm)  6.61 us
    ppermute x2, starting transfers between devices, clip_totals(): across = lax.ppermute(mine, AXES, cross_pairs)  5.42 us
    ppermute x2, starting transfers between devices, clip_totals(): partner = lax.ppermute(mine, AXES, [(i, i ^ 1) for i in range(n)])  4.98 us
    unnamed x24, local copies, waits for them, and re-layouts  2.78 us
  transfers between devices with their start and end apart: 8, of which 2 were waited for; matrix products, arithmetic and copies ran while one was open for 0% of the time, Pallas kernels for 0%

profile of v10, /device:TPU:1, one launch (start us, length us, event | category | flops | bytes accessed | tf_op | source)
XLA Modules:
  0.0 133.4 jit_solution(11768738835759602056)
XLA Ops:
  0.0 1.0 copy.52
  1.0 0.0 copy-start.5
  1.0 0.0 copy-start.9
  1.1 0.1 reshape.60
  1.1 0.0 copy-start.6
  1.1 0.0 copy-start.7
  1.2 3.3 %convert_reduce_fusion = (f32[48,128]{1,0:T(8,128)S(1)}, f32[48,128]{1,0:T(8,128)S(1)}, bf16[48,2,8,8,128]{4,0,3,2,1:T(8,128)(2,1)}) fusion(bf16[48,2,8,8,3]{0,4,3,2,1:T(4,128)(2,1)S(1)} %reshape.60, bf16[3,3,3,3,128]{4,3,2,1,0:T(4,128)(2,1)} %param.16), kind=kOutput, calls=%fused_computation.4 | convolution fusion | flops 57446400 | bytes 1679616 | tf_op jit(solution)/shard_map/conv_general_dilated | solution.py:23
  4.5 0.1 copy.53
  4.6 0.1 copy.54
  4.8 0.1 pad.25.clone
  4.9 0.2 fusion.33
  5.1 0.6 fusion.73
  5.7 1.3 maximum_bitcast_fusion
  7.1 3.3 %collective-permute-start = (f32[2,66]{1,0:T(2,128)S(1)}, f32[2,66]{1,0:T(2,128)S(1)}, u32[]{:S(2)}, u32[]{:S(2)}) collective-permute-start(f32[2,66]{1,0:T(2,128)S(1)} %pad_maximum_fusion.2), channel_id=1, source_target_pairs={{0,1},{1,0},{2,3},{3,2},{4,5},{5,4},{6,7},{7,6},{8,9},{9,8},{10,11... | collective-permute-start | bytes 1592 | tf_op jit(solution)/shard_map/ppermute | solution.py:57
  10.4 1.9 %collective-permute-start.1 = (f32[2,66]{1,0:T(2,128)S(1)}, f32[2,66]{1,0:T(2,128)S(1)}, u32[]{:S(2)}, u32[]{:S(2)}) collective-permute-start(f32[2,66]{1,0:T(2,128)S(1)} %pad_maximum_fusion.2), channel_id=1, source_target_pairs={{1,2},{3,4},{5,6},{7,8},{9,10},{11,12},{13,14},{15,16},{17,18},{19... | collective-permute-start | bytes 1592 | tf_op jit(solution)/shard_map/ppermute | solution.py:59
  12.3 3.4 %collective-permute-start.2 = (f32[2,66]{1,0:T(2,128)S(1)}, f32[2,66]{1,0:T(2,128)S(1)}, u32[]{:S(2)}, u32[]{:S(2)}) collective-permute-start(f32[2,66]{1,0:T(2,128)S(1)} %pad_maximum_fusion.2), channel_id=1, source_target_pairs={{0,2},{1,3},{2,4},{3,5},{4,6},{5,7},{6,8},{7,9},{8,10},{9,11},{10,... | collective-permute-start | bytes 1592 | tf_op jit(solution)/shard_map/ppermute | solution.py:45
  15.7 1.3 collective-permute-start.3
  17.0 0.2 convert_reduce_fusion.2
  17.2 0.2 convert_reduce_fusion.3
  17.3 0.1 copy.55
  17.4 0.0 collective-permute-done.2
  17.5 2.7 %collective-permute-done.3 = f32[2,66]{1,0:T(2,128)S(1)} collective-permute-done((f32[2,66]{1,0:T(2,128)S(1)}, f32[2,66]{1,0:T(2,128)S(1)}, u32[]{:S(2)}, u32[]{:S(2)}) %collective-permute-start.3) | collective-permute-done | bytes 560 | tf_op jit(solution)/shard_map/ppermute | solution.py:45
  20.2 0.0 collective-permute-done
  20.2 0.0 collective-permute-done.1
  20.2 0.1 slice_reduce_fusion.1
  20.3 0.3 convolution_add_fusion.2
  20.7 0.1 copy.57
  20.8 0.1 copy.58
  20.8 0.0 copy-done.6
  20.9 0.0 copy-start.2
  20.9 0.0 copy-start.3
  20.9 4.4 %convert_reduce_fusion.1 = (f32[48,256]{1,0:T(8,128)S(1)}, f32[48,256]{1,0:T(8,128)S(1)}, bf16[48,2,4,4,256]{4,0,3,2,1:T(8,128)(2,1)S(1)}) fusion(bf16[3,3,3,128,256]{4,3,2,1,0:T(8,128)(2,1)S(1)} %copy-done, bf16[48,2,8,8,128]{4,0,3,2,1:T(8,128)(2,1)} %get-tuple-element.27, f32[128]{0:T(128)S(1)} %copy-done.6, f32[128]{0:T(128)S(1)} %copy-done.7, ...), kind=kOutput, calls=%fused_computation.19 | convolution fusion | flops 1151705088 | bytes 4277248 | tf_op jit(solution)/shard_map/conv_general_dilated | solution.py:23
  25.3 0.1 copy.60
  25.5 0.1 copy.59
  25.6 0.2 fusion.38
  25.8 0.7 maximum_bitcast_fusion.2
  26.6 0.7 maximum_bitcast_fusion.3
  27.3 1.7 %collective-permute-start.4 = (f32[2,66]{1,0:T(2,128)S(1)}, f32[2,66]{1,0:T(2,128)S(1)}, u32[]{:S(2)}, u32[]{:S(2)}) collective-permute-start(f32[2,66]{1,0:T(2,128)S(1)} %pad_maximum_fusion.3), channel_id=1, source_target_pairs={{0,1},{1,0},{2,3},{3,2},{4,5},{5,4},{6,7},{7,6},{8,9},{9,8},{10,11... | collective-permute-start | bytes 1592 | tf_op jit(solution)/shard_map/ppermute | solution.py:57
  28.9 3.5 %collective-permute-start.5 = (f32[2,66]{1,0:T(2,128)S(1)}, f32[2,66]{1,0:T(2,128)S(1)}, u32[]{:S(2)}, u32[]{:S(2)}) collective-permute-start(f32[2,66]{1,0:T(2,128)S(1)} %pad_maximum_fusion.3), channel_id=1, source_target_pairs={{1,2},{3,4},{5,6},{7,8},{9,10},{11,12},{13,14},{15,16},{17,18},{19... | collective-permute-start | bytes 1592 | tf_op jit(solution)/shard_map/ppermute | solution.py:59
  32.5 3.4 %collective-permute-start.6 = (f32[2,66]{1,0:T(2,128)S(1)}, f32[2,66]{1,0:T(2,128)S(1)}, u32[]{:S(2)}, u32[]{:S(2)}) collective-permute-start(f32[2,66]{1,0:T(2,128)S(1)} %pad_maximum_fusion.3), channel_id=1, source_target_pairs={{0,2},{1,3},{2,4},{3,5},{4,6},{5,7},{6,8},{7,9},{8,10},{9,11},{10,... | collective-permute-start | bytes 1592 | tf_op jit(solution)/shard_map/ppermute | solution.py:45
  35.8 1.3 collective-permute-start.7
  37.1 0.1 copy.61
  37.2 0.0 collective-permute-done.6
  37.3 3.9 %collective-permute-done.7 = f32[2,66]{1,0:T(2,128)S(1)} collective-permute-done((f32[2,66]{1,0:T(2,128)S(1)}, f32[2,66]{1,0:T(2,128)S(1)}, u32[]{:S(2)}, u32[]{:S(2)}) %collective-permute-start.7) | collective-permute-done | bytes 560 | tf_op jit(solution)/shard_map/ppermute | solution.py:45
  41.2 0.0 collective-permute-done.4
  41.2 0.1 slice_reduce_fusion
  41.3 0.3 convolution_add_fusion.1
  41.7 0.1 copy.63
  41.8 0.1 copy.64
  41.9 0.0 copy-done.2
  41.9 0.6 fusion.20
  42.4 0.0 copy-start.1
  42.5 0.0 copy-start.4
  42.5 0.4 copy.65
  42.9 0.2 reshape.61
  43.1 0.2 copy-done.1
  43.3 0.4 fusion.10
  43.7 0.4 fusion.26
  44.1 0.2 copy.69
  44.3 52.8 %all_to_all.10 = bf16[64,2,32,128]{3,2,1,0:T(8,128)(2,1)S(1)} all-to-all(bf16[64,2,32,128]{3,2,1,0:T(8,128)(2,1)S(1)} %bitcast.64), channel_id=1, replica_groups=mesh['slab'=4,'dev'=64] {'dev'}, dimensions={0} | all-to-all | bytes 2097152 | tf_op jit(solution)/shard_map/all_to_all | solution.py:167
  97.2 0.5 fusion.27
  97.7 0.2 copy.71
  97.9 34.5 %all_to_all.11 = bf16[64,2,32,128]{3,2,1,0:T(8,128)(2,1)S(1)} all-to-all(bf16[64,2,32,128]{3,2,1,0:T(8,128)(2,1)S(1)} %bitcast.65), channel_id=1, replica_groups=mesh['slab'=4,'dev'=64] {'dev'}, dimensions={0} | all-to-all | bytes 2097152 | tf_op jit(solution)/shard_map/all_to_all | solution.py:175
  132.4 1.0 copy.81
  (37 shorter events, 0.4 us)
Async XLA Ops:
  0.0 20.8 %copy-start = (bf16[3,3,3,128,256]{4,3,2,1,0:T(8,128)(2,1)S(1)}, bf16[3,3,3,128,256]{4,3,2,1,0:T(8,128)(2,1)}, u32[]{:S(2)}) copy-start(bf16[3,3,3,128,256]{4,3,2,1,0:T(8,128)(2,1)} %param.19) | copy-start | bytes 5308420
  0.0 4.8 %copy-start.8 = (s32[48]{0:T(128)S(1)}, s32[48]{0:T(128)}, u32[]{:S(2)}) copy-start(s32[48]{0:T(128)} %param.13) | copy-start | bytes 580
  1.0 15.9 %copy-start.5 = (s32[128,1]{0,1:T(1,128)S(1)}, s32[128,1]{0,1:T(1,128)}, u32[]{:S(2)}) copy-start(s32[128,1]{0,1:T(1,128)} %param.15) | copy-start | bytes 1540
  1.0 16.1 %copy-start.9 = (s32[48,1]{0,1:T(1,128)S(1)}, s32[48,1]{0,1:T(1,128)}, u32[]{:S(2)}) copy-start(s32[48,1]{0,1:T(1,128)} %param.14) | copy-start | bytes 580
  1.1 19.7 %copy-start.6 = (f32[128]{0:T(128)S(1)}, f32[128]{0:T(128)}, u32[]{:S(2)}) copy-start(f32[128]{0:T(128)} %param.18) | copy-start | bytes 1540
  1.1 19.7 %copy-start.7 = (f32[128]{0:T(128)S(1)}, f32[128]{0:T(128)}, u32[]{:S(2)}) copy-start(f32[128]{0:T(128)} %param.17) | copy-start | bytes 1540
  7.1 13.1 %collective-permute-start = (f32[2,66]{1,0:T(2,128)S(1)}, f32[2,66]{1,0:T(2,128)S(1)}, u32[]{:S(2)}, u32[]{:S(2)}) collective-permute-start(f32[2,66]{1,0:T(2,128)S(1)} %pad_maximum_fusion.2), channel_id=1, source_target_pairs={{0,1},{1,0},{2,3},{3,2},{4,5},{5,4},{6,7},{7,6},{8,9},{9,8},{10,11... | collective-permute-start | bytes 1592 | tf_op jit(solution)/shard_map/ppermute | solution.py:57
  10.4 9.8 %collective-permute-start.1 = (f32[2,66]{1,0:T(2,128)S(1)}, f32[2,66]{1,0:T(2,128)S(1)}, u32[]{:S(2)}, u32[]{:S(2)}) collective-permute-start(f32[2,66]{1,0:T(2,128)S(1)} %pad_maximum_fusion.2), channel_id=1, source_target_pairs={{1,2},{3,4},{5,6},{7,8},{9,10},{11,12},{13,14},{15,16},{17,18},{19... | collective-permute-start | bytes 1592 | tf_op jit(solution)/shard_map/ppermute | solution.py:59
  12.3 5.2 %collective-permute-start.2 = (f32[2,66]{1,0:T(2,128)S(1)}, f32[2,66]{1,0:T(2,128)S(1)}, u32[]{:S(2)}, u32[]{:S(2)}) collective-permute-start(f32[2,66]{1,0:T(2,128)S(1)} %pad_maximum_fusion.2), channel_id=1, source_target_pairs={{0,2},{1,3},{2,4},{3,5},{4,6},{5,7},{6,8},{7,9},{8,10},{9,11},{10,... | collective-permute-start | bytes 1592 | tf_op jit(solution)/shard_map/ppermute | solution.py:45
  15.7 4.5 %collective-permute-start.3 = (f32[2,66]{1,0:T(2,128)S(1)}, f32[2,66]{1,0:T(2,128)S(1)}, u32[]{:S(2)}, u32[]{:S(2)}) collective-permute-start(f32[2,66]{1,0:T(2,128)S(1)} %pad_maximum_fusion.2), channel_id=1, source_target_pairs={{2,0},{3,1},{4,2},{5,3},{6,4},{7,5},{8,6},{9,7},{10,8},{11,9},{12,... | collective-permute-start | bytes 1592 | tf_op jit(solution)/shard_map/ppermute | solution.py:45
  20.9 21.0 %copy-start.2 = (f32[256]{0:T(256)S(1)}, f32[256]{0:T(256)}, u32[]{:S(2)}) copy-start(f32[256]{0:T(256)} %param.21) | copy-start | bytes 3076
  20.9 21.0 %copy-start.3 = (f32[256]{0:T(256)S(1)}, f32[256]{0:T(256)}, u32[]{:S(2)}) copy-start(f32[256]{0:T(256)} %param.20) | copy-start | bytes 3076
  27.3 13.9 %collective-permute-start.4 = (f32[2,66]{1,0:T(2,128)S(1)}, f32[2,66]{1,0:T(2,128)S(1)}, u32[]{:S(2)}, u32[]{:S(2)}) collective-permute-start(f32[2,66]{1,0:T(2,128)S(1)} %pad_maximum_fusion.3), channel_id=1, source_target_pairs={{0,1},{1,0},{2,3},{3,2},{4,5},{5,4},{6,7},{7,6},{8,9},{9,8},{10,11... | collective-permute-start | bytes 1592 | tf_op jit(solution)/shard_map/ppermute | solution.py:57
  28.9 12.2 %collective-permute-start.5 = (f32[2,66]{1,0:T(2,128)S(1)}, f32[2,66]{1,0:T(2,128)S(1)}, u32[]{:S(2)}, u32[]{:S(2)}) collective-permute-start(f32[2,66]{1,0:T(2,128)S(1)} %pad_maximum_fusion.3), channel_id=1, source_target_pairs={{1,2},{3,4},{5,6},{7,8},{9,10},{11,12},{13,14},{15,16},{17,18},{19... | collective-permute-start | bytes 1592 | tf_op jit(solution)/shard_map/ppermute | solution.py:59
  32.5 4.8 %collective-permute-start.6 = (f32[2,66]{1,0:T(2,128)S(1)}, f32[2,66]{1,0:T(2,128)S(1)}, u32[]{:S(2)}, u32[]{:S(2)}) collective-permute-start(f32[2,66]{1,0:T(2,128)S(1)} %pad_maximum_fusion.3), channel_id=1, source_target_pairs={{0,2},{1,3},{2,4},{3,5},{4,6},{5,7},{6,8},{7,9},{8,10},{9,11},{10,... | collective-permute-start | bytes 1592 | tf_op jit(solution)/shard_map/ppermute | solution.py:45
  35.8 5.3 %collective-permute-start.7 = (f32[2,66]{1,0:T(2,128)S(1)}, f32[2,66]{1,0:T(2,128)S(1)}, u32[]{:S(2)}, u32[]{:S(2)}) collective-permute-start(f32[2,66]{1,0:T(2,128)S(1)} %pad_maximum_fusion.3), channel_id=1, source_target_pairs={{2,0},{3,1},{4,2},{5,3},{6,4},{7,5},{8,6},{9,7},{10,8},{11,9},{12,... | collective-permute-start | bytes 1592 | tf_op jit(solution)/shard_map/ppermute | solution.py:45
  42.4 0.8 copy-start.1
  42.5 0.8 copy-start.4

commit v11 on v8

--- a/solution.py
+++ b/solution.py
@@ -67,8 +67,8 @@
     return own + jnp.dot(match, received[:, 1:], precision=precise)
 
 
-def finish_stats(totals, per_tile):
-    voxels = totals[:, -1:] * per_tile
+def finish_stats(totals, counts, per_tile):
+    voxels = counts * per_tile
     means = totals[:, :GROUPS] / voxels
     variance = totals[:, GROUPS : 2 * GROUPS] / voxels - means * means
     return (means, lax.rsqrt(variance + epsilon))
@@ -111,13 +111,14 @@
     hidden = conv_local(tiles, conv_first, 1).astype(jnp.bfloat16)
     sums, squares = group_sums(hidden.astype(jnp.float32))
     totals = clip_totals(clips, jnp.concatenate([sums, squares, ones], axis=1))
-    means, scales = finish_stats(totals, FR * HT * WT * (C1 // GROUPS))
+    counts = totals[:, -1:]
+    means, scales = finish_stats(totals, counts, FR * HT * WT * (C1 // GROUPS))
     active = normalize(hidden, means, scales, gain_first, bias_first)
 
     down = conv_local(active, conv_down, 2).astype(jnp.bfloat16)
     sums, squares = group_sums(down.astype(jnp.float32))
-    totals = clip_totals(clips, jnp.concatenate([sums, squares, ones], axis=1))
-    means, scales = finish_stats(totals, LROWS * (C2 // GROUPS))
+    totals = clip_totals(clips, jnp.concatenate([sums, squares], axis=1))
+    means, scales = finish_stats(totals, counts, LROWS * (C2 // GROUPS))
     active = normalize(down, means, scales, gain_second, bias_second)
 
     flat = active.reshape(-1, C2)

time: 120 us -> 120 us (level)
  no operation moved by 1% of the time
where the time goes in v11:
time: 120 us; the launch traced here: 119 us
  blocking collectives  76.9 us (64%)
  starting transfers between devices  14.1 us (12%)
  matrix products  10 us (8%)
  waiting for transfers between devices  8.57 us (7%)
  local copies, waits for them, and re-layouts  5.26 us (4%)
  other arithmetic  3.92 us (3%)
    all_to_all x1, blocking collectives, per_device(): lax.all_to_all(outgoing.reshape(group_width, capacity, LROWS, LAT), 'dev'...  42.4 us
    all_to_all x1, blocking collectives, per_device(): lax.all_to_all(forward.reshape(group_width, capacity, LROWS, LAT), 'dev',...  34.5 us
    ppermute x4, starting transfers between devices, shifted(): return lax.ppermute(x, AXES, perm)  10.5 us
    conv_general_dilated x2, matrix products, conv_local(): lax.conv_general_dilated(inputs, kernel, (1, stride, stride), ((2, 0), (1...  7.74 us
    ppermute x4, waiting for transfers between devices, shifted(): return lax.ppermute(x, AXES, perm)  7.14 us
    ppermute x2, starting transfers between devices, clip_totals(): partner = lax.ppermute(bundle, AXES, [(i, i ^ 1) for i in range(n)])  3.58 us
    unnamed x24, local copies, waits for them, and re-layouts  2.78 us
    another operation x5, other arithmetic, clip_totals(): mine = jnp.stack([to_left, to_right])  2.75 us
  transfers between devices with their start and end apart: 6, of which 4 were waited for; matrix products, arithmetic and copies ran while one was open for 0% of the time, Pallas kernels for 0%

profile of v11, /device:TPU:1, one launch (start us, length us, event | category | flops | bytes accessed | tf_op | source)
XLA Modules:
  0.0 119.2 jit_solution(8769864736718896322)
XLA Ops:
  0.0 0.0 copy-start
  0.0 1.0 copy.52
  1.0 0.0 copy-start.5
  1.0 0.1 reshape.60
  1.1 0.0 copy-start.6
  1.1 0.0 copy-start.7
  1.1 3.3 %convert_reduce_fusion = (f32[48,128]{1,0:T(8,128)S(1)}, f32[48,128]{1,0:T(8,128)S(1)}, bf16[48,2,8,8,128]{4,0,3,2,1:T(8,128)(2,1)}) fusion(bf16[48,2,8,8,3]{0,4,3,2,1:T(4,128)(2,1)S(1)} %reshape.60, bf16[3,3,3,3,128]{4,3,2,1,0:T(4,128)(2,1)} %param.16), kind=kOutput, calls=%fused_computation.4 | convolution fusion | flops 57446400 | bytes 1679616 | tf_op jit(solution)/shard_map/conv_general_dilated | solution.py:23
  4.5 0.1 copy.53
  4.6 0.1 copy.54
  4.8 0.0 copy-done.8
  4.8 0.1 pad.32.clone
  4.9 0.2 fusion.33
  5.1 0.6 fusion.69
  5.7 1.3 %maximum_bitcast_fusion = (f32[1,66]{1,0:T(1,128)S(1)}, f32[1,66]{1,0:T(1,128)S(1)}) fusion(f32[65]{0:T(128)S(1)} %get-tuple-element.21, f32[1]{0:T(128)} %get-tuple-element.27, f32[65]{0:T(128)S(1)} %get-tuple-element.22, f32[1]{0:T(128)} %get-tuple-element.28), kind=kLoop, calls=%fused_computation.105 | loop fusion | flops 132 | bytes 1056 | tf_op jit(solution)/shard_map/stack | solution.py:55
  7.1 4.4 %collective-permute-start = (f32[2,66]{1,0:T(2,128)S(1)}, f32[2,66]{1,0:T(2,128)S(1)}, u32[]{:S(2)}, u32[]{:S(2)}) collective-permute-start(f32[2,66]{1,0:T(2,128)S(1)} %pad_maximum_fusion.4), channel_id=1, source_target_pairs={{0,2},{1,3},{2,4},{3,5},{4,6},{5,7},{6,8},{7,9},{8,10},{9,11},{10,... | collective-permute-start | bytes 1592 | tf_op jit(solution)/shard_map/ppermute | solution.py:45
  11.4 1.3 %collective-permute-start.1 = (f32[2,66]{1,0:T(2,128)S(1)}, f32[2,66]{1,0:T(2,128)S(1)}, u32[]{:S(2)}, u32[]{:S(2)}) collective-permute-start(f32[2,66]{1,0:T(2,128)S(1)} %pad_maximum_fusion.4), channel_id=1, source_target_pairs={{2,0},{3,1},{4,2},{5,3},{6,4},{7,5},{8,6},{9,7},{10,8},{11,9},{12,... | collective-permute-start | bytes 1592 | tf_op jit(solution)/shard_map/ppermute | solution.py:45
  12.8 0.2 convert_reduce_fusion.2
  12.9 0.0 collective-permute-done
  12.9 3.0 %collective-permute-done.1 = f32[2,66]{1,0:T(2,128)S(1)} collective-permute-done((f32[2,66]{1,0:T(2,128)S(1)}, f32[2,66]{1,0:T(2,128)S(1)}, u32[]{:S(2)}, u32[]{:S(2)}) %collective-permute-start.1) | collective-permute-done | bytes 560 | tf_op jit(solution)/shard_map/ppermute | solution.py:45
  16.0 2.0 %collective-permute-start.2 = (f32[6,66]{1,0:T(8,128)S(1)}, f32[6,66]{1,0:T(8,128)S(1)}, u32[]{:S(2)}, u32[]{:S(2)}) collective-permute-start(f32[6,66]{1,0:T(8,128)S(1)} %pad_maximum_fusion), channel_id=1, source_target_pairs={{0,1},{1,0},{2,3},{3,2},{4,5},{5,4},{6,7},{7,6},{8,9},{9,8},{10,11... | collective-permute-start | bytes 4760 | tf_op jit(solution)/shard_map/ppermute | solution.py:59
  18.0 0.1 copy.55
  18.1 0.7 collective-permute-done.2
  18.8 0.1 slice_reduce_fusion.1
  18.9 0.3 convolution_add_fusion.1
  19.3 0.1 copy.57
  19.4 0.1 copy.58
  19.5 0.0 copy-done.6
  19.5 0.0 copy-done.7
  19.5 0.0 copy-start.9
  19.5 0.0 copy-start.2
  19.5 0.0 copy-start.3
  19.5 4.4 %convert_reduce_fusion.1 = (f32[48,256]{1,0:T(8,128)S(1)}, f32[48,256]{1,0:T(8,128)S(1)}, bf16[48,2,4,4,256]{4,0,3,2,1:T(8,128)(2,1)S(1)}) fusion(bf16[3,3,3,128,256]{4,3,2,1,0:T(8,128)(2,1)S(1)} %copy-done, bf16[48,2,8,8,128]{4,0,3,2,1:T(8,128)(2,1)} %get-tuple-element.29, f32[128]{0:T(128)S(1)} %copy-done.6, f32[128]{0:T(128)S(1)} %copy-done.7, ...), kind=kOutput, calls=%fused_computation.19 | convolution fusion | flops 1151705088 | bytes 4277248 | tf_op jit(solution)/shard_map/conv_general_dilated | solution.py:23
  23.9 0.1 copy.60
  24.1 0.1 copy.59
  24.2 0.2 fusion.38
  24.4 0.7 maximum_bitcast_fusion.2
  25.2 0.7 maximum_bitcast_fusion.3
  25.9 3.5 %collective-permute-start.3 = (f32[2,65]{1,0:T(2,128)S(1)}, f32[2,65]{1,0:T(2,128)S(1)}, u32[]{:S(2)}, u32[]{:S(2)}) collective-permute-start(f32[2,65]{1,0:T(2,128)S(1)} %pad_maximum_fusion.5), channel_id=1, source_target_pairs={{0,2},{1,3},{2,4},{3,5},{4,6},{5,7},{6,8},{7,9},{8,10},{9,11},{10,... | collective-permute-start | bytes 1568 | tf_op jit(solution)/shard_map/ppermute | solution.py:45
  29.4 1.3 %collective-permute-start.4 = (f32[2,65]{1,0:T(2,128)S(1)}, f32[2,65]{1,0:T(2,128)S(1)}, u32[]{:S(2)}, u32[]{:S(2)}) collective-permute-start(f32[2,65]{1,0:T(2,128)S(1)} %pad_maximum_fusion.5), channel_id=1, source_target_pairs={{2,0},{3,1},{4,2},{5,3},{6,4},{7,5},{8,6},{9,7},{10,8},{11,9},{12,... | collective-permute-start | bytes 1568 | tf_op jit(solution)/shard_map/ppermute | solution.py:45
  30.7 0.2 convert_reduce_fusion.3
  30.9 0.0 collective-permute-done.3
  30.9 4.1 %collective-permute-done.4 = f32[2,65]{1,0:T(2,128)S(1)} collective-permute-done((f32[2,65]{1,0:T(2,128)S(1)}, f32[2,65]{1,0:T(2,128)S(1)}, u32[]{:S(2)}, u32[]{:S(2)}) %collective-permute-start.4) | collective-permute-done | bytes 552 | tf_op jit(solution)/shard_map/ppermute | solution.py:45
  35.0 1.6 %collective-permute-start.5 = (f32[6,65]{1,0:T(8,128)S(1)}, f32[6,65]{1,0:T(8,128)S(1)}, u32[]{:S(2)}, u32[]{:S(2)}) collective-permute-start(f32[6,65]{1,0:T(8,128)S(1)} %pad_maximum_fusion.1), channel_id=1, source_target_pairs={{0,1},{1,0},{2,3},{3,2},{4,5},{5,4},{6,7},{7,6},{8,9},{9,8},{10,11... | collective-permute-start | bytes 4688 | tf_op jit(solution)/shard_map/ppermute | solution.py:59
  36.6 0.1 copy.61
  36.7 0.7 collective-permute-done.5
  37.5 0.1 slice_reduce_fusion
  37.6 0.3 convolution_add_fusion.2
  37.9 0.1 copy.63
  38.0 0.1 copy.64
  38.1 0.0 copy-done.2
  38.1 0.5 fusion.20
  38.6 0.0 copy-start.1
  38.7 0.0 copy-start.4
  38.7 0.4 copy.65
  39.1 0.2 reshape.61
  39.3 0.2 copy-done.1
  39.5 0.4 fusion.10
  39.9 0.4 fusion.26
  40.3 0.2 copy.69
  40.6 42.4 %all_to_all.10 = bf16[64,2,32,128]{3,2,1,0:T(8,128)(2,1)S(1)} all-to-all(bf16[64,2,32,128]{3,2,1,0:T(8,128)(2,1)S(1)} %bitcast.64), channel_id=1, replica_groups=mesh['slab'=4,'dev'=64] {'dev'}, dimensions={0} | all-to-all | bytes 2097152 | tf_op jit(solution)/shard_map/all_to_all | solution.py:167
  83.0 0.5 fusion.27
  83.5 0.2 copy.71
  83.7 34.5 %all_to_all.11 = bf16[64,2,32,128]{3,2,1,0:T(8,128)(2,1)S(1)} all-to-all(bf16[64,2,32,128]{3,2,1,0:T(8,128)(2,1)S(1)} %bitcast.65), channel_id=1, replica_groups=mesh['slab'=4,'dev'=64] {'dev'}, dimensions={0} | all-to-all | bytes 2097152 | tf_op jit(solution)/shard_map/all_to_all | solution.py:175
  118.2 1.0 copy.81
  (34 shorter events, 0.4 us)
Async XLA Ops:
  0.0 19.4 %copy-start = (bf16[3,3,3,128,256]{4,3,2,1,0:T(8,128)(2,1)S(1)}, bf16[3,3,3,128,256]{4,3,2,1,0:T(8,128)(2,1)}, u32[]{:S(2)}) copy-start(bf16[3,3,3,128,256]{4,3,2,1,0:T(8,128)(2,1)} %param.19) | copy-start | bytes 5308420
  0.0 4.8 %copy-start.8 = (s32[48]{0:T(128)S(1)}, s32[48]{0:T(128)}, u32[]{:S(2)}) copy-start(s32[48]{0:T(128)} %param.13) | copy-start | bytes 580
  1.0 11.7 %copy-start.5 = (s32[128,1]{0,1:T(1,128)S(1)}, s32[128,1]{0,1:T(1,128)}, u32[]{:S(2)}) copy-start(s32[128,1]{0,1:T(1,128)} %param.15) | copy-start | bytes 1540
  1.1 18.3 %copy-start.6 = (f32[128]{0:T(128)S(1)}, f32[128]{0:T(128)}, u32[]{:S(2)}) copy-start(f32[128]{0:T(128)} %param.18) | copy-start | bytes 1540
  1.1 18.3 %copy-start.7 = (f32[128]{0:T(128)S(1)}, f32[128]{0:T(128)}, u32[]{:S(2)}) copy-start(f32[128]{0:T(128)} %param.17) | copy-start | bytes 1540
  7.1 5.9 %collective-permute-start = (f32[2,66]{1,0:T(2,128)S(1)}, f32[2,66]{1,0:T(2,128)S(1)}, u32[]{:S(2)}, u32[]{:S(2)}) collective-permute-start(f32[2,66]{1,0:T(2,128)S(1)} %pad_maximum_fusion.4), channel_id=1, source_target_pairs={{0,2},{1,3},{2,4},{3,5},{4,6},{5,7},{6,8},{7,9},{8,10},{9,11},{10,... | collective-permute-start | bytes 1592 | tf_op jit(solution)/shard_map/ppermute | solution.py:45
  11.4 4.5 %collective-permute-start.1 = (f32[2,66]{1,0:T(2,128)S(1)}, f32[2,66]{1,0:T(2,128)S(1)}, u32[]{:S(2)}, u32[]{:S(2)}) collective-permute-start(f32[2,66]{1,0:T(2,128)S(1)} %pad_maximum_fusion.4), channel_id=1, source_target_pairs={{2,0},{3,1},{4,2},{5,3},{6,4},{7,5},{8,6},{9,7},{10,8},{11,9},{12,... | collective-permute-start | bytes 1592 | tf_op jit(solution)/shard_map/ppermute | solution.py:45
  16.0 2.8 %collective-permute-start.2 = (f32[6,66]{1,0:T(8,128)S(1)}, f32[6,66]{1,0:T(8,128)S(1)}, u32[]{:S(2)}, u32[]{:S(2)}) collective-permute-start(f32[6,66]{1,0:T(8,128)S(1)} %pad_maximum_fusion), channel_id=1, source_target_pairs={{0,1},{1,0},{2,3},{3,2},{4,5},{5,4},{6,7},{7,6},{8,9},{9,8},{10,11... | collective-permute-start | bytes 4760 | tf_op jit(solution)/shard_map/ppermute | solution.py:59
  19.5 11.2 %copy-start.9 = (s32[48,1]{0,1:T(1,128)S(1)}, s32[48,1]{0,1:T(1,128)}, u32[]{:S(2)}) copy-start(s32[48,1]{0,1:T(1,128)} %param.14) | copy-start | bytes 580
  19.5 18.6 %copy-start.2 = (f32[256]{0:T(256)S(1)}, f32[256]{0:T(256)}, u32[]{:S(2)}) copy-start(f32[256]{0:T(256)} %param.21) | copy-start | bytes 3076
  19.5 18.6 %copy-start.3 = (f32[256]{0:T(256)S(1)}, f32[256]{0:T(256)}, u32[]{:S(2)}) copy-start(f32[256]{0:T(256)} %param.20) | copy-start | bytes 3076
  25.9 5.0 %collective-permute-start.3 = (f32[2,65]{1,0:T(2,128)S(1)}, f32[2,65]{1,0:T(2,128)S(1)}, u32[]{:S(2)}, u32[]{:S(2)}) collective-permute-start(f32[2,65]{1,0:T(2,128)S(1)} %pad_maximum_fusion.5), channel_id=1, source_target_pairs={{0,2},{1,3},{2,4},{3,5},{4,6},{5,7},{6,8},{7,9},{8,10},{9,11},{10,... | collective-permute-start | bytes 1568 | tf_op jit(solution)/shard_map/ppermute | solution.py:45
  29.4 5.6 %collective-permute-start.4 = (f32[2,65]{1,0:T(2,128)S(1)}, f32[2,65]{1,0:T(2,128)S(1)}, u32[]{:S(2)}, u32[]{:S(2)}) collective-permute-start(f32[2,65]{1,0:T(2,128)S(1)} %pad_maximum_fusion.5), channel_id=1, source_target_pairs={{2,0},{3,1},{4,2},{5,3},{6,4},{7,5},{8,6},{9,7},{10,8},{11,9},{12,... | collective-permute-start | bytes 1568 | tf_op jit(solution)/shard_map/ppermute | solution.py:45
  35.0 2.4 %collective-permute-start.5 = (f32[6,65]{1,0:T(8,128)S(1)}, f32[6,65]{1,0:T(8,128)S(1)}, u32[]{:S(2)}, u32[]{:S(2)}) collective-permute-start(f32[6,65]{1,0:T(8,128)S(1)} %pad_maximum_fusion.1), channel_id=1, source_target_pairs={{0,1},{1,0},{2,3},{3,2},{4,5},{5,4},{6,7},{7,6},{8,9},{9,8},{10,11... | collective-permute-start | bytes 4688 | tf_op jit(solution)/shard_map/ppermute | solution.py:59
  38.6 0.8 copy-start.1
  38.7 0.8 copy-start.4

commit v12 on v11

--- a/solution.py
+++ b/solution.py
@@ -162,7 +162,8 @@
     tiles = pixels.reshape(how_many, FR, HT, WT, 3)
     latents = encode(tiles, tile_clip, weights)
 
-    latents, target = lax.optimization_barrier((latents, target))
+    source = jnp.argmax(target[None, :] == jnp.arange(slots, dtype=jnp.int32)[:, None], axis=1)
+    latents, source = lax.optimization_barrier((latents, source.astype(jnp.int32)))
     outgoing = route(latents.reshape(how_many, LROWS * LAT), place, slots)
     arrived = lax.all_to_all(
         outgoing.reshape(group_width, capacity, LROWS, LAT),
@@ -171,7 +172,7 @@
         concat_axis=0,
         tiled=True,
     ).reshape(slots, LROWS, LAT)
-    forward = route(arrived.reshape(slots, LROWS * LAT), target, slots)
+    forward = jnp.take(arrived.reshape(slots, LROWS * LAT), source, axis=0)
     received = lax.all_to_all(
         forward.reshape(group_width, capacity, LROWS, LAT),
         "dev",

time: 120 us -> 127 us (1.058)
  blocking collectives: 76.9 us -> 34.5 us
  waiting for transfers between devices: 8.57 us -> 36.2 us
  starting transfers between devices: 14.1 us -> 28.1 us
  local copies, waits for them, and re-layouts: 5.26 us -> 12.3 us
    all_to_all x1 -> x0, blocking collectives: 42.4 us -> none  [per_device(): lax.all_to_all(outgoing.reshape(group_width, capacity, LROWS, LAT), 'dev'...]
    all_to_all x0 -> x1, waiting for transfers between devices: none -> 28.3 us  [per_device(): lax.all_to_all(outgoing.reshape(group_width, capacity, LROWS, LAT), 'dev'...]
    all_to_all x0 -> x1, starting transfers between devices: none -> 14.1 us  [per_device(): lax.all_to_all(outgoing.reshape(group_width, capacity, LROWS, LAT), 'dev'...]
    unnamed x24 -> x27, local copies, waits for them, and re-layouts: 2.78 us -> 7.56 us
    gather x0 -> x1, local copies, waits for them, and re-layouts: none -> 2.16 us  [per_device(): forward = jnp.take(arrived.reshape(slots, LROWS * LAT), source, axis=0)]
  transfers between devices with their start and end apart: 6 -> 7, of which waited for: 4 -> 4; matrix products, arithmetic and copies ran while one was open for 0% -> 1% of each run, Pallas kernels for 0% -> 0%
where the time goes in v12:
time: 127 us; the launch traced here: 126 us
  waiting for transfers between devices  36.2 us (29%)
  blocking collectives  34.5 us (27%)
  starting transfers between devices  28.1 us (22%)
  local copies, waits for them, and re-layouts  12.3 us (10%)
  matrix products  9.53 us (8%)
  other arithmetic  4.84 us (4%)
    all_to_all x1, blocking collectives, per_device(): lax.all_to_all(forward.reshape(group_width, capacity, LROWS, LAT), 'dev',...  34.5 us
    all_to_all x1, waiting for transfers between devices, per_device(): lax.all_to_all(outgoing.reshape(group_width, capacity, LROWS, LAT), 'dev'...  28.3 us
    all_to_all x1, starting transfers between devices, per_device(): lax.all_to_all(outgoing.reshape(group_width, capacity, LROWS, LAT), 'dev'...  14.1 us
    ppermute x4, starting transfers between devices, shifted(): return lax.ppermute(x, AXES, perm)  10.5 us
    conv_general_dilated x2, matrix products, conv_local(): lax.conv_general_dilated(inputs, kernel, (1, stride, stride), ((2, 0), (1...  7.74 us
    unnamed x27, local copies, waits for them, and re-layouts  7.56 us
    ppermute x4, waiting for transfers between devices, shifted(): return lax.ppermute(x, AXES, perm)  7.13 us
    ppermute x2, starting transfers between devices, clip_totals(): partner = lax.ppermute(bundle, AXES, [(i, i ^ 1) for i in range(n)])  3.57 us
  transfers between devices with their start and end apart: 7, of which 4 were waited for; matrix products, arithmetic and copies ran while one was open for 1% of the time, Pallas kernels for 0%

profile of v12, /device:TPU:1, one launch (start us, length us, event | category | flops | bytes accessed | tf_op | source)
XLA Modules:
  0.0 126.1 jit_solution(10225497604849178812)
XLA Ops:
  0.0 1.0 copy.52
  1.0 0.1 reshape.76
  1.1 0.0 copy-start.9
  1.1 0.0 copy-start.6
  1.1 0.0 copy-start.7
  1.1 0.0 copy-start.8
  1.1 3.3 %convert_reduce_fusion = (f32[48,128]{1,0:T(8,128)S(1)}, f32[48,128]{1,0:T(8,128)S(1)}, bf16[48,2,8,8,128]{4,0,3,2,1:T(8,128)(2,1)}) fusion(bf16[48,2,8,8,3]{0,4,3,2,1:T(4,128)(2,1)S(1)} %reshape.76, bf16[3,3,3,3,128]{4,3,2,1,0:T(4,128)(2,1)} %param.16), kind=kOutput, calls=%fused_computation.4 | convolution fusion | flops 57446400 | bytes 1679616 | tf_op jit(solution)/shard_map/conv_general_dilated | solution.py:23
  4.5 0.1 copy.53
  4.6 0.1 copy.54
  4.8 0.1 pad.32.clone
  4.9 0.2 fusion.30
  5.1 0.6 fusion.65
  5.7 1.3 %maximum_bitcast_fusion = (f32[1,66]{1,0:T(1,128)S(1)}, f32[1,66]{1,0:T(1,128)S(1)}) fusion(f32[65]{0:T(128)S(1)} %get-tuple-element.23, f32[1]{0:T(128)} %get-tuple-element.29, f32[65]{0:T(128)S(1)} %get-tuple-element.24, f32[1]{0:T(128)} %get-tuple-element.30), kind=kLoop, calls=%fused_computation.107 | loop fusion | flops 132 | bytes 1056 | tf_op jit(solution)/shard_map/stack | solution.py:55
  7.1 4.4 %collective-permute-start = (f32[2,66]{1,0:T(2,128)S(1)}, f32[2,66]{1,0:T(2,128)S(1)}, u32[]{:S(2)}, u32[]{:S(2)}) collective-permute-start(f32[2,66]{1,0:T(2,128)S(1)} %pad_maximum_fusion.4), channel_id=1, source_target_pairs={{0,2},{1,3},{2,4},{3,5},{4,6},{5,7},{6,8},{7,9},{8,10},{9,11},{10,... | collective-permute-start | bytes 1592 | tf_op jit(solution)/shard_map/ppermute | solution.py:45
  11.5 1.3 %collective-permute-start.1 = (f32[2,66]{1,0:T(2,128)S(1)}, f32[2,66]{1,0:T(2,128)S(1)}, u32[]{:S(2)}, u32[]{:S(2)}) collective-permute-start(f32[2,66]{1,0:T(2,128)S(1)} %pad_maximum_fusion.4), channel_id=1, source_target_pairs={{2,0},{3,1},{4,2},{5,3},{6,4},{7,5},{8,6},{9,7},{10,8},{11,9},{12,... | collective-permute-start | bytes 1592 | tf_op jit(solution)/shard_map/ppermute | solution.py:45
  12.8 0.2 convert_reduce_fusion.2
  13.0 3.0 %collective-permute-done.1 = f32[2,66]{1,0:T(2,128)S(1)} collective-permute-done((f32[2,66]{1,0:T(2,128)S(1)}, f32[2,66]{1,0:T(2,128)S(1)}, u32[]{:S(2)}, u32[]{:S(2)}) %collective-permute-start.1) | collective-permute-done | bytes 560 | tf_op jit(solution)/shard_map/ppermute | solution.py:45
  16.0 2.0 %collective-permute-start.2 = (f32[6,66]{1,0:T(8,128)S(1)}, f32[6,66]{1,0:T(8,128)S(1)}, u32[]{:S(2)}, u32[]{:S(2)}) collective-permute-start(f32[6,66]{1,0:T(8,128)S(1)} %pad_maximum_fusion), channel_id=1, source_target_pairs={{0,1},{1,0},{2,3},{3,2},{4,5},{5,4},{6,7},{7,6},{8,9},{9,8},{10,11... | collective-permute-start | bytes 4760 | tf_op jit(solution)/shard_map/ppermute | solution.py:59
  18.0 0.7 iota_reduce_fusion
  18.7 0.1 copy.55
  18.8 0.0 collective-permute-done.2
  18.8 0.1 slice_reduce_fusion.1
  18.9 0.3 convolution_add_fusion.1
  19.3 0.1 copy.57
  19.4 0.1 copy.58
  19.5 0.0 copy-done.7
  19.5 0.0 copy-start.10
  19.5 4.4 %convert_reduce_fusion.1 = (f32[48,256]{1,0:T(8,128)S(1)}, f32[48,256]{1,0:T(8,128)S(1)}, bf16[48,2,4,4,256]{4,0,3,2,1:T(8,128)(2,1)S(1)}) fusion(bf16[3,3,3,128,256]{4,3,2,1,0:T(8,128)(2,1)S(1)} %copy-done, bf16[48,2,8,8,128]{4,0,3,2,1:T(8,128)(2,1)} %get-tuple-element.31, f32[128]{0:T(128)S(1)} %copy-done.7, f32[128]{0:T(128)S(1)} %copy-done.8, ...), kind=kOutput, calls=%fused_computation.19 | convolution fusion | flops 1151705088 | bytes 4277248 | tf_op jit(solution)/shard_map/conv_general_dilated | solution.py:23
  23.9 0.0 copy-start.4
  23.9 0.1 copy.60
  24.1 0.1 copy.59
  24.2 0.2 fusion.35
  24.5 0.7 maximum_bitcast_fusion.2
  25.2 0.7 maximum_bitcast_fusion.3
  25.9 3.5 %collective-permute-start.3 = (f32[2,65]{1,0:T(2,128)S(1)}, f32[2,65]{1,0:T(2,128)S(1)}, u32[]{:S(2)}, u32[]{:S(2)}) collective-permute-start(f32[2,65]{1,0:T(2,128)S(1)} %pad_maximum_fusion.5), channel_id=1, source_target_pairs={{0,2},{1,3},{2,4},{3,5},{4,6},{5,7},{6,8},{7,9},{8,10},{9,11},{10,... | collective-permute-start | bytes 1568 | tf_op jit(solution)/shard_map/ppermute | solution.py:45
  29.4 1.3 %collective-permute-start.4 = (f32[2,65]{1,0:T(2,128)S(1)}, f32[2,65]{1,0:T(2,128)S(1)}, u32[]{:S(2)}, u32[]{:S(2)}) collective-permute-start(f32[2,65]{1,0:T(2,128)S(1)} %pad_maximum_fusion.5), channel_id=1, source_target_pairs={{2,0},{3,1},{4,2},{5,3},{6,4},{7,5},{8,6},{9,7},{10,8},{11,9},{12,... | collective-permute-start | bytes 1568 | tf_op jit(solution)/shard_map/ppermute | solution.py:45
  30.7 0.2 convert_reduce_fusion.3
  30.9 4.1 %collective-permute-done.4 = f32[2,65]{1,0:T(2,128)S(1)} collective-permute-done((f32[2,65]{1,0:T(2,128)S(1)}, f32[2,65]{1,0:T(2,128)S(1)}, u32[]{:S(2)}, u32[]{:S(2)}) %collective-permute-start.4) | collective-permute-done | bytes 552 | tf_op jit(solution)/shard_map/ppermute | solution.py:45
  35.0 1.6 %collective-permute-start.5 = (f32[6,65]{1,0:T(8,128)S(1)}, f32[6,65]{1,0:T(8,128)S(1)}, u32[]{:S(2)}, u32[]{:S(2)}) collective-permute-start(f32[6,65]{1,0:T(8,128)S(1)} %pad_maximum_fusion.1), channel_id=1, source_target_pairs={{0,1},{1,0},{2,3},{3,2},{4,5},{5,4},{6,7},{7,6},{8,9},{9,8},{10,11... | collective-permute-start | bytes 4688 | tf_op jit(solution)/shard_map/ppermute | solution.py:59
  36.6 0.1 copy.61
  36.7 0.7 collective-permute-done.5
  37.5 0.1 slice_reduce_fusion
  37.6 0.3 convolution_add_fusion.2
  37.9 0.1 copy.63
  38.0 0.1 copy.64
  38.1 0.5 fusion.20
  38.7 0.0 copy-start.2
  38.7 0.0 copy-start.5
  38.7 0.4 copy.65
  39.1 0.2 reshape.77
  39.3 0.2 copy-done.2
  39.5 0.4 fusion.10
  39.9 0.4 fusion.26
  40.3 1.2 copy.69
  41.5 14.1 %all-to-all-start = ((bf16[64,2,32,128]{3,2,1,0:T(8,128)(2,1)}), bf16[64,2,32,128]{3,2,1,0:T(8,128)(2,1)S(1)}, u32[]{:S(2)}, u32[]{:S(2)}) async-start(bf16[64,2,32,128]{3,2,1,0:T(8,128)(2,1)} %bitcast.65), calls=%async_computation | async-start | bytes 2097152 | tf_op jit(solution)/shard_map/all_to_all | solution.py:168
  55.6 0.1 broadcast_in_dim.14
  55.8 28.3 %all-to-all-done = bf16[64,2,32,128]{3,2,1,0:T(8,128)(2,1)S(1)} async-done(((bf16[64,2,32,128]{3,2,1,0:T(8,128)(2,1)}), bf16[64,2,32,128]{3,2,1,0:T(8,128)(2,1)S(1)}, u32[]{:S(2)}, u32[]{:S(2)}) %all-to-all-start) | async-done | bytes 1048608 | tf_op jit(solution)/shard_map/all_to_all | solution.py:168
  84.1 1.0 copy-done.1
  85.1 1.7 %copy.77 = bf16[16,8,32,128]{3,1,2,0:T(8,128)(2,1)S(1)} copy(bf16[16,8,32,128]{3,2,1,0:T(8,128)(2,1)} %bitcast.64) | data formatting | bytes 2097152
  86.8 2.2 %gather_fusion = bf16[128,4096]{1,0:T(8,128)(2,1)} fusion(bf16[128,4096]{1,0:T(8,128)(2,1)S(1)} %bitcast.62, s32[1024]{0:T(1024)S(1)} %pad_clamp_fusion), kind=kCustom, calls=%fused_computation | custom fusion | bytes 2097664 | tf_op jit(solution)/shard_map/jit(_take)/gather | solution.py:175
  88.9 1.5 %copy.71 = bf16[16,8,32,128]{3,2,1,0:T(8,128)(2,1)S(1)} copy(bf16[16,8,32,128]{3,1,2,0:T(8,128)(2,1)} %bitcast.63) | data formatting | bytes 2097152
  90.4 0.2 broadcast_select_fusion
  90.6 34.5 %all_to_all.10 = bf16[64,2,32,128]{3,2,1,0:T(8,128)(2,1)S(1)} all-to-all(bf16[64,2,32,128]{3,2,1,0:T(8,128)(2,1)S(1)} %broadcast_select_fusion), channel_id=1, replica_groups=mesh['slab'=4,'dev'=64] {'dev'}, dimensions={0} | all-to-all | bytes 2097152 | tf_op jit(solution)/shard_map/all_to_all | solution.py:176
  125.1 1.0 copy.79
  (44 shorter events, 0.5 us)
Async XLA Ops:
  0.0 19.5 %copy-start = (bf16[3,3,3,128,256]{4,3,2,1,0:T(8,128)(2,1)S(1)}, bf16[3,3,3,128,256]{4,3,2,1,0:T(8,128)(2,1)}, u32[]{:S(2)}) copy-start(bf16[3,3,3,128,256]{4,3,2,1,0:T(8,128)(2,1)} %param.19) | copy-start | bytes 5308420
  1.1 3.7 %copy-start.9 = (s32[48]{0:T(128)S(1)}, s32[48]{0:T(128)}, u32[]{:S(2)}) copy-start(s32[48]{0:T(128)} %param.13) | copy-start | bytes 580
  1.1 11.6 %copy-start.6 = (s32[128,1]{0,1:T(1,128)S(1)}, s32[128,1]{0,1:T(1,128)}, u32[]{:S(2)}) copy-start(s32[128,1]{0,1:T(1,128)} %param.15) | copy-start | bytes 1540
  1.1 18.4 %copy-start.7 = (f32[128]{0:T(128)S(1)}, f32[128]{0:T(128)}, u32[]{:S(2)}) copy-start(f32[128]{0:T(128)} %param.18) | copy-start | bytes 1540
  1.1 18.4 %copy-start.8 = (f32[128]{0:T(128)S(1)}, f32[128]{0:T(128)}, u32[]{:S(2)}) copy-start(f32[128]{0:T(128)} %param.17) | copy-start | bytes 1540
  7.1 5.9 %collective-permute-start = (f32[2,66]{1,0:T(2,128)S(1)}, f32[2,66]{1,0:T(2,128)S(1)}, u32[]{:S(2)}, u32[]{:S(2)}) collective-permute-start(f32[2,66]{1,0:T(2,128)S(1)} %pad_maximum_fusion.4), channel_id=1, source_target_pairs={{0,2},{1,3},{2,4},{3,5},{4,6},{5,7},{6,8},{7,9},{8,10},{9,11},{10,... | collective-permute-start | bytes 1592 | tf_op jit(solution)/shard_map/ppermute | solution.py:45
  11.5 4.5 %collective-permute-start.1 = (f32[2,66]{1,0:T(2,128)S(1)}, f32[2,66]{1,0:T(2,128)S(1)}, u32[]{:S(2)}, u32[]{:S(2)}) collective-permute-start(f32[2,66]{1,0:T(2,128)S(1)} %pad_maximum_fusion.4), channel_id=1, source_target_pairs={{2,0},{3,1},{4,2},{5,3},{6,4},{7,5},{8,6},{9,7},{10,8},{11,9},{12,... | collective-permute-start | bytes 1592 | tf_op jit(solution)/shard_map/ppermute | solution.py:45
  16.0 2.8 %collective-permute-start.2 = (f32[6,66]{1,0:T(8,128)S(1)}, f32[6,66]{1,0:T(8,128)S(1)}, u32[]{:S(2)}, u32[]{:S(2)}) collective-permute-start(f32[6,66]{1,0:T(8,128)S(1)} %pad_maximum_fusion), channel_id=1, source_target_pairs={{0,1},{1,0},{2,3},{3,2},{4,5},{5,4},{6,7},{7,6},{8,9},{9,8},{10,11... | collective-permute-start | bytes 4760 | tf_op jit(solution)/shard_map/ppermute | solution.py:59
  19.5 11.2 %copy-start.10 = (s32[48,1]{0,1:T(1,128)S(1)}, s32[48,1]{0,1:T(1,128)}, u32[]{:S(2)}) copy-start(s32[48,1]{0,1:T(1,128)} %param.14) | copy-start | bytes 580
  23.9 14.2 %copy-start.3 = (f32[256]{0:T(256)S(1)}, f32[256]{0:T(256)}, u32[]{:S(2)}) copy-start(f32[256]{0:T(256)} %param.21) | copy-start | bytes 3076
  23.9 14.2 %copy-start.4 = (f32[256]{0:T(256)S(1)}, f32[256]{0:T(256)}, u32[]{:S(2)}) copy-start(f32[256]{0:T(256)} %param.20) | copy-start | bytes 3076
  25.9 5.0 %collective-permute-start.3 = (f32[2,65]{1,0:T(2,128)S(1)}, f32[2,65]{1,0:T(2,128)S(1)}, u32[]{:S(2)}, u32[]{:S(2)}) collective-permute-start(f32[2,65]{1,0:T(2,128)S(1)} %pad_maximum_fusion.5), channel_id=1, source_target_pairs={{0,2},{1,3},{2,4},{3,5},{4,6},{5,7},{6,8},{7,9},{8,10},{9,11},{10,... | collective-permute-start | bytes 1568 | tf_op jit(solution)/shard_map/ppermute | solution.py:45
  29.4 5.6 %collective-permute-start.4 = (f32[2,65]{1,0:T(2,128)S(1)}, f32[2,65]{1,0:T(2,128)S(1)}, u32[]{:S(2)}, u32[]{:S(2)}) collective-permute-start(f32[2,65]{1,0:T(2,128)S(1)} %pad_maximum_fusion.5), channel_id=1, source_target_pairs={{2,0},{3,1},{4,2},{5,3},{6,4},{7,5},{8,6},{9,7},{10,8},{11,9},{12,... | collective-permute-start | bytes 1568 | tf_op jit(solution)/shard_map/ppermute | solution.py:45
  35.0 2.4 %collective-permute-start.5 = (f32[6,65]{1,0:T(8,128)S(1)}, f32[6,65]{1,0:T(8,128)S(1)}, u32[]{:S(2)}, u32[]{:S(2)}) collective-permute-start(f32[6,65]{1,0:T(8,128)S(1)} %pad_maximum_fusion.1), channel_id=1, source_target_pairs={{0,1},{1,0},{2,3},{3,2},{4,5},{5,4},{6,7},{7,6},{8,9},{9,8},{10,11... | collective-permute-start | bytes 4688 | tf_op jit(solution)/shard_map/ppermute | solution.py:59
  38.7 0.8 copy-start.2
  38.7 0.8 copy-start.5
  41.5 42.6 %all-to-all-start = ((bf16[64,2,32,128]{3,2,1,0:T(8,128)(2,1)}), bf16[64,2,32,128]{3,2,1,0:T(8,128)(2,1)S(1)}, u32[]{:S(2)}, u32[]{:S(2)}) async-start(bf16[64,2,32,128]{3,2,1,0:T(8,128)(2,1)} %bitcast.65), calls=%async_computation | async-start | bytes 2097152 | tf_op jit(solution)/shard_map/all_to_all | solution.py:168
  84.1 1.0 copy-start.1

commit v13 on v11

--- a/solution.py
+++ b/solution.py
@@ -121,9 +121,8 @@
     means, scales = finish_stats(totals, counts, LROWS * (C2 // GROUPS))
     active = normalize(down, means, scales, gain_second, bias_second)
 
-    flat = active.reshape(-1, C2)
-    latent = jnp.dot(flat, project, preferred_element_type=jnp.float32) + project_bias
-    return latent.astype(jnp.bfloat16).reshape(how_many, LROWS, LAT)
+    latent = jnp.einsum("tfhwc,cd->tfhwd", active, project, preferred_element_type=jnp.float32)
+    return (latent + project_bias).astype(jnp.bfloat16).reshape(how_many, LROWS, LAT)
 
 
 def per_device(

time: 120 us -> 119 us (level)
  no operation moved by 1% of the time
where the time goes in v13:
time: 119 us; the launch traced here: 118 us
  blocking collectives  76.9 us (65%)
  starting transfers between devices  14.1 us (12%)
  matrix products  10.4 us (9%)
  waiting for transfers between devices  8.57 us (7%)
  local copies, waits for them, and re-layouts  4.45 us (4%)
  other arithmetic  3.37 us (3%)
    all_to_all x1, blocking collectives, per_device(): lax.all_to_all(outgoing.reshape(group_width, capacity, LROWS, LAT), 'dev'...  42.4 us
    all_to_all x1, blocking collectives, per_device(): lax.all_to_all(forward.reshape(group_width, capacity, LROWS, LAT), 'dev',...  34.5 us
    ppermute x4, starting transfers between devices, shifted(): return lax.ppermute(x, AXES, perm)  10.5 us
    conv_general_dilated x2, matrix products, conv_local(): lax.conv_general_dilated(inputs, kernel, (1, stride, stride), ((2, 0), (1...  7.74 us
    ppermute x4, waiting for transfers between devices, shifted(): return lax.ppermute(x, AXES, perm)  7.14 us
    ppermute x2, starting transfers between devices, clip_totals(): partner = lax.ppermute(bundle, AXES, [(i, i ^ 1) for i in range(n)])  3.58 us
    another operation x5, other arithmetic, clip_totals(): mine = jnp.stack([to_left, to_right])  2.75 us
    unnamed x24, local copies, waits for them, and re-layouts  2.56 us
  transfers between devices with their start and end apart: 6, of which 4 were waited for; matrix products, arithmetic and copies ran while one was open for 0% of the time, Pallas kernels for 0%

profile of v13, /device:TPU:1, one launch (start us, length us, event | category | flops | bytes accessed | tf_op | source)
XLA Modules:
  0.0 118.2 jit_solution(17990086550210581383)
XLA Ops:
  0.0 0.0 copy-start
  0.0 1.0 copy.52
  1.0 0.0 copy-start.4
  1.0 0.1 reshape.57
  1.1 0.0 copy-start.5
  1.1 0.0 copy-start.6
  1.1 3.3 %convert_reduce_fusion = (f32[48,128]{1,0:T(8,128)S(1)}, f32[48,128]{1,0:T(8,128)S(1)}, bf16[48,2,8,8,128]{4,0,3,2,1:T(8,128)(2,1)}) fusion(bf16[48,2,8,8,3]{0,4,3,2,1:T(4,128)(2,1)S(1)} %reshape.57, bf16[3,3,3,3,128]{4,3,2,1,0:T(4,128)(2,1)} %param.16), kind=kOutput, calls=%fused_computation.4 | convolution fusion | flops 57446400 | bytes 1679616 | tf_op jit(solution)/shard_map/conv_general_dilated | solution.py:23
  4.5 0.1 copy.53
  4.6 0.1 copy.54
  4.8 0.0 copy-done.7
  4.8 0.1 pad.32.clone
  4.9 0.2 fusion.35
  5.1 0.6 fusion.72
  5.7 1.3 %maximum_bitcast_fusion = (f32[1,66]{1,0:T(1,128)S(1)}, f32[1,66]{1,0:T(1,128)S(1)}) fusion(f32[65]{0:T(128)S(1)} %get-tuple-element.21, f32[1]{0:T(128)} %get-tuple-element.27, f32[65]{0:T(128)S(1)} %get-tuple-element.22, f32[1]{0:T(128)} %get-tuple-element.28), kind=kLoop, calls=%fused_computation.106 | loop fusion | flops 132 | bytes 1056 | tf_op jit(solution)/shard_map/stack | solution.py:55
  7.1 4.4 %collective-permute-start = (f32[2,66]{1,0:T(2,128)S(1)}, f32[2,66]{1,0:T(2,128)S(1)}, u32[]{:S(2)}, u32[]{:S(2)}) collective-permute-start(f32[2,66]{1,0:T(2,128)S(1)} %pad_maximum_fusion.4), channel_id=1, source_target_pairs={{0,2},{1,3},{2,4},{3,5},{4,6},{5,7},{6,8},{7,9},{8,10},{9,11},{10,... | collective-permute-start | bytes 1592 | tf_op jit(solution)/shard_map/ppermute | solution.py:45
  11.4 1.3 %collective-permute-start.1 = (f32[2,66]{1,0:T(2,128)S(1)}, f32[2,66]{1,0:T(2,128)S(1)}, u32[]{:S(2)}, u32[]{:S(2)}) collective-permute-start(f32[2,66]{1,0:T(2,128)S(1)} %pad_maximum_fusion.4), channel_id=1, source_target_pairs={{2,0},{3,1},{4,2},{5,3},{6,4},{7,5},{8,6},{9,7},{10,8},{11,9},{12,... | collective-permute-start | bytes 1592 | tf_op jit(solution)/shard_map/ppermute | solution.py:45
  12.7 0.0 copy-done.4
  12.8 0.2 convert_reduce_fusion.2
  12.9 0.0 collective-permute-done
  12.9 3.0 %collective-permute-done.1 = f32[2,66]{1,0:T(2,128)S(1)} collective-permute-done((f32[2,66]{1,0:T(2,128)S(1)}, f32[2,66]{1,0:T(2,128)S(1)}, u32[]{:S(2)}, u32[]{:S(2)}) %collective-permute-start.1) | collective-permute-done | bytes 560 | tf_op jit(solution)/shard_map/ppermute | solution.py:45
  16.0 2.0 %collective-permute-start.2 = (f32[6,66]{1,0:T(8,128)S(1)}, f32[6,66]{1,0:T(8,128)S(1)}, u32[]{:S(2)}, u32[]{:S(2)}) collective-permute-start(f32[6,66]{1,0:T(8,128)S(1)} %pad_maximum_fusion), channel_id=1, source_target_pairs={{0,1},{1,0},{2,3},{3,2},{4,5},{5,4},{6,7},{7,6},{8,9},{9,8},{10,11... | collective-permute-start | bytes 4760 | tf_op jit(solution)/shard_map/ppermute | solution.py:59
  18.0 0.1 copy.55
  18.1 0.7 collective-permute-done.2
  18.8 0.1 slice_reduce_fusion.1
  18.9 0.3 convolution_add_fusion.1
  19.3 0.1 copy.57
  19.4 0.1 copy.58
  19.4 0.0 copy-done
  19.5 0.0 copy-done.5
  19.5 0.0 copy-done.6
  19.5 0.0 copy-start.8
  19.5 0.0 copy-start.1
  19.5 0.0 copy-start.2
  19.5 0.0 copy-start.3
  19.5 0.0 copy-start.9
  19.5 4.4 %convert_reduce_fusion.1 = (f32[48,256]{1,0:T(8,128)S(1)}, f32[48,256]{1,0:T(8,128)S(1)}, bf16[48,2,4,4,256]{4,0,3,2,1:T(8,128)(2,1)S(1)}) fusion(bf16[3,3,3,128,256]{4,3,2,1,0:T(8,128)(2,1)S(1)} %copy-done, bf16[48,2,8,8,128]{4,0,3,2,1:T(8,128)(2,1)} %get-tuple-element.29, f32[128]{0:T(128)S(1)} %copy-done.5, f32[128]{0:T(128)S(1)} %copy-done.6, ...), kind=kOutput, calls=%fused_computation.17 | convolution fusion | flops 1151705088 | bytes 4277248 | tf_op jit(solution)/shard_map/conv_general_dilated | solution.py:23
  24.0 0.1 copy.60
  24.1 0.1 copy.59
  24.3 0.2 fusion.40
  24.5 0.7 maximum_bitcast_fusion.2
  25.2 0.7 maximum_bitcast_fusion.3
  25.9 3.5 %collective-permute-start.3 = (f32[2,65]{1,0:T(2,128)S(1)}, f32[2,65]{1,0:T(2,128)S(1)}, u32[]{:S(2)}, u32[]{:S(2)}) collective-permute-start(f32[2,65]{1,0:T(2,128)S(1)} %pad_maximum_fusion.5), channel_id=1, source_target_pairs={{0,2},{1,3},{2,4},{3,5},{4,6},{5,7},{6,8},{7,9},{8,10},{9,11},{10,... | collective-permute-start | bytes 1568 | tf_op jit(solution)/shard_map/ppermute | solution.py:45
  29.4 1.3 %collective-permute-start.4 = (f32[2,65]{1,0:T(2,128)S(1)}, f32[2,65]{1,0:T(2,128)S(1)}, u32[]{:S(2)}, u32[]{:S(2)}) collective-permute-start(f32[2,65]{1,0:T(2,128)S(1)} %pad_maximum_fusion.5), channel_id=1, source_target_pairs={{2,0},{3,1},{4,2},{5,3},{6,4},{7,5},{8,6},{9,7},{10,8},{11,9},{12,... | collective-permute-start | bytes 1568 | tf_op jit(solution)/shard_map/ppermute | solution.py:45
  30.7 0.0 copy-done.8
  30.7 0.2 convert_reduce_fusion.3
  30.9 0.0 collective-permute-done.3
  30.9 4.1 %collective-permute-done.4 = f32[2,65]{1,0:T(2,128)S(1)} collective-permute-done((f32[2,65]{1,0:T(2,128)S(1)}, f32[2,65]{1,0:T(2,128)S(1)}, u32[]{:S(2)}, u32[]{:S(2)}) %collective-permute-start.4) | collective-permute-done | bytes 552 | tf_op jit(solution)/shard_map/ppermute | solution.py:45
  35.1 1.6 %collective-permute-start.5 = (f32[6,65]{1,0:T(8,128)S(1)}, f32[6,65]{1,0:T(8,128)S(1)}, u32[]{:S(2)}, u32[]{:S(2)}) collective-permute-start(f32[6,65]{1,0:T(8,128)S(1)} %pad_maximum_fusion.1), channel_id=1, source_target_pairs={{0,1},{1,0},{2,3},{3,2},{4,5},{5,4},{6,7},{7,6},{8,9},{9,8},{10,11... | collective-permute-start | bytes 4688 | tf_op jit(solution)/shard_map/ppermute | solution.py:59
  36.6 0.1 copy.61
  36.7 0.7 collective-permute-done.5
  37.5 0.1 slice_reduce_fusion
  37.6 0.3 convolution_add_fusion.2
  37.9 0.1 copy.63
  38.0 0.1 copy.64
  38.1 0.0 copy-done.1
  38.1 0.0 copy-done.2
  38.1 0.7 fusion.27
  38.9 0.4 fusion.25
  39.3 0.2 copy.70
  39.5 42.4 %all_to_all.10 = bf16[64,2,32,128]{3,2,1,0:T(8,128)(2,1)S(1)} all-to-all(bf16[64,2,32,128]{3,2,1,0:T(8,128)(2,1)S(1)} %bitcast.70), channel_id=1, replica_groups=mesh['slab'=4,'dev'=64] {'dev'}, dimensions={0} | all-to-all | bytes 2097152 | tf_op jit(solution)/shard_map/all_to_all | solution.py:166
  82.0 0.5 fusion.26
  82.5 0.2 copy.72
  82.7 34.5 %all_to_all.11 = bf16[64,2,32,128]{3,2,1,0:T(8,128)(2,1)S(1)} all-to-all(bf16[64,2,32,128]{3,2,1,0:T(8,128)(2,1)S(1)} %bitcast.71), channel_id=1, replica_groups=mesh['slab'=4,'dev'=64] {'dev'}, dimensions={0} | all-to-all | bytes 2097152 | tf_op jit(solution)/shard_map/all_to_all | solution.py:174
  117.2 1.0 copy.82
  (31 shorter events, 0.4 us)
Async XLA Ops:
  0.0 19.4 %copy-start = (bf16[3,3,3,128,256]{4,3,2,1,0:T(8,128)(2,1)S(1)}, bf16[3,3,3,128,256]{4,3,2,1,0:T(8,128)(2,1)}, u32[]{:S(2)}) copy-start(bf16[3,3,3,128,256]{4,3,2,1,0:T(8,128)(2,1)} %param.19) | copy-start | bytes 5308420
  0.0 4.8 %copy-start.7 = (s32[48]{0:T(128)S(1)}, s32[48]{0:T(128)}, u32[]{:S(2)}) copy-start(s32[48]{0:T(128)} %param.13) | copy-start | bytes 580
  1.0 11.7 %copy-start.4 = (s32[128,1]{0,1:T(1,128)S(1)}, s32[128,1]{0,1:T(1,128)}, u32[]{:S(2)}) copy-start(s32[128,1]{0,1:T(1,128)} %param.15) | copy-start | bytes 1540
  1.1 18.3 %copy-start.5 = (f32[128]{0:T(128)S(1)}, f32[128]{0:T(128)}, u32[]{:S(2)}) copy-start(f32[128]{0:T(128)} %param.18) | copy-start | bytes 1540
  1.1 18.3 %copy-start.6 = (f32[128]{0:T(128)S(1)}, f32[128]{0:T(128)}, u32[]{:S(2)}) copy-start(f32[128]{0:T(128)} %param.17) | copy-start | bytes 1540
  7.1 5.9 %collective-permute-start = (f32[2,66]{1,0:T(2,128)S(1)}, f32[2,66]{1,0:T(2,128)S(1)}, u32[]{:S(2)}, u32[]{:S(2)}) collective-permute-start(f32[2,66]{1,0:T(2,128)S(1)} %pad_maximum_fusion.4), channel_id=1, source_target_pairs={{0,2},{1,3},{2,4},{3,5},{4,6},{5,7},{6,8},{7,9},{8,10},{9,11},{10,... | collective-permute-start | bytes 1592 | tf_op jit(solution)/shard_map/ppermute | solution.py:45
  11.4 4.5 %collective-permute-start.1 = (f32[2,66]{1,0:T(2,128)S(1)}, f32[2,66]{1,0:T(2,128)S(1)}, u32[]{:S(2)}, u32[]{:S(2)}) collective-permute-start(f32[2,66]{1,0:T(2,128)S(1)} %pad_maximum_fusion.4), channel_id=1, source_target_pairs={{2,0},{3,1},{4,2},{5,3},{6,4},{7,5},{8,6},{9,7},{10,8},{11,9},{12,... | collective-permute-start | bytes 1592 | tf_op jit(solution)/shard_map/ppermute | solution.py:45
  16.0 2.8 %collective-permute-start.2 = (f32[6,66]{1,0:T(8,128)S(1)}, f32[6,66]{1,0:T(8,128)S(1)}, u32[]{:S(2)}, u32[]{:S(2)}) collective-permute-start(f32[6,66]{1,0:T(8,128)S(1)} %pad_maximum_fusion), channel_id=1, source_target_pairs={{0,1},{1,0},{2,3},{3,2},{4,5},{5,4},{6,7},{7,6},{8,9},{9,8},{10,11... | collective-permute-start | bytes 4760 | tf_op jit(solution)/shard_map/ppermute | solution.py:59
  19.5 11.2 %copy-start.8 = (s32[48,1]{0,1:T(1,128)S(1)}, s32[48,1]{0,1:T(1,128)}, u32[]{:S(2)}) copy-start(s32[48,1]{0,1:T(1,128)} %param.14) | copy-start | bytes 580
  19.5 18.6 %copy-start.1 = (bf16[256,128]{1,0:T(8,128)(2,1)S(1)}, bf16[256,128]{1,0:T(8,128)(2,1)}, u32[]{:S(2)}) copy-start(bf16[256,128]{1,0:T(8,128)(2,1)} %param.22) | copy-start | bytes 196612
  19.5 18.6 %copy-start.2 = (f32[256]{0:T(256)S(1)}, f32[256]{0:T(256)}, u32[]{:S(2)}) copy-start(f32[256]{0:T(256)} %param.21) | copy-start | bytes 3076
  19.5 18.6 %copy-start.3 = (f32[256]{0:T(256)S(1)}, f32[256]{0:T(256)}, u32[]{:S(2)}) copy-start(f32[256]{0:T(256)} %param.20) | copy-start | bytes 3076
  19.5 18.6 %copy-start.9 = (f32[128]{0:T(128)S(1)}, f32[128]{0:T(128)}, u32[]{:S(2)}) copy-start(f32[128]{0:T(128)} %param.23) | copy-start | bytes 1540
  25.9 5.0 %collective-permute-start.3 = (f32[2,65]{1,0:T(2,128)S(1)}, f32[2,65]{1,0:T(2,128)S(1)}, u32[]{:S(2)}, u32[]{:S(2)}) collective-permute-start(f32[2,65]{1,0:T(2,128)S(1)} %pad_maximum_fusion.5), channel_id=1, source_target_pairs={{0,2},{1,3},{2,4},{3,5},{4,6},{5,7},{6,8},{7,9},{8,10},{9,11},{10,... | collective-permute-start | bytes 1568 | tf_op jit(solution)/shard_map/ppermute | solution.py:45
  29.4 5.6 %collective-permute-start.4 = (f32[2,65]{1,0:T(2,128)S(1)}, f32[2,65]{1,0:T(2,128)S(1)}, u32[]{:S(2)}, u32[]{:S(2)}) collective-permute-start(f32[2,65]{1,0:T(2,128)S(1)} %pad_maximum_fusion.5), channel_id=1, source_target_pairs={{2,0},{3,1},{4,2},{5,3},{6,4},{7,5},{8,6},{9,7},{10,8},{11,9},{12,... | collective-permute-start | bytes 1568 | tf_op jit(solution)/shard_map/ppermute | solution.py:45
  35.1 2.4 %collective-permute-start.5 = (f32[6,65]{1,0:T(8,128)S(1)}, f32[6,65]{1,0:T(8,128)S(1)}, u32[]{:S(2)}, u32[]{:S(2)}) collective-permute-start(f32[6,65]{1,0:T(8,128)S(1)} %pad_maximum_fusion.1), channel_id=1, source_target_pairs={{0,1},{1,0},{2,3},{3,2},{4,5},{5,4},{6,7},{7,6},{8,9},{9,8},{10,11... | collective-permute-start | bytes 4688 | tf_op jit(solution)/shard_map/ppermute | solution.py:59
